TPU v7x, 768 devices: a whole 4x8x12 slice. The times are simulated.
768 devices in a mesh: span: 8 (over y_lo, x), seq: 8 (over y_hi, core), mp: 12 (over z).
Axes of the slice: x: 4, y: 8 (y_hi: 4, y_lo: 2; y = y_hi * 2 + y_lo), z: 12, core: 2. Of those that a mesh axis runs over, the one named last changes fastest.
Arguments:
- queries: bfloat16 [8, 512, 6144], P('span', 'seq', 'mp'), may hold values from -30 to 30
- keys: bfloat16 [8, 512, 1024], P('span', 'seq'), may hold values from -30 to 30
- values: bfloat16 [8, 512, 1024], P('span', 'seq'), may hold values from -6 to 6
- clip_ids: int32 [512], P('seq'), may hold values from 0 to 5, never falling along the last dimension, each value on 1 to 256 neighbouring positions
- block_mask: int32 [8, 8], replicated, may hold values from 0 to 1, as said below
- out_weight: bfloat16 [6144, 6144], P('mp'), may hold values from -0.078125 to 0.078125
Outputs:
- projected: bfloat16 [8, 512, 6144], P('span', 'seq', 'mp')
Inputs may be any that keep to these rules, and one draw needn't show every extreme that they name: block_mask[c][c] is 1; block_mask[c][c2] is 0 unless c - 3 < c2 <= c. `clip_ids`: clip ids never fall along the rows; each clip has 1 to 256 rows, one exactly that many.
All inputs are finite; a program needn't handle non-finite values.
Results may differ from a plain program's by a relative error of at most 0.017.
Values may be sent and summed in bfloat16 or wider, within the bound.
No kernel may reach another device: no remote copies, remote signals or barrier semaphores. Data moves between devices by JAX's collectives and lax.ppermute only.
A program may use at most 64 MiB of HBM per device.

v0:
```python
import jax
import jax.numpy as jnp
from jax import lax
from jax.sharding import PartitionSpec as P

HEAD_DIM = 128
WINDOW = 3
GROUP = 6


def passed_along(x, axis, by):
    size = lax.axis_size(axis)
    pairs = [(i, i + by) for i in range(size) if 0 <= i + by < size]
    return lax.ppermute(x, axis, pairs)


def on_device(queries, keys, values, clip_ids, block_mask, out_weight):
    row_count = queries.shape[1]
    local_width = queries.shape[2]
    head_count = local_width // HEAD_DIM
    kv_width = keys.shape[2]
    kv_count = kv_width // HEAD_DIM
    score_scale = HEAD_DIM ** (-0.5)
    span_index = lax.axis_index("span")
    first_head = lax.axis_index("mp") * head_count
    kv_choice = (first_head + jnp.arange(head_count, dtype=jnp.int32)) // GROUP
    packed = jnp.concatenate([keys, values], axis=2)
    query_heads = jnp.transpose(queries[0].reshape(row_count, head_count, HEAD_DIM), (1, 0, 2))
    mask_row = lax.dynamic_index_in_dim(block_mask, span_index, 0, keepdims=False)
    visible = []
    for j in range(WINDOW):
        earlier = span_index - j
        entry = lax.dynamic_index_in_dim(mask_row, jnp.maximum(earlier, 0), 0, keepdims=False)
        visible.append(jnp.where(earlier >= 0, entry, 0))
    initial = (
        jnp.full((head_count, row_count), -1e30, jnp.float32),
        jnp.zeros((head_count, row_count), jnp.float32),
        jnp.zeros((head_count, row_count, HEAD_DIM), jnp.float32),
    )
    stacked = [packed[0]]
    for j in range(1, WINDOW):
        stacked.append(passed_along(packed[0], "span", j))
    running_max, running_total, running_acc = initial
    blocks = lax.all_gather(jnp.stack(stacked, axis=0), "seq", axis=1, tiled=True)
    key_clips = lax.all_gather(clip_ids[None, :], "seq", axis=1, tiled=True)
    piece_rows = blocks.shape[1]
    for j in range(WINDOW):
        key_all = blocks[j, :, :kv_width].reshape(piece_rows, kv_count, HEAD_DIM)
        value_all = blocks[j, :, kv_width:].reshape(piece_rows, kv_count, HEAD_DIM)
        key_block = jnp.take(key_all, kv_choice, axis=1)
        value_block = jnp.take(value_all, kv_choice, axis=1)
        s = (
            jnp.einsum("hqd,khd->hqk", query_heads, key_block, preferred_element_type=jnp.float32)
            * score_scale
        )
        allowed = (visible[j] == 1) & (clip_ids[:, None] == key_clips[0][None, :])
        s = jnp.where(allowed[None], s, -jnp.inf)
        new_max = jnp.maximum(running_max, jnp.max(s, axis=2))
        p = jnp.exp(s - new_max[:, :, None])
        factor = jnp.exp(running_max - new_max)
        running_total = running_total * factor + jnp.sum(p, axis=2)
        running_acc = running_acc * factor[:, :, None] + jnp.einsum(
            "hqk,khd->hqd", p.astype(jnp.bfloat16), value_block, preferred_element_type=jnp.float32
        )
        running_max = new_max
    result = (running_max, running_total, running_acc)
    final_max, final_total, final_acc = result
    attended = final_acc / final_total[:, :, None]
    attended = (
        jnp.transpose(attended, (1, 0, 2)).reshape(row_count, local_width).astype(jnp.bfloat16)
    )
    partial_sum = jnp.dot(attended, out_weight, preferred_element_type=jnp.float32)[None]
    return lax.psum_scatter(partial_sum.astype(jnp.bfloat16), "mp", scatter_dimension=2, tiled=True)


def solution(mesh):
    in_specs = (
        P("span", "seq", "mp"),
        P("span", "seq", None),
        P("span", "seq", None),
        P("seq"),
        P(),
        P("mp", None),
    )
    out_specs = P("span", "seq", "mp")
    return jax.shard_map(
        on_device, mesh=mesh, in_specs=in_specs, out_specs=out_specs, check_vma=False
    )
```

profile of v0, /device:TPU:6, one launch (start us, length us, event | category | flops | bytes accessed | tf_op | source)
XLA Modules:
  0.0 217.7 jit_solution(18139470743887456620)
XLA Ops:
  6.5 0.0 all-gather.3.cloned.1.call-start
  6.5 0.9 constant_dynamic-update-slice_fusion.1
  7.5 0.9 constant_dynamic-update-slice_fusion
  8.4 4.3 %collective-permute-start.1 = (bf16[64,2048]{1,0:T(8,128)(2,1)S(1)}, bf16[64,2048]{1,0:T(8,128)(2,1)S(1)}, u32[]{:S(2)}, u32[]{:S(2)}) collective-permute-start(bf16[64,2048]{1,0:T(8,128)(2,1)S(1)} %bitcast.145), channel_id=1, source_target_pairs={{0,192},{96,288},{192,384},{288,480},{384,576},{480,672},{1,193},{... | collective-permute-start | bytes 786440 | tf_op jit(solution)/shard_map/ppermute | solution.py:14
  12.7 4.0 %collective-permute-start = (bf16[64,2048]{1,0:T(8,128)(2,1)S(1)}, bf16[64,2048]{1,0:T(8,128)(2,1)S(1)}, u32[]{:S(2)}, u32[]{:S(2)}) collective-permute-start(bf16[64,2048]{1,0:T(8,128)(2,1)S(1)} %bitcast.146), channel_id=1, source_target_pairs={{0,96},{96,192},{192,288},{288,384},{384,480},{480,576},{576,672},... | collective-permute-start | bytes 786440 | tf_op jit(solution)/shard_map/ppermute | solution.py:14
  16.7 3.1 %collective-permute-done.1 = bf16[64,2048]{1,0:T(8,128)(2,1)S(1)} collective-permute-done((bf16[64,2048]{1,0:T(8,128)(2,1)S(1)}, bf16[64,2048]{1,0:T(8,128)(2,1)S(1)}, u32[]{:S(2)}, u32[]{:S(2)}) %collective-permute-start.1) | collective-permute-done | bytes 262176 | tf_op jit(solution)/shard_map/ppermute | solution.py:14
  19.8 4.1 %collective-permute-done = bf16[64,2048]{1,0:T(8,128)(2,1)S(1)} collective-permute-done((bf16[64,2048]{1,0:T(8,128)(2,1)S(1)}, bf16[64,2048]{1,0:T(8,128)(2,1)S(1)}, u32[]{:S(2)}, u32[]{:S(2)}) %collective-permute-start) | collective-permute-done | bytes 262176 | tf_op jit(solution)/shard_map/ppermute | solution.py:14
  23.9 1.0 pad_maximum_fusion
  24.8 0.0 all-gather.3.cloned.1.call-update
  24.9 0.0 reduce-scatter.2.cloned.1.call-start
  25.0 0.9 reshape_squeeze.22
  25.8 1.4 fusion.76
  29.2 1.3 dynamic-slice.3
  31.1 0.9 dynamic-update-slice
  32.0 11.7 %all-reduce = s32[512]{0:T(512)S(1)} all-reduce(s32[512]{0:T(512)S(1)} %dynamic-update-slice), channel_id=2, replica_groups=mesh['span'=8,'seq'=8,'mp'=12] {'seq'}, use_global_device_ids=true, to_apply=%add | all-reduce | flops 512 | bytes 4096
  43.7 0.8 compare_and_fusion
  44.5 60.7 %all-gather.3.cloned.1.call-done = bf16[3,512,2048]{2,1,0:T(8,128)(2,1)} async-done(((bf16[3,64,2048]{2,1,0:T(8,128)(2,1)}), bf16[3,512,2048]{2,1,0:T(8,128)(2,1)}) %all-gather.3.cloned.1.call-update) | async-done | bytes 6291472 | tf_op jit(solution)/shard_map/all_gather | solution.py:44
  105.2 5.0 %fusion.75 = (bf16[1,512,1024]{2,1,0:T(8,128)(2,1)S(1)}, bf16[1,512,1024]{2,1,0:T(8,128)(2,1)}, bf16[1,512,1024]{2,1,0:T(8,128)(2,1)S(1)}, bf16[1,512,1024]{2,1,...) fusion(bf16[3,512,2048]{2,1,0:T(8,128)(2,1)} %all-gather.3.cloned.1.call-done), kind=kLoop, calls=%fused_computation.104 | loop fusion | bytes 12582912 | tf_op jit(solution)/shard_map/slice | solution.py:49
  110.2 2.3 %copy.35 = bf16[1,512,1024]{1,2,0:T(8,128)(2,1)} copy(bf16[1,512,1024]{2,1,0:T(8,128)(2,1)} %get-tuple-element.14) | data formatting | bytes 2097152
  112.5 2.3 %copy.24 = bf16[512,8,128]{2,0,1:T(8,128)(2,1)} copy(bf16[512,8,128]{0,2,1:T(8,128)(2,1)} %bitcast.139) | data formatting | bytes 2097152 | tf_op jit(solution)/shard_map/reshape;squeeze | solution.py:49
  114.8 2.3 %copy.34 = bf16[1,512,1024]{1,2,0:T(8,128)(2,1)} copy(bf16[1,512,1024]{2,1,0:T(8,128)(2,1)} %get-tuple-element.15) | data formatting | bytes 2097152
  117.1 2.3 %copy.21 = bf16[512,8,128]{2,0,1:T(8,128)(2,1)} copy(bf16[512,8,128]{0,2,1:T(8,128)(2,1)} %bitcast.140) | data formatting | bytes 2097152 | tf_op jit(solution)/shard_map/reshape;squeeze | solution.py:48
  119.4 2.6 %gather_fusion.1 = bf16[4,512,128]{2,1,0:T(8,128)(2,1)} fusion(bf16[512,8,128]{2,0,1:T(8,128)(2,1)} %copy.24, s32[1024]{0:T(1024)S(1)} %pad_clamp_fusion), kind=kCustom, calls=%fused_computation.1.clone | custom fusion | bytes 1048592 | tf_op jit(solution)/shard_map/jit(_take)/gather | solution.py:51
  122.0 2.6 %gather_fusion = bf16[4,512,128]{2,1,0:T(8,128)(2,1)} fusion(bf16[512,8,128]{2,0,1:T(8,128)(2,1)} %copy.21, s32[1024]{0:T(1024)S(1)} %pad_clamp_fusion), kind=kCustom, calls=%fused_computation.clone | custom fusion | bytes 1048592 | tf_op jit(solution)/shard_map/jit(_take)/gather | solution.py:50
  124.7 2.3 %copy.38 = bf16[1,512,1024]{1,2,0:T(8,128)(2,1)} copy(bf16[1,512,1024]{2,1,0:T(8,128)(2,1)} %get-tuple-element.11) | data formatting | bytes 2097152
  127.0 2.3 %copy.30 = bf16[512,8,128]{2,0,1:T(8,128)(2,1)} copy(bf16[512,8,128]{0,2,1:T(8,128)(2,1)} %bitcast.141) | data formatting | bytes 2097152 | tf_op jit(solution)/shard_map/reshape;squeeze | solution.py:48
  129.2 2.6 %gather_fusion.4 = bf16[4,512,128]{2,1,0:T(8,128)(2,1)} fusion(bf16[512,8,128]{2,0,1:T(8,128)(2,1)} %copy.30, s32[1024]{0:T(1024)S(1)} %pad_clamp_fusion), kind=kCustom, calls=%fused_computation.4.clone | custom fusion | bytes 1048592 | tf_op jit(solution)/shard_map/jit(_take)/gather | solution.py:50
  131.9 1.3 copy.36
  133.2 1.6 copy.26
  134.8 1.4 gather_fusion.2
  136.2 0.5 copy.37
  136.8 0.7 copy.28
  137.5 1.4 gather_fusion.3
  138.9 0.5 copy.39
  139.4 0.0 slice-start
  139.4 1.3 copy.32
  140.8 0.0 copy-start
  140.8 1.9 gather_fusion.5
  142.7 0.0 copy-start.1
  142.7 1.5 fusion.79
  144.3 1.5 fusion.77
  145.8 0.0 slice-start.1
  145.8 1.6 fusion.78
  147.4 0.2 fusion.37
  147.7 0.3 fusion.33
  148.0 0.0 copy-done
  148.0 0.3 fusion.12
  148.3 0.0 copy-done.1
  148.3 0.3 fusion.10
  148.7 0.3 fusion.14
  149.0 0.0 slice-done
  149.0 0.0 slice-done.1
  149.0 2.1 fusion
  151.1 0.0 reduce-scatter.2.cloned.1.call-update
  151.1 59.8 %reduce-scatter.2.cloned.1.call-done = bf16[1,64,512]{2,1,0:T(8,128)(2,1)} async-done(((bf16[1,64,6144]{2,1,0:T(8,128)(2,1)}), bf16[1,64,512]{2,1,0:T(8,128)(2,1)}) %reduce-scatter.2.cloned.1.call-update) | async-done | bytes 65552 | tf_op jit(solution)/shard_map/reduce_scatter | solution.py:73
  (7 shorter events, 0.1 us)
Async XLA Ops:
  6.5 98.7 %all-gather.3.cloned.1.call-start = ((), (), s32[]{:S(2)}) async-start(), calls=%async_computation.1 | async-start | bytes 7077888 | tf_op jit(solution)/shard_map/all_gather | solution.py:44
  8.4 11.4 %collective-permute-start.1 = (bf16[64,2048]{1,0:T(8,128)(2,1)S(1)}, bf16[64,2048]{1,0:T(8,128)(2,1)S(1)}, u32[]{:S(2)}, u32[]{:S(2)}) collective-permute-start(bf16[64,2048]{1,0:T(8,128)(2,1)S(1)} %bitcast.145), channel_id=1, source_target_pairs={{0,192},{96,288},{192,384},{288,480},{384,576},{480,672},{1,193},{... | collective-permute-start | bytes 786440 | tf_op jit(solution)/shard_map/ppermute | solution.py:14
  12.7 11.2 %collective-permute-start = (bf16[64,2048]{1,0:T(8,128)(2,1)S(1)}, bf16[64,2048]{1,0:T(8,128)(2,1)S(1)}, u32[]{:S(2)}, u32[]{:S(2)}) collective-permute-start(bf16[64,2048]{1,0:T(8,128)(2,1)S(1)} %bitcast.146), channel_id=1, source_target_pairs={{0,96},{96,192},{192,288},{288,384},{384,480},{480,576},{576,672},... | collective-permute-start | bytes 786440 | tf_op jit(solution)/shard_map/ppermute | solution.py:14
  24.9 186.0 %reduce-scatter.2.cloned.1.call-start = ((), (), s32[]{:S(2)}) async-start(), calls=%async_computation.2 | async-start | bytes 851968 | tf_op jit(solution)/shard_map/reduce_scatter | solution.py:73
  139.4 9.5 %slice-start = ((s8[6291456]{0:T(1024)(128)(4,1)}), s8[2097152]{0:T(1024)(128)(4,1)S(1)}, s32[]{:S(2)}) async-start(s8[6291456]{0:T(1024)(128)(4,1)} %bitcast.137), calls=%async_computation.3 | async-start | bytes 4194304
  140.8 7.3 %copy-start = (bf16[4,512,128]{2,1,0:T(8,128)(2,1)S(1)}, bf16[4,512,128]{2,1,0:T(8,128)(2,1)}, u32[]{:S(2)}) copy-start(bf16[4,512,128]{2,1,0:T(8,128)(2,1)} %gather_fusion.1) | copy-start | bytes 1572868
  142.7 5.6 %copy-start.1 = (bf16[4,512,128]{2,1,0:T(8,128)(2,1)S(1)}, bf16[4,512,128]{2,1,0:T(8,128)(2,1)}, u32[]{:S(2)}) copy-start(bf16[4,512,128]{2,1,0:T(8,128)(2,1)} %gather_fusion.3) | copy-start | bytes 1572868
  145.8 3.2 %slice-start.1 = ((s8[6291456]{0:T(1024)(128)(4,1)}), s8[4194304]{0:T(1024)(128)(4,1)S(1)}, s32[]{:S(2)}) async-start(s8[6291456]{0:T(1024)(128)(4,1)} %bitcast.137), calls=%async_computation.4 | async-start | bytes 8388608
Sparse Core Ops, SparseCore 0:
  25.0 80.1 all-gather.2
  151.2 59.5 reduce-scatter.1
where the time goes:
time: 218 us
  waiting for transfers between devices  128 us (59%)
  local copies, waits for them, and re-layouts  43.7 us (20%)
  between operations  16.2 us (7%)
  blocking collectives  11.7 us (5%)
  starting transfers between devices  8.38 us (4%)
  matrix products  7.67 us (4%)
  other arithmetic  2.39 us (1%)
    all_gather x1, waiting for transfers between devices, on_device(): lax.all_gather(jnp.stack(stacked, axis=0), 'seq', axis=1, tiled=True)  60.7 us
    reduce_scatter x1, waiting for transfers between devices, on_device(): lax.psum_scatter(partial_sum.astype(jnp.bfloat16), 'mp', scatter_dimensio...  59.8 us
    unnamed x18, local copies, waits for them, and re-layouts  12.3 us
    unnamed x1, blocking collectives  11.7 us
    ppermute x2, starting transfers between devices, passed_along(): return lax.ppermute(x, axis, pairs)  8.33 us
    ppermute x2, waiting for transfers between devices, passed_along(): return lax.ppermute(x, axis, pairs)  7.15 us
    gather x3, local copies, waits for them, and re-layouts, on_device(): key_block = jnp.take(key_all, kv_choice, axis=1)  6.7 us
    another operation x3, local copies, waits for them, and re-layouts, on_device(): key_all = blocks[j, :, :kv_width].reshape(piece_rows, kv_count, HEAD_DIM)  6.18 us
  transfers between devices with their start and end apart: 4, of which 4 were waited for; matrix products, arithmetic and copies ran while one was open for 2% of the time, Pallas kernels for 0%

commit v1 on v0

v1 whole, which is shorter than its diff:
```python
import jax
import jax.numpy as jnp
from jax import lax
from jax.sharding import PartitionSpec as P

HEAD_DIM = 128
WINDOW = 3
GROUP = 6
KV_SLOTS = 2


def passed_along(x, axis, by):
    size = lax.axis_size(axis)
    pairs = [(i, i + by) for i in range(size) if 0 <= i + by < size]
    return lax.ppermute(x, axis, pairs)


def on_device(queries, keys, values, clip_ids, block_mask, out_weight):
    row_count = queries.shape[1]
    local_width = queries.shape[2]
    head_count = local_width // HEAD_DIM
    kv_count = keys.shape[2] // HEAD_DIM
    score_scale = HEAD_DIM ** (-0.5)
    span_index = lax.axis_index("span")
    first_head = lax.axis_index("mp") * head_count
    first_kv = jnp.minimum(first_head // GROUP, kv_count - KV_SLOTS)
    kv_slot = (first_head + jnp.arange(head_count, dtype=jnp.int32)) // GROUP - first_kv
    kv_start = first_kv * HEAD_DIM
    slot_width = KV_SLOTS * HEAD_DIM
    own_keys = lax.dynamic_slice_in_dim(keys[0], kv_start, slot_width, 1)
    own_values = lax.dynamic_slice_in_dim(values[0], kv_start, slot_width, 1)
    packed = jnp.concatenate([own_keys, own_values], axis=1)
    mask_row = lax.dynamic_index_in_dim(block_mask, span_index, 0, keepdims=False)
    visible = []
    for j in range(WINDOW):
        earlier = span_index - j
        entry = lax.dynamic_index_in_dim(mask_row, jnp.maximum(earlier, 0), 0, keepdims=False)
        visible.append(jnp.where(earlier >= 0, entry, 0))
    stacked = [packed]
    for j in range(1, WINDOW):
        stacked.append(passed_along(packed, "span", j))
    blocks = lax.all_gather(jnp.stack(stacked, axis=0), "seq", axis=1, tiled=True)
    key_clips = lax.all_gather(clip_ids, "seq", axis=0, tiled=True)
    piece_rows = blocks.shape[1]
    window_rows = WINDOW * piece_rows
    kv = blocks.reshape(window_rows, 2, KV_SLOTS, HEAD_DIM)
    key_all = kv[:, 0]
    value_all = kv[:, 1]
    query_heads = queries[0].reshape(row_count, head_count, HEAD_DIM)
    s_both = jnp.einsum(
        "qhd,kad->ahqk", query_heads, key_all, preferred_element_type=jnp.float32
    )
    pick = kv_slot[:, None, None] == 0
    s = jnp.where(pick, s_both[0], s_both[1]) * score_scale
    span_ok = jnp.stack(visible) == 1
    allowed = span_ok[None, :, None] & (clip_ids[:, None, None] == key_clips[None, None, :])
    allowed = allowed.reshape(row_count, window_rows)
    s = jnp.where(allowed[None], s, -jnp.inf)
    top = jnp.max(s, axis=2, keepdims=True)
    p = jnp.exp(s - top)
    total = jnp.sum(p, axis=2, keepdims=True)
    acc_both = jnp.einsum(
        "hqk,kad->ahqd", p.astype(jnp.bfloat16), value_all, preferred_element_type=jnp.float32
    )
    acc = jnp.where(pick, acc_both[0], acc_both[1])
    attended = acc / total
    attended = (
        jnp.transpose(attended, (1, 0, 2)).reshape(row_count, local_width).astype(jnp.bfloat16)
    )
    partial_sum = jnp.dot(attended, out_weight, preferred_element_type=jnp.float32)[None]
    return lax.psum_scatter(partial_sum.astype(jnp.bfloat16), "mp", scatter_dimension=2, tiled=True)


def solution(mesh):
    in_specs = (
        P("span", "seq", "mp"),
        P("span", "seq", None),
        P("span", "seq", None),
        P("seq"),
        P(),
        P("mp", None),
    )
    out_specs = P("span", "seq", "mp")
    return jax.shard_map(
        on_device, mesh=mesh, in_specs=in_specs, out_specs=out_specs, check_vma=False
    )
```

time: 218 us -> 137 us (0.63)
  waiting for transfers between devices: 128 us -> 84.9 us
  local copies, waits for them, and re-layouts: 43.7 us -> 10.4 us
  matrix products: 7.67 us -> 3.34 us
    all_gather x1, waiting for transfers between devices: 60.7 us -> 24.7 us  [on_device(): lax.all_gather(jnp.stack(stacked, axis=0), 'seq', axis=1, tiled=True)]
    gather x6 -> x0, local copies, waits for them, and re-layouts: 12.7 us -> none  [the longest x3 6.7 us: on_device(): key_block = jnp.take(key_all, kv_choice, axis=1)]
    another operation x7 -> x1, local copies, waits for them, and re-layouts: 11.3 us -> 0.86 us  [on_device(): query_heads = queries[0].reshape(row_count, head_count, HEAD_DIM)]
    unnamed x18 -> x8, local copies, waits for them, and re-layouts: 12.3 us -> 3.56 us
    dot_general x6 -> x2, matrix products: 5.59 us -> 1.2 us  [the longest x1 0.62 us: on_device(): jnp.einsum('hqk,kad->ahqd', p.astype(jnp.bfloat16), value_all, preferred_...]
    slice x1, local copies, waits for them, and re-layouts: 5.02 us -> 1.13 us  [on_device(): value_all = kv[:, 1]]
    ppermute x2, waiting for transfers between devices: 7.15 us -> 3.32 us  [passed_along(): return lax.ppermute(x, axis, pairs)]
    reduce_scatter x1, waiting for transfers between devices: 59.8 us -> 56.9 us  [on_device(): lax.psum_scatter(partial_sum.astype(jnp.bfloat16), 'mp', scatter_dimensio...]
  transfers between devices with their start and end apart: 4 -> 4, of which waited for: 4 -> 3; matrix products, arithmetic and copies ran while one was open for 2% -> 4% of each run, Pallas kernels for 0% -> 0%
where the time goes in v1:
time: 137 us
  waiting for transfers between devices  84.9 us (62%)
  between operations  16.2 us (12%)
  blocking collectives  11.7 us (9%)
  local copies, waits for them, and re-layouts  10.4 us (8%)
  starting transfers between devices  7.77 us (6%)
  matrix products  3.34 us (2%)
  other arithmetic  2.58 us (2%)
    reduce_scatter x1, waiting for transfers between devices, on_device(): lax.psum_scatter(partial_sum.astype(jnp.bfloat16), 'mp', scatter_dimensio...  56.9 us
    all_gather x1, waiting for transfers between devices, on_device(): lax.all_gather(jnp.stack(stacked, axis=0), 'seq', axis=1, tiled=True)  24.7 us
    unnamed x1, blocking collectives  11.7 us
    ppermute x2, starting transfers between devices, passed_along(): return lax.ppermute(x, axis, pairs)  7.73 us
    unnamed x8, local copies, waits for them, and re-layouts  3.56 us
    ppermute x2, waiting for transfers between devices, passed_along(): return lax.ppermute(x, axis, pairs)  3.32 us
  transfers between devices with their start and end apart: 4, of which 3 were waited for; matrix products, arithmetic and copies ran while one was open for 4% of the time, Pallas kernels for 0%

profile of v1, /device:TPU:6, one launch (start us, length us, event | category | flops | bytes accessed | tf_op | source)
XLA Modules:
  0.0 136.8 jit_solution(12500659516389806868)
XLA Ops:
  6.5 0.0 all-gather.2.cloned.1.call-start
  6.5 0.8 dynamic-slice_bitcast_fusion
  7.3 3.4 %collective-permute-start = (bf16[64,512]{1,0:T(8,128)(2,1)S(1)}, bf16[64,512]{1,0:T(8,128)(2,1)S(1)}, u32[]{:S(2)}, u32[]{:S(2)}) collective-permute-start(bf16[64,512]{1,0:T(8,128)(2,1)S(1)} %get-tuple-element.8), channel_id=1, source_target_pairs={{0,96},{96,192},{192,288},{288,384},{384,480},{480,576},{576,672},... | collective-permute-start | bytes 196616 | tf_op jit(solution)/shard_map/ppermute | solution.py:15
  10.7 4.3 %collective-permute-start.1 = (bf16[64,512]{1,0:T(8,128)(2,1)S(1)}, bf16[64,512]{1,0:T(8,128)(2,1)S(1)}, u32[]{:S(2)}, u32[]{:S(2)}) collective-permute-start(bf16[64,512]{1,0:T(8,128)(2,1)S(1)} %get-tuple-element.8), channel_id=1, source_target_pairs={{0,192},{96,288},{192,384},{288,480},{384,576},{480,672},{1,193},{... | collective-permute-start | bytes 196616 | tf_op jit(solution)/shard_map/ppermute | solution.py:15
  15.1 0.0 collective-permute-done
  15.1 3.3 %collective-permute-done.1 = bf16[64,512]{1,0:T(8,128)(2,1)S(1)} collective-permute-done((bf16[64,512]{1,0:T(8,128)(2,1)S(1)}, bf16[64,512]{1,0:T(8,128)(2,1)S(1)}, u32[]{:S(2)}, u32[]{:S(2)}) %collective-permute-start.1) | collective-permute-done | bytes 65568 | tf_op jit(solution)/shard_map/ppermute | solution.py:15
  18.4 0.7 pad_maximum_fusion
  19.1 0.0 all-gather.2.cloned.1.call-update
  19.1 0.0 reduce-scatter.2.cloned.1.call-start
  19.2 0.9 reshape_squeeze.3
  20.1 1.5 %fusion.23 = (s32[1,1]{1,0:T(1,128)}, s32[1,1]{1,0:T(1,128)}, s32[1,1]{1,0:T(1,128)}) fusion(s32[8,8]{1,0:T(8,128)} %param.10, s32[]{:T(128)S(6)} %select_n.60, s32[]{:T(128)S(6)} %max.16, s32[]{:T(128)S(6)} %max.20, s32[]{:T(128)S(6)} %max.18), kind=kLoop, calls=%fused_computation.41 | loop fusion | bytes 40 | tf_op jit(solution)/shard_map/jit(dynamic_index_in_dim)/dynamic_slice | solution.py:37
  23.5 0.1 add_compare_fusion
  23.6 0.1 and.38
  23.7 1.3 dynamic-slice.5
  25.6 0.9 dynamic-update-slice
  26.5 11.7 %all-reduce = s32[512]{0:T(512)S(1)} all-reduce(s32[512]{0:T(512)S(1)} %dynamic-update-slice), channel_id=1, replica_groups=mesh['span'=8,'seq'=8,'mp'=12] {'seq'}, use_global_device_ids=true, to_apply=%add | all-reduce | flops 512 | bytes 4096
  38.2 0.7 broadcast_compare_fusion
  38.9 0.1 and.41
  39.0 0.1 copy.17
  39.1 0.1 broadcast_and_fusion
  39.2 24.7 %all-gather.2.cloned.1.call-done = bf16[3,512,512]{2,1,0:T(8,128)(2,1)} async-done(((bf16[3,64,512]{2,1,0:T(8,128)(2,1)}), bf16[3,512,512]{2,1,0:T(8,128)(2,1)}) %all-gather.2.cloned.1.call-update) | async-done | bytes 1572880 | tf_op jit(solution)/shard_map/all_gather | solution.py:42
  63.9 2.4 %reshape.104 = bf16[1536,2,2,128]{3,2,1,0:T(2,128)(2,1)S(1)} reshape(bf16[3,512,512]{2,1,0:T(8,128)(2,1)} %all-gather.2.cloned.1.call-done) | data formatting | bytes 3145728 | tf_op jit(solution)/shard_map/reshape | solution.py:46
  66.3 1.1 fusion.22
  67.4 0.6 convolution_bitcast_fusion
  68.0 0.0 slice-start
  68.0 0.4 fusion.21
  68.4 0.0 slice-start.1
  68.4 0.5 exponential_reduce_fusion
  69.0 0.6 convolution_bitcast_fusion.1
  69.6 0.6 slice-done
  70.2 0.8 slice-done.1
  71.0 2.1 %fusion = bf16[1,64,6144]{2,1,0:T(8,128)(2,1)} fusion(bf16[512,6144]{1,0:T(8,128)(2,1)S(1)} %bitcast.88, f32[4,64]{1,0:T(4,128)S(1)} %exponential_reduce_fusion, f32[2,4,64,128]{3,2,1,0:T(8,128)S(1)} %convolution_bitcast_fusion.1, pred[4]{0:T(512)(128)(4,1)S(1)} %subtract_compare_fusion), kind=kOutput, calls=%fused_computation.1 | convolution fusion | flops 403144704 | bytes 7341060 | tf_op jit(solution)/shard_map/dot_general | solution.py:70
  73.1 0.0 reduce-scatter.2.cloned.1.call-update
  73.1 56.9 %reduce-scatter.2.cloned.1.call-done = bf16[1,64,512]{2,1,0:T(8,128)(2,1)} async-done(((bf16[1,64,6144]{2,1,0:T(8,128)(2,1)}), bf16[1,64,512]{2,1,0:T(8,128)(2,1)}) %reduce-scatter.2.cloned.1.call-update) | async-done | bytes 65552 | tf_op jit(solution)/shard_map/reduce_scatter | solution.py:71
  (5 shorter events, 0.1 us)
Async XLA Ops:
  6.5 57.4 %all-gather.2.cloned.1.call-start = ((), (), s32[]{:S(2)}) async-start(), calls=%async_computation.1 | async-start | bytes 1769472 | tf_op jit(solution)/shard_map/all_gather | solution.py:42
  7.3 7.7 %collective-permute-start = (bf16[64,512]{1,0:T(8,128)(2,1)S(1)}, bf16[64,512]{1,0:T(8,128)(2,1)S(1)}, u32[]{:S(2)}, u32[]{:S(2)}) collective-permute-start(bf16[64,512]{1,0:T(8,128)(2,1)S(1)} %get-tuple-element.8), channel_id=1, source_target_pairs={{0,96},{96,192},{192,288},{288,384},{384,480},{480,576},{576,672},... | collective-permute-start | bytes 196616 | tf_op jit(solution)/shard_map/ppermute | solution.py:15
  10.7 7.7 %collective-permute-start.1 = (bf16[64,512]{1,0:T(8,128)(2,1)S(1)}, bf16[64,512]{1,0:T(8,128)(2,1)S(1)}, u32[]{:S(2)}, u32[]{:S(2)}) collective-permute-start(bf16[64,512]{1,0:T(8,128)(2,1)S(1)} %get-tuple-element.8), channel_id=1, source_target_pairs={{0,192},{96,288},{192,384},{288,480},{384,576},{480,672},{1,193},{... | collective-permute-start | bytes 196616 | tf_op jit(solution)/shard_map/ppermute | solution.py:15
  19.1 110.9 %reduce-scatter.2.cloned.1.call-start = ((), (), s32[]{:S(2)}) async-start(), calls=%async_computation.2 | async-start | bytes 851968 | tf_op jit(solution)/shard_map/reduce_scatter | solution.py:71
  68.0 2.2 %slice-start = ((s8[6291456]{0:T(1024)(128)(4,1)}), s8[4194304]{0:T(1024)(128)(4,1)S(1)}, s32[]{:S(2)}) async-start(s8[6291456]{0:T(1024)(128)(4,1)} %bitcast.87), calls=%async_computation.3 | async-start | bytes 8388608
  68.4 2.5 %slice-start.1 = ((s8[6291456]{0:T(1024)(128)(4,1)}), s8[2097152]{0:T(1024)(128)(4,1)S(1)}, s32[]{:S(2)}) async-start(s8[6291456]{0:T(1024)(128)(4,1)} %bitcast.87), calls=%async_computation.4 | async-start | bytes 4194304
Sparse Core Ops, SparseCore 0:
  19.3 44.5 all-gather.1
  73.3 56.6 reduce-scatter.1

commit v2 on v1

--- a/solution.py
+++ b/solution.py
@@ -7,6 +7,7 @@
 WINDOW = 3
 GROUP = 6
 KV_SLOTS = 2
+CLIP_PAD = 16
 
 
 def passed_along(x, axis, by):
@@ -39,11 +40,17 @@
     stacked = [packed]
     for j in range(1, WINDOW):
         stacked.append(passed_along(packed, "span", j))
-    blocks = lax.all_gather(jnp.stack(stacked, axis=0), "seq", axis=1, tiled=True)
-    key_clips = lax.all_gather(clip_ids, "seq", axis=0, tiled=True)
-    piece_rows = blocks.shape[1]
+    clip_row = jnp.zeros((CLIP_PAD, packed.shape[1]), jnp.bfloat16)
+    clip_row = clip_row.at[0, :row_count].set(clip_ids.astype(jnp.bfloat16))
+    outgoing = jnp.concatenate(stacked + [clip_row], axis=0)
+    seq_count = lax.axis_size("seq")
+    outgoing = jnp.broadcast_to(outgoing[None], (seq_count,) + outgoing.shape)
+    gathered = lax.all_to_all(outgoing, "seq", 0, 0, tiled=True)
+    kv_rows = gathered[:, : WINDOW * row_count].reshape(seq_count, WINDOW, row_count, -1)
+    key_clips = gathered[:, WINDOW * row_count, :row_count].reshape(-1)
+    piece_rows = seq_count * row_count
     window_rows = WINDOW * piece_rows
-    kv = blocks.reshape(window_rows, 2, KV_SLOTS, HEAD_DIM)
+    kv = jnp.transpose(kv_rows, (1, 0, 2, 3)).reshape(window_rows, 2, KV_SLOTS, HEAD_DIM)
     key_all = kv[:, 0]
     value_all = kv[:, 1]
     query_heads = queries[0].reshape(row_count, head_count, HEAD_DIM)
@@ -53,7 +60,8 @@
     pick = kv_slot[:, None, None] == 0
     s = jnp.where(pick, s_both[0], s_both[1]) * score_scale
     span_ok = jnp.stack(visible) == 1
-    allowed = span_ok[None, :, None] & (clip_ids[:, None, None] == key_clips[None, None, :])
+    query_clips = clip_ids.astype(jnp.bfloat16)
+    allowed = span_ok[None, :, None] & (query_clips[:, None, None] == key_clips[None, None, :])
     allowed = allowed.reshape(row_count, window_rows)
     s = jnp.where(allowed[None], s, -jnp.inf)
     top = jnp.max(s, axis=2, keepdims=True)
@@ -67,8 +75,15 @@
     attended = (
         jnp.transpose(attended, (1, 0, 2)).reshape(row_count, local_width).astype(jnp.bfloat16)
     )
-    partial_sum = jnp.dot(attended, out_weight, preferred_element_type=jnp.float32)[None]
-    return lax.psum_scatter(partial_sum.astype(jnp.bfloat16), "mp", scatter_dimension=2, tiled=True)
+    mp_count = lax.axis_size("mp")
+    out_width = out_weight.shape[1] // mp_count
+    weight_parts = out_weight.reshape(local_width, mp_count, out_width)
+    partial_sum = jnp.einsum(
+        "qi,icj->cqj", attended, weight_parts, preferred_element_type=jnp.float32
+    ).astype(jnp.bfloat16)
+    received = lax.all_to_all(partial_sum, "mp", 0, 0, tiled=True)
+    projected = jnp.sum(received.astype(jnp.float32), axis=0)
+    return projected.astype(jnp.bfloat16)[None]
 
 
 def solution(mesh):

time: 137 us -> 120 us (0.88); the launches traced: 137 us -> 118 us
  waiting for transfers between devices: 84.9 us -> 30.2 us
  blocking collectives: 11.7 us -> 47.3 us
  between operations: 16.2 us -> 2.1 us
  starting transfers between devices: 7.77 us -> 14.7 us
  local copies, waits for them, and re-layouts: 10.4 us -> 14.5 us
  matrix products: 3.34 us -> 5.97 us
    reduce_scatter x1 -> x0, waiting for transfers between devices: 56.9 us -> none  [on_device(): lax.psum_scatter(partial_sum.astype(jnp.bfloat16), 'mp', scatter_dimensio...]
    all_to_all x0 -> x1, blocking collectives: none -> 47.3 us  [on_device(): received = lax.all_to_all(partial_sum, 'mp', 0, 0, tiled=True)]
    all_to_all x0 -> x1, waiting for transfers between devices: none -> 28.7 us  [on_device(): gathered = lax.all_to_all(outgoing, 'seq', 0, 0, tiled=True)]
    all_gather x1 -> x0, waiting for transfers between devices: 24.7 us -> none  [on_device(): lax.all_gather(jnp.stack(stacked, axis=0), 'seq', axis=1, tiled=True)]
    unnamed x1 -> x0, blocking collectives: 11.7 us -> none
    all_to_all x0 -> x1, starting transfers between devices: none -> 6.33 us  [on_device(): gathered = lax.all_to_all(outgoing, 'seq', 0, 0, tiled=True)]
    unnamed x8 -> x4, local copies, waits for them, and re-layouts: 3.56 us -> 8.75 us
    dot_general x1, matrix products: 2.15 us -> 4.78 us  [on_device(): jnp.einsum('qi,icj->cqj', attended, weight_parts, preferred_element_type=...]
  transfers between devices with their start and end apart: 4 -> 3, of which waited for: 3 -> 2; matrix products, arithmetic and copies ran while one was open for 4% -> 9% of each run, Pallas kernels for 0% -> 0%
where the time goes in v2:
time: 120 us; the launch traced here: 118 us
  blocking collectives  47.3 us (39%)
  waiting for transfers between devices  30.2 us (25%)
  starting transfers between devices  14.7 us (12%)
  local copies, waits for them, and re-layouts  14.5 us (12%)
  matrix products  5.97 us (5%)
  other arithmetic  2.75 us (2%)
  between operations  2.1 us (2%)
    all_to_all x1, blocking collectives, on_device(): received = lax.all_to_all(partial_sum, 'mp', 0, 0, tiled=True)  47.3 us
    all_to_all x1, waiting for transfers between devices, on_device(): gathered = lax.all_to_all(outgoing, 'seq', 0, 0, tiled=True)  28.7 us
    unnamed x4, local copies, waits for them, and re-layouts  8.75 us
    ppermute x2, starting transfers between devices, passed_along(): return lax.ppermute(x, axis, pairs)  8.33 us
    all_to_all x1, starting transfers between devices, on_device(): gathered = lax.all_to_all(outgoing, 'seq', 0, 0, tiled=True)  6.33 us
    dot_general x1, matrix products, on_device(): jnp.einsum('qi,icj->cqj', attended, weight_parts, preferred_element_type=...  4.78 us
  transfers between devices with their start and end apart: 3, of which 2 were waited for; matrix products, arithmetic and copies ran while one was open for 9% of the time, Pallas kernels for 0%

profile of v2, /device:TPU:6, one launch (start us, length us, event | category | flops | bytes accessed | tf_op | source)
XLA Modules:
  0.0 117.6 jit_solution(2200661575820015582)
XLA Ops:
  0.0 0.8 dynamic-slice_bitcast_fusion
  0.8 4.3 %collective-permute-start.1 = (bf16[64,512]{1,0:T(8,128)(2,1)S(1)}, bf16[64,512]{1,0:T(8,128)(2,1)S(1)}, u32[]{:S(2)}, u32[]{:S(2)}) collective-permute-start(bf16[64,512]{1,0:T(8,128)(2,1)S(1)} %pad_maximum_fusion), channel_id=1, source_target_pairs={{0,192},{96,288},{192,384},{288,480},{384,576},{480,672},{1,193},{... | collective-permute-start | bytes 196616 | tf_op jit(solution)/shard_map/ppermute | solution.py:16
  5.1 4.0 %collective-permute-start = (bf16[64,512]{1,0:T(8,128)(2,1)S(1)}, bf16[64,512]{1,0:T(8,128)(2,1)S(1)}, u32[]{:S(2)}, u32[]{:S(2)}) collective-permute-start(bf16[64,512]{1,0:T(8,128)(2,1)S(1)} %pad_maximum_fusion), channel_id=1, source_target_pairs={{0,96},{96,192},{192,288},{288,384},{384,480},{480,576},{576,672},... | collective-permute-start | bytes 196616 | tf_op jit(solution)/shard_map/ppermute | solution.py:16
  9.1 0.7 fusion.23
  9.8 0.0 collective-permute-done.1
  9.8 1.5 %collective-permute-done = bf16[64,512]{1,0:T(8,128)(2,1)S(1)} collective-permute-done((bf16[64,512]{1,0:T(8,128)(2,1)S(1)}, bf16[64,512]{1,0:T(8,128)(2,1)S(1)}, u32[]{:S(2)}, u32[]{:S(2)}) %collective-permute-start) | collective-permute-done | bytes 65568 | tf_op jit(solution)/shard_map/ppermute | solution.py:16
  11.3 1.3 %broadcast_in_dim.50 = bf16[8,208,512]{2,1,0:T(8,128)(2,1)} broadcast(bf16[208,512]{1,0:T(8,128)(2,1)S(1)} %fusion.11), dimensions={1,2} | broadcast | bytes 1916928 | tf_op jit(solution)/shard_map/broadcast_in_dim | solution.py:47
  12.6 0.0 copy-start
  12.6 6.3 %all-to-all-start = ((bf16[8,208,512]{2,1,0:T(8,128)(2,1)}), bf16[8,208,512]{2,1,0:T(8,128)(2,1)S(1)}, u32[]{:S(2)}, u32[]{:S(2)}) async-start(bf16[8,208,512]{2,1,0:T(8,128)(2,1)} %broadcast_in_dim.50), calls=%async_computation | async-start | bytes 3407872 | tf_op jit(solution)/shard_map/all_to_all | solution.py:48
  19.0 1.5 %fusion.22 = (s32[1,1]{1,0:T(1,128)}, s32[1,1]{1,0:T(1,128)}, s32[1,1]{1,0:T(1,128)}) fusion(s32[8,8]{1,0:T(8,128)} %param.12, s32[]{:T(128)S(6)} %select_n.60, s32[]{:T(128)S(6)} %max.16, s32[]{:T(128)S(6)} %max.20, s32[]{:T(128)S(6)} %max.18), kind=kLoop, calls=%fused_computation.43 | loop fusion | bytes 40 | tf_op jit(solution)/shard_map/jit(dynamic_index_in_dim)/dynamic_slice | solution.py:38
  22.4 0.1 add_compare_fusion
  22.5 0.1 and.41
  22.6 0.0 copy-done
  22.6 8.7 %copy.21 = bf16[512,6144]{0,1:T(8,128)(2,1)} copy(bf16[512,6144]{1,0:T(8,128)(2,1)} %param.13) | data formatting | bytes 12582912 | tf_op args[5]
  31.3 28.7 %all-to-all-done = bf16[8,208,512]{2,1,0:T(8,128)(2,1)S(1)} async-done(((bf16[8,208,512]{2,1,0:T(8,128)(2,1)}), bf16[8,208,512]{2,1,0:T(8,128)(2,1)S(1)}, u32[]{:S(2)}, u32[]{:S(2)}) %all-to-all-start) | async-done | bytes 1703968 | tf_op jit(solution)/shard_map/all_to_all | solution.py:48
  60.1 0.1 eq.38
  60.2 0.1 slice.48
  60.3 0.1 copy.38
  60.4 0.4 reshape.145
  60.8 1.1 fusion.21
  62.0 0.1 broadcast_compare_fusion
  62.1 0.1 and.44
  62.2 0.1 copy.28
  62.2 0.1 broadcast_and_fusion
  62.3 0.6 convolution_bitcast_fusion
  62.9 0.4 fusion.20
  63.3 0.5 exponential_reduce_fusion
  63.9 0.6 convolution_bitcast_fusion.1
  64.5 0.1 fusion.17
  64.6 0.1 copy.20
  64.7 4.8 %fusion.2 = bf16[12,64,512]{2,1,0:T(8,128)(2,1)S(1)} fusion(bf16[64,512,1]{1,0,2:T(8,128)(2,1)S(1)} %reshape.151, bf16[512,12,512]{0,2,1:T(8,128)(2,1)} %bitcast.83), kind=kOutput, calls=%fused_computation.8 | convolution fusion | flops 403046400 | bytes 7143424 | tf_op jit(solution)/shard_map/qi,icj->cqj/dot_general | solution.py:81
  69.5 47.3 %all_to_all.10 = bf16[12,64,512]{2,1,0:T(8,128)(2,1)S(1)} all-to-all(bf16[12,64,512]{2,1,0:T(8,128)(2,1)S(1)} %fusion.2), channel_id=1, replica_groups=mesh['span'=8,'seq'=8,'mp'=12] {'mp'}, dimensions={0} | all-to-all | bytes 1572864 | tf_op jit(solution)/shard_map/all_to_all | solution.py:84
  116.8 0.7 reduce_sum.22
  (7 shorter events, 0.1 us)
Async XLA Ops:
  0.8 9.0 %collective-permute-start.1 = (bf16[64,512]{1,0:T(8,128)(2,1)S(1)}, bf16[64,512]{1,0:T(8,128)(2,1)S(1)}, u32[]{:S(2)}, u32[]{:S(2)}) collective-permute-start(bf16[64,512]{1,0:T(8,128)(2,1)S(1)} %pad_maximum_fusion), channel_id=1, source_target_pairs={{0,192},{96,288},{192,384},{288,480},{384,576},{480,672},{1,193},{... | collective-permute-start | bytes 196616 | tf_op jit(solution)/shard_map/ppermute | solution.py:16
  5.1 6.2 %collective-permute-start = (bf16[64,512]{1,0:T(8,128)(2,1)S(1)}, bf16[64,512]{1,0:T(8,128)(2,1)S(1)}, u32[]{:S(2)}, u32[]{:S(2)}) collective-permute-start(bf16[64,512]{1,0:T(8,128)(2,1)S(1)} %pad_maximum_fusion), channel_id=1, source_target_pairs={{0,96},{96,192},{192,288},{288,384},{384,480},{480,576},{576,672},... | collective-permute-start | bytes 196616 | tf_op jit(solution)/shard_map/ppermute | solution.py:16
  12.6 10.0 %copy-start = (bf16[1,64,512]{2,1,0:T(8,128)(2,1)S(1)}, bf16[1,64,512]{2,1,0:T(8,128)(2,1)}, u32[]{:S(2)}) copy-start(bf16[1,64,512]{2,1,0:T(8,128)(2,1)} %param.8) | copy-start | bytes 196612
  12.6 47.4 %all-to-all-start = ((bf16[8,208,512]{2,1,0:T(8,128)(2,1)}), bf16[8,208,512]{2,1,0:T(8,128)(2,1)S(1)}, u32[]{:S(2)}, u32[]{:S(2)}) async-start(bf16[8,208,512]{2,1,0:T(8,128)(2,1)} %broadcast_in_dim.50), calls=%async_computation | async-start | bytes 3407872 | tf_op jit(solution)/shard_map/all_to_all | solution.py:48

commit v3 on v2

--- a/solution.py
+++ b/solution.py
@@ -44,8 +44,13 @@
     clip_row = clip_row.at[0, :row_count].set(clip_ids.astype(jnp.bfloat16))
     outgoing = jnp.concatenate(stacked + [clip_row], axis=0)
     seq_count = lax.axis_size("seq")
-    outgoing = jnp.broadcast_to(outgoing[None], (seq_count,) + outgoing.shape)
-    gathered = lax.all_to_all(outgoing, "seq", 0, 0, tiled=True)
+    held = [outgoing]
+    for shift in range(2, seq_count, 2):
+        pairs = [(i, (i + shift) % seq_count) for i in range(seq_count)]
+        held.append(lax.ppermute(outgoing, "seq", pairs))
+    held = jnp.stack(held, axis=0)
+    partner = lax.ppermute(held, "seq", [(i, i ^ 1) for i in range(seq_count)])
+    gathered = jnp.concatenate([held, partner], axis=0)
     kv_rows = gathered[:, : WINDOW * row_count].reshape(seq_count, WINDOW, row_count, -1)
     key_clips = gathered[:, WINDOW * row_count, :row_count].reshape(-1)
     piece_rows = seq_count * row_count
@@ -77,10 +82,10 @@
     )
     mp_count = lax.axis_size("mp")
     out_width = out_weight.shape[1] // mp_count
-    weight_parts = out_weight.reshape(local_width, mp_count, out_width)
-    partial_sum = jnp.einsum(
-        "qi,icj->cqj", attended, weight_parts, preferred_element_type=jnp.float32
-    ).astype(jnp.bfloat16)
+    partial_sum = jnp.dot(attended, out_weight, preferred_element_type=jnp.float32)
+    partial_sum = jnp.transpose(
+        partial_sum.astype(jnp.bfloat16).reshape(row_count, mp_count, out_width), (1, 0, 2)
+    )
     received = lax.all_to_all(partial_sum, "mp", 0, 0, tiled=True)
     projected = jnp.sum(received.astype(jnp.float32), axis=0)
     return projected.astype(jnp.bfloat16)[None]

time: 120 us -> 102 us (0.85)
  the two profiles are of different devices: /device:TPU:6 before, /device:TPU:60 now
where the time goes in v3:
time: 102 us; the launch traced here: 101 us
  blocking collectives  47.6 us (47%)
  waiting for transfers between devices  19.5 us (19%)
  starting transfers between devices  19 us (19%)
  local copies, waits for them, and re-layouts  8.06 us (8%)
  other arithmetic  2.76 us (3%)
  matrix products  2.45 us (2%)
  between operations  2.06 us (2%)
    all_to_all x1, blocking collectives, on_device(): received = lax.all_to_all(partial_sum, 'mp', 0, 0, tiled=True)  47.6 us
    ppermute x3, waiting for transfers between devices, on_device(): held.append(lax.ppermute(outgoing, 'seq', pairs))  13.4 us
    ppermute x3, starting transfers between devices, on_device(): held.append(lax.ppermute(outgoing, 'seq', pairs))  12.7 us
    ppermute x2, starting transfers between devices, passed_along(): return lax.ppermute(x, axis, pairs)  4.4 us
    ppermute x2, waiting for transfers between devices, passed_along(): return lax.ppermute(x, axis, pairs)  3.91 us
    ppermute x1, waiting for transfers between devices, on_device(): partner = lax.ppermute(held, 'seq', [(i, i ^ 1) for i in range(seq_count)])  2.17 us
  transfers between devices with their start and end apart: 6, of which 6 were waited for; matrix products, arithmetic and copies ran while one was open for 2% of the time, Pallas kernels for 0%

profile of v3, /device:TPU:60, one launch (start us, length us, event | category | flops | bytes accessed | tf_op | source)
XLA Modules:
  0.0 101.4 jit_solution(18415553773150654859)
XLA Ops:
  0.0 0.0 copy-start
  0.0 0.8 dynamic-slice_bitcast_fusion
  0.8 1.3 %collective-permute-start.1 = (bf16[64,512]{1,0:T(8,128)(2,1)S(1)}, bf16[64,512]{1,0:T(8,128)(2,1)S(1)}, u32[]{:S(2)}, u32[]{:S(2)}) collective-permute-start(bf16[64,512]{1,0:T(8,128)(2,1)S(1)} %pad_maximum_fusion.1), channel_id=1, source_target_pairs={{0,192},{96,288},{192,384},{288,480},{384,576},{480,672},{1,193},{... | collective-permute-start | bytes 196616 | tf_op jit(solution)/shard_map/ppermute | solution.py:16
  2.1 3.1 %collective-permute-start = (bf16[64,512]{1,0:T(8,128)(2,1)S(1)}, bf16[64,512]{1,0:T(8,128)(2,1)S(1)}, u32[]{:S(2)}, u32[]{:S(2)}) collective-permute-start(bf16[64,512]{1,0:T(8,128)(2,1)S(1)} %pad_maximum_fusion.1), channel_id=1, source_target_pairs={{0,96},{96,192},{192,288},{288,384},{384,480},{480,576},{576,672},... | collective-permute-start | bytes 196616 | tf_op jit(solution)/shard_map/ppermute | solution.py:16
  5.2 0.7 fusion.25
  5.9 2.7 %collective-permute-done.1 = bf16[64,512]{1,0:T(8,128)(2,1)S(1)} collective-permute-done((bf16[64,512]{1,0:T(8,128)(2,1)S(1)}, bf16[64,512]{1,0:T(8,128)(2,1)S(1)}, u32[]{:S(2)}, u32[]{:S(2)}) %collective-permute-start.1) | collective-permute-done | bytes 65568 | tf_op jit(solution)/shard_map/ppermute | solution.py:16
  8.6 1.2 %collective-permute-done = bf16[64,512]{1,0:T(8,128)(2,1)S(1)} collective-permute-done((bf16[64,512]{1,0:T(8,128)(2,1)S(1)}, bf16[64,512]{1,0:T(8,128)(2,1)S(1)}, u32[]{:S(2)}, u32[]{:S(2)}) %collective-permute-start) | collective-permute-done | bytes 65568 | tf_op jit(solution)/shard_map/ppermute | solution.py:16
  9.8 4.0 %collective-permute-start.4 = (bf16[208,512]{1,0:T(8,128)(2,1)S(1)}, bf16[208,512]{1,0:T(8,128)(2,1)S(1)}, u32[]{:S(2)}, u32[]{:S(2)}) collective-permute-start(bf16[208,512]{1,0:T(8,128)(2,1)S(1)} %get-tuple-element.18), channel_id=1, source_target_pairs={{0,72},{12,84},{24,0},{36,12},{48,24},{60,36},{72,48},{84,60},{1,7... | collective-permute-start | bytes 638984 | tf_op jit(solution)/shard_map/ppermute | solution.py:50
  13.9 2.9 %collective-permute-start.3 = (bf16[208,512]{1,0:T(8,128)(2,1)S(1)}, bf16[208,512]{1,0:T(8,128)(2,1)S(1)}, u32[]{:S(2)}, u32[]{:S(2)}) collective-permute-start(bf16[208,512]{1,0:T(8,128)(2,1)S(1)} %get-tuple-element.18), channel_id=1, source_target_pairs={{0,48},{12,60},{24,72},{36,84},{48,0},{60,12},{72,24},{84,36},{1,4... | collective-permute-start | bytes 638984 | tf_op jit(solution)/shard_map/ppermute | solution.py:50
  16.8 5.7 %collective-permute-start.2 = (bf16[208,512]{1,0:T(8,128)(2,1)S(1)}, bf16[208,512]{1,0:T(8,128)(2,1)S(1)}, u32[]{:S(2)}, u32[]{:S(2)}) collective-permute-start(bf16[208,512]{1,0:T(8,128)(2,1)S(1)} %get-tuple-element.18), channel_id=1, source_target_pairs={{0,24},{12,36},{24,48},{36,60},{48,72},{60,84},{72,0},{84,12},{1,2... | collective-permute-start | bytes 638984 | tf_op jit(solution)/shard_map/ppermute | solution.py:50
  22.6 1.4 %fusion.24 = (s32[1,1]{1,0:T(1,128)}, s32[1,1]{1,0:T(1,128)}, s32[1,1]{1,0:T(1,128)}) fusion(s32[8,8]{1,0:T(8,128)} %param.12, s32[]{:T(128)S(6)} %select_n.60, s32[]{:T(128)S(6)} %max.16, s32[]{:T(128)S(6)} %max.20, s32[]{:T(128)S(6)} %max.18), kind=kLoop, calls=%fused_computation.50 | loop fusion | bytes 40 | tf_op jit(solution)/shard_map/jit(dynamic_index_in_dim)/dynamic_slice | solution.py:38
  25.8 1.9 %collective-permute-done.4 = bf16[208,512]{1,0:T(8,128)(2,1)S(1)} collective-permute-done((bf16[208,512]{1,0:T(8,128)(2,1)S(1)}, bf16[208,512]{1,0:T(8,128)(2,1)S(1)}, u32[]{:S(2)}, u32[]{:S(2)}) %collective-permute-start.4) | collective-permute-done | bytes 213024 | tf_op jit(solution)/shard_map/ppermute | solution.py:50
  27.7 2.3 %collective-permute-done.3 = bf16[208,512]{1,0:T(8,128)(2,1)S(1)} collective-permute-done((bf16[208,512]{1,0:T(8,128)(2,1)S(1)}, bf16[208,512]{1,0:T(8,128)(2,1)S(1)}, u32[]{:S(2)}, u32[]{:S(2)}) %collective-permute-start.3) | collective-permute-done | bytes 213024 | tf_op jit(solution)/shard_map/ppermute | solution.py:50
  30.0 9.2 %collective-permute-done.2 = bf16[208,512]{1,0:T(8,128)(2,1)S(1)} collective-permute-done((bf16[208,512]{1,0:T(8,128)(2,1)S(1)}, bf16[208,512]{1,0:T(8,128)(2,1)S(1)}, u32[]{:S(2)}, u32[]{:S(2)}) %collective-permute-start.2) | collective-permute-done | bytes 213024 | tf_op jit(solution)/shard_map/ppermute | solution.py:50
  39.2 0.1 pad_maximum_fusion
  39.3 1.9 %collective-permute-start.5 = (bf16[4,208,512]{2,1,0:T(8,128)(2,1)S(1)}, bf16[4,208,512]{2,1,0:T(8,128)(2,1)}, u32[]{:S(2)}, u32[]{:S(2)}) collective-permute-start(bf16[4,208,512]{2,1,0:T(8,128)(2,1)S(1)} %pad_maximum_fusion), channel_id=1, source_target_pairs={{0,12},{12,0},{24,36},{36,24},{48,60},{60,48},{72,84},{84,72},{1,1... | collective-permute-start | bytes 2555912 | tf_op jit(solution)/shard_map/ppermute | solution.py:52
  41.2 0.1 add_compare_fusion
  41.3 0.1 and.41
  41.4 0.0 copy-done
  41.5 2.2 %collective-permute-done.5 = bf16[4,208,512]{2,1,0:T(8,128)(2,1)} collective-permute-done((bf16[4,208,512]{2,1,0:T(8,128)(2,1)S(1)}, bf16[4,208,512]{2,1,0:T(8,128)(2,1)}, u32[]{:S(2)}, u32[]{:S(2)}) %collective-permute-start.5) | collective-permute-done | bytes 852000 | tf_op jit(solution)/shard_map/ppermute | solution.py:52
  43.7 1.2 %constant_dynamic-update-slice_fusion = bf16[8,208,512]{2,1,0:T(8,128)(2,1)S(1)} fusion(bf16[8,208,512]{2,1,0:T(8,128)(2,1)S(1)} %constant_dynamic-update-slice_fusion.1, bf16[4,208,512]{2,1,0:T(8,128)(2,1)} %collective-permute-done.5), kind=kLoop, calls=%fused_computation.36 | loop fusion | bytes 1703936 | tf_op jit(solution)/shard_map/concatenate | solution.py:53
  45.0 0.1 slice.48
  45.1 0.1 eq.38
  45.2 0.1 copy.49
  45.3 0.4 reshape.144
  45.8 1.1 %fusion.23 = (bf16[1536,1,2,128]{3,2,1,0:T(2,128)(2,1)S(1)}, bf16[1536,1,2,128]{3,2,1,0:T(2,128)(2,1)S(1)}) fusion(bf16[1536,2,2,128]{3,2,1,0:T(2,128)(2,1)S(1)} %reshape.144), kind=kLoop, calls=%fused_computation.49 | loop fusion | bytes 3145728 | tf_op jit(solution)/shard_map/slice | solution.py:60
  46.9 0.1 broadcast_compare_fusion
  47.0 0.1 and.44
  47.1 0.1 copy.35
  47.2 0.1 broadcast_and_fusion
  47.3 0.6 convolution_bitcast_fusion
  47.8 0.0 slice-start
  47.8 0.4 fusion.21
  48.3 0.0 slice-start.1
  48.3 0.5 exponential_reduce_fusion
  48.8 0.6 convolution_bitcast_fusion.1
  49.4 0.6 slice-done
  50.0 0.8 slice-done.1
  50.8 1.3 %convolution_convert_fusion = bf16[64,6144]{1,0:T(8,128)(2,1)S(1)} fusion(bf16[512,6144]{1,0:T(8,128)(2,1)S(1)} %bitcast.101, f32[4,64]{1,0:T(4,128)S(1)} %exponential_reduce_fusion, f32[2,4,64,128]{3,2,1,0:T(8,128)S(1)} %convolution_bitcast_fusion.1, pred[4]{0:T(512)(128)(4,1)S(1)} %subtract_compare_fusion), kind=kOutput, calls=%fused_computation | convolution fusion | flops 403144704 | bytes 7341060 | tf_op jit(solution)/shard_map/dot_general | solution.py:85
  52.1 0.5 reshape.145
  52.6 0.4 copy.29
  53.1 47.6 %all_to_all.5 = bf16[12,64,512]{2,1,0:T(8,128)(2,1)S(1)} all-to-all(bf16[12,64,512]{2,1,0:T(8,128)(2,1)S(1)} %copy.29), channel_id=1, replica_groups=mesh['span'=8,'seq'=8,'mp'=12] {'mp'}, dimensions={0} | all-to-all | bytes 1572864 | tf_op jit(solution)/shard_map/all_to_all | solution.py:89
  100.7 0.7 reduce_sum.22
  (10 shorter events, 0.2 us)
Async XLA Ops:
  0.0 41.4 %copy-start = (bf16[1,64,512]{2,1,0:T(8,128)(2,1)S(1)}, bf16[1,64,512]{2,1,0:T(8,128)(2,1)}, u32[]{:S(2)}) copy-start(bf16[1,64,512]{2,1,0:T(8,128)(2,1)} %param.8) | copy-start | bytes 196612
  0.8 7.8 %collective-permute-start.1 = (bf16[64,512]{1,0:T(8,128)(2,1)S(1)}, bf16[64,512]{1,0:T(8,128)(2,1)S(1)}, u32[]{:S(2)}, u32[]{:S(2)}) collective-permute-start(bf16[64,512]{1,0:T(8,128)(2,1)S(1)} %pad_maximum_fusion.1), channel_id=1, source_target_pairs={{0,192},{96,288},{192,384},{288,480},{384,576},{480,672},{1,193},{... | collective-permute-start | bytes 196616 | tf_op jit(solution)/shard_map/ppermute | solution.py:16
  2.1 7.7 %collective-permute-start = (bf16[64,512]{1,0:T(8,128)(2,1)S(1)}, bf16[64,512]{1,0:T(8,128)(2,1)S(1)}, u32[]{:S(2)}, u32[]{:S(2)}) collective-permute-start(bf16[64,512]{1,0:T(8,128)(2,1)S(1)} %pad_maximum_fusion.1), channel_id=1, source_target_pairs={{0,96},{96,192},{192,288},{288,384},{384,480},{480,576},{576,672},... | collective-permute-start | bytes 196616 | tf_op jit(solution)/shard_map/ppermute | solution.py:16
  9.8 17.9 %collective-permute-start.4 = (bf16[208,512]{1,0:T(8,128)(2,1)S(1)}, bf16[208,512]{1,0:T(8,128)(2,1)S(1)}, u32[]{:S(2)}, u32[]{:S(2)}) collective-permute-start(bf16[208,512]{1,0:T(8,128)(2,1)S(1)} %get-tuple-element.18), channel_id=1, source_target_pairs={{0,72},{12,84},{24,0},{36,12},{48,24},{60,36},{72,48},{84,60},{1,7... | collective-permute-start | bytes 638984 | tf_op jit(solution)/shard_map/ppermute | solution.py:50
  13.9 16.1 %collective-permute-start.3 = (bf16[208,512]{1,0:T(8,128)(2,1)S(1)}, bf16[208,512]{1,0:T(8,128)(2,1)S(1)}, u32[]{:S(2)}, u32[]{:S(2)}) collective-permute-start(bf16[208,512]{1,0:T(8,128)(2,1)S(1)} %get-tuple-element.18), channel_id=1, source_target_pairs={{0,48},{12,60},{24,72},{36,84},{48,0},{60,12},{72,24},{84,36},{1,4... | collective-permute-start | bytes 638984 | tf_op jit(solution)/shard_map/ppermute | solution.py:50
  16.8 22.4 %collective-permute-start.2 = (bf16[208,512]{1,0:T(8,128)(2,1)S(1)}, bf16[208,512]{1,0:T(8,128)(2,1)S(1)}, u32[]{:S(2)}, u32[]{:S(2)}) collective-permute-start(bf16[208,512]{1,0:T(8,128)(2,1)S(1)} %get-tuple-element.18), channel_id=1, source_target_pairs={{0,24},{12,36},{24,48},{36,60},{48,72},{60,84},{72,0},{84,12},{1,2... | collective-permute-start | bytes 638984 | tf_op jit(solution)/shard_map/ppermute | solution.py:50
  39.3 4.4 %collective-permute-start.5 = (bf16[4,208,512]{2,1,0:T(8,128)(2,1)S(1)}, bf16[4,208,512]{2,1,0:T(8,128)(2,1)}, u32[]{:S(2)}, u32[]{:S(2)}) collective-permute-start(bf16[4,208,512]{2,1,0:T(8,128)(2,1)S(1)} %pad_maximum_fusion), channel_id=1, source_target_pairs={{0,12},{12,0},{24,36},{36,24},{48,60},{60,48},{72,84},{84,72},{1,1... | collective-permute-start | bytes 2555912 | tf_op jit(solution)/shard_map/ppermute | solution.py:52
  47.8 2.2 %slice-start = ((s8[6291456]{0:T(1024)(128)(4,1)}), s8[4194304]{0:T(1024)(128)(4,1)S(1)}, s32[]{:S(2)}) async-start(s8[6291456]{0:T(1024)(128)(4,1)} %bitcast.100), calls=%async_computation.1 | async-start | bytes 8388608
  48.3 2.5 %slice-start.1 = ((s8[6291456]{0:T(1024)(128)(4,1)}), s8[2097152]{0:T(1024)(128)(4,1)S(1)}, s32[]{:S(2)}) async-start(s8[6291456]{0:T(1024)(128)(4,1)} %bitcast.100), calls=%async_computation.2 | async-start | bytes 4194304

commit v4 on v3

--- a/solution.py
+++ b/solution.py
@@ -83,12 +83,28 @@
     mp_count = lax.axis_size("mp")
     out_width = out_weight.shape[1] // mp_count
     partial_sum = jnp.dot(attended, out_weight, preferred_element_type=jnp.float32)
-    partial_sum = jnp.transpose(
-        partial_sum.astype(jnp.bfloat16).reshape(row_count, mp_count, out_width), (1, 0, 2)
-    )
-    received = lax.all_to_all(partial_sum, "mp", 0, 0, tiled=True)
-    projected = jnp.sum(received.astype(jnp.float32), axis=0)
-    return projected.astype(jnp.bfloat16)[None]
+    partial_sum = partial_sum.reshape(row_count, mp_count, out_width)
+    trio = 3
+    trios = mp_count // trio
+    place = lax.axis_index("mp") % trio
+    by_trio = jnp.transpose(
+        partial_sum.reshape(row_count, trios, trio, out_width), (2, 1, 0, 3)
+    ).astype(jnp.bfloat16)
+    summed = lax.dynamic_index_in_dim(by_trio, place, 0, keepdims=False).astype(jnp.float32)
+    for step in range(1, trio):
+        pairs = [(i, trio * (i // trio) + (i % trio + step) % trio) for i in range(mp_count)]
+        target = (place + step) % trio
+        sent = lax.dynamic_index_in_dim(by_trio, target, 0, keepdims=False)
+        summed = summed + lax.ppermute(sent, "mp", pairs).astype(jnp.float32)
+    partial_trio = summed.astype(jnp.bfloat16)
+    group = lax.axis_index("mp") // trio
+    total_sum = lax.dynamic_index_in_dim(partial_trio, group, 0, keepdims=False).astype(jnp.float32)
+    for step in range(1, trios):
+        pairs = [(i, (i + trio * step) % mp_count) for i in range(mp_count)]
+        target = (group + step) % trios
+        sent = lax.dynamic_index_in_dim(partial_trio, target, 0, keepdims=False)
+        total_sum = total_sum + lax.ppermute(sent, "mp", pairs).astype(jnp.float32)
+    return total_sum.astype(jnp.bfloat16)[None]
 
 
 def solution(mesh):

time: 102 us -> 117 us (1.15)
  the two profiles are of different devices: /device:TPU:60 before, /device:TPU:64 now
where the time goes in v4:
time: 117 us; the launch traced here: 116 us
  starting transfers between devices  54.9 us (47%)
  waiting for transfers between devices  30.2 us (26%)
  local copies, waits for them, and re-layouts  19.9 us (17%)
  matrix products  5.98 us (5%)
  other arithmetic  2.91 us (2%)
  between operations  2.3 us (2%)
    ppermute x3, starting transfers between devices, on_device(): total_sum = total_sum + lax.ppermute(sent, 'mp', pairs).astype(jnp.float32)  23 us
    ppermute x3, starting transfers between devices, on_device(): held.append(lax.ppermute(outgoing, 'seq', pairs))  15.7 us
    unnamed x13, local copies, waits for them, and re-layouts  12.2 us
    ppermute x3, waiting for transfers between devices, on_device(): held.append(lax.ppermute(outgoing, 'seq', pairs))  11.2 us
    ppermute x2, waiting for transfers between devices, on_device(): summed = summed + lax.ppermute(sent, 'mp', pairs).astype(jnp.float32)  10.6 us
    ppermute x2, starting transfers between devices, passed_along(): return lax.ppermute(x, axis, pairs)  8.04 us
    ppermute x3, waiting for transfers between devices, on_device(): total_sum = total_sum + lax.ppermute(sent, 'mp', pairs).astype(jnp.float32)  7.12 us
    ppermute x2, starting transfers between devices, on_device(): summed = summed + lax.ppermute(sent, 'mp', pairs).astype(jnp.float32)  6.2 us
  transfers between devices with their start and end apart: 11, of which 7 were waited for; matrix products, arithmetic and copies ran while one was open for 12% of the time, Pallas kernels for 0%

profile of v4, /device:TPU:64, one launch (start us, length us, event | category | flops | bytes accessed | tf_op | source)
XLA Modules:
  0.0 116.2 jit_solution(11836501788173171766)
XLA Ops:
  0.0 0.0 copy-start.3
  0.0 0.8 dynamic-slice_bitcast_fusion.5
  0.8 3.4 %collective-permute-start = (bf16[64,512]{1,0:T(8,128)(2,1)S(1)}, bf16[64,512]{1,0:T(8,128)(2,1)S(1)}, u32[]{:S(2)}, u32[]{:S(2)}) collective-permute-start(bf16[64,512]{1,0:T(8,128)(2,1)S(1)} %pad_maximum_fusion.1), channel_id=1, source_target_pairs={{0,96},{96,192},{192,288},{288,384},{384,480},{480,576},{576,672},... | collective-permute-start | bytes 196616 | tf_op jit(solution)/shard_map/ppermute | solution.py:16
  4.2 4.6 %collective-permute-start.1 = (bf16[64,512]{1,0:T(8,128)(2,1)S(1)}, bf16[64,512]{1,0:T(8,128)(2,1)S(1)}, u32[]{:S(2)}, u32[]{:S(2)}) collective-permute-start(bf16[64,512]{1,0:T(8,128)(2,1)S(1)} %pad_maximum_fusion.1), channel_id=1, source_target_pairs={{0,192},{96,288},{192,384},{288,480},{384,576},{480,672},{1,193},{... | collective-permute-start | bytes 196616 | tf_op jit(solution)/shard_map/ppermute | solution.py:16
  8.9 0.7 fusion.30
  9.5 0.0 collective-permute-done
  9.5 1.2 %collective-permute-done.1 = bf16[64,512]{1,0:T(8,128)(2,1)S(1)} collective-permute-done((bf16[64,512]{1,0:T(8,128)(2,1)S(1)}, bf16[64,512]{1,0:T(8,128)(2,1)S(1)}, u32[]{:S(2)}, u32[]{:S(2)}) %collective-permute-start.1) | collective-permute-done | bytes 65568 | tf_op jit(solution)/shard_map/ppermute | solution.py:16
  10.8 4.5 %collective-permute-start.2 = (bf16[208,512]{1,0:T(8,128)(2,1)S(1)}, bf16[208,512]{1,0:T(8,128)(2,1)S(1)}, u32[]{:S(2)}, u32[]{:S(2)}) collective-permute-start(bf16[208,512]{1,0:T(8,128)(2,1)S(1)} %get-tuple-element.18), channel_id=1, source_target_pairs={{0,24},{12,36},{24,48},{36,60},{48,72},{60,84},{72,0},{84,12},{1,2... | collective-permute-start | bytes 638984 | tf_op jit(solution)/shard_map/ppermute | solution.py:50
  15.3 5.9 %collective-permute-start.3 = (bf16[208,512]{1,0:T(8,128)(2,1)S(1)}, bf16[208,512]{1,0:T(8,128)(2,1)S(1)}, u32[]{:S(2)}, u32[]{:S(2)}) collective-permute-start(bf16[208,512]{1,0:T(8,128)(2,1)S(1)} %get-tuple-element.18), channel_id=1, source_target_pairs={{0,48},{12,60},{24,72},{36,84},{48,0},{60,12},{72,24},{84,36},{1,4... | collective-permute-start | bytes 638984 | tf_op jit(solution)/shard_map/ppermute | solution.py:50
  21.2 5.3 %collective-permute-start.4 = (bf16[208,512]{1,0:T(8,128)(2,1)S(1)}, bf16[208,512]{1,0:T(8,128)(2,1)S(1)}, u32[]{:S(2)}, u32[]{:S(2)}) collective-permute-start(bf16[208,512]{1,0:T(8,128)(2,1)S(1)} %get-tuple-element.18), channel_id=1, source_target_pairs={{0,72},{12,84},{24,0},{36,12},{48,24},{60,36},{72,48},{84,60},{1,7... | collective-permute-start | bytes 638984 | tf_op jit(solution)/shard_map/ppermute | solution.py:50
  26.5 1.5 %fusion.29 = (s32[1,1]{1,0:T(1,128)}, s32[1,1]{1,0:T(1,128)}, s32[1,1]{1,0:T(1,128)}) fusion(s32[8,8]{1,0:T(8,128)} %param.12, s32[]{:T(128)S(6)} %select_n.112, s32[]{:T(128)S(6)} %max.16, s32[]{:T(128)S(6)} %max.20, s32[]{:T(128)S(6)} %max.18), kind=kLoop, calls=%fused_computation.62 | loop fusion | bytes 40 | tf_op jit(solution)/shard_map/jit(dynamic_index_in_dim)/dynamic_slice | solution.py:38
  29.9 0.0 collective-permute-done.2
  29.9 0.0 copy-start
  29.9 3.8 %collective-permute-done.3 = bf16[208,512]{1,0:T(8,128)(2,1)S(1)} collective-permute-done((bf16[208,512]{1,0:T(8,128)(2,1)S(1)}, bf16[208,512]{1,0:T(8,128)(2,1)S(1)}, u32[]{:S(2)}, u32[]{:S(2)}) %collective-permute-start.3) | collective-permute-done | bytes 213024 | tf_op jit(solution)/shard_map/ppermute | solution.py:50
  33.7 0.0 copy-start.1
  33.7 7.5 %collective-permute-done.4 = bf16[208,512]{1,0:T(8,128)(2,1)S(1)} collective-permute-done((bf16[208,512]{1,0:T(8,128)(2,1)S(1)}, bf16[208,512]{1,0:T(8,128)(2,1)S(1)}, u32[]{:S(2)}, u32[]{:S(2)}) %collective-permute-start.4) | collective-permute-done | bytes 213024 | tf_op jit(solution)/shard_map/ppermute | solution.py:50
  41.1 0.0 copy-start.2
  41.1 0.0 copy-done
  41.1 0.0 copy-done.1
  41.1 0.7 copy-done.2
  41.8 0.1 pad_maximum_fusion
  41.9 1.9 %collective-permute-start.5 = (bf16[4,208,512]{2,1,0:T(8,128)(2,1)S(1)}, bf16[4,208,512]{2,1,0:T(8,128)(2,1)S(1)}, u32[]{:S(2)}, u32[]{:S(2)}) collective-permute-start(bf16[4,208,512]{2,1,0:T(8,128)(2,1)S(1)} %pad_maximum_fusion), channel_id=1, source_target_pairs={{0,12},{12,0},{24,36},{36,24},{48,60},{60,48},{72,84},{84,72},{1,1... | collective-permute-start | bytes 2555912 | tf_op jit(solution)/shard_map/ppermute | solution.py:52
  43.9 0.1 add_compare_fusion
  44.0 0.0 copy-done.3
  44.0 0.1 and.66
  44.1 8.7 %copy.30 = bf16[512,6144]{0,1:T(8,128)(2,1)} copy(bf16[512,6144]{1,0:T(8,128)(2,1)} %param.13) | data formatting | bytes 12582912 | tf_op args[5]
  52.8 0.9 constant_dynamic-update-slice_fusion.3
  53.7 0.9 constant_dynamic-update-slice_fusion.2
  54.7 0.9 constant_dynamic-update-slice_fusion.1
  55.6 0.0 collective-permute-done.5
  55.6 0.1 constant_dynamic-update-slice_fusion
  55.7 0.1 slice.48
  55.8 1.2 %copy.50 = bf16[8,3,64,512]{3,2,0,1:T(8,128)(2,1)} copy(bf16[8,3,64,512]{3,2,1,0:T(8,128)(2,1)S(1)} %bitcast.124) | data formatting | bytes 3145728 | tf_op jit(solution)/shard_map/reshape | solution.py:54
  57.1 2.4 %reshape.146 = bf16[1536,2,2,128]{3,2,1,0:T(2,128)(2,1)S(1)} reshape(bf16[3,8,64,512]{3,2,1,0:T(8,128)(2,1)} %bitcast.125) | data formatting | bytes 3145728 | tf_op jit(solution)/shard_map/reshape | solution.py:58
  59.4 1.1 fusion.28
  60.6 0.1 eq.45
  60.7 0.1 broadcast_compare_fusion
  60.8 0.1 and.69
  60.9 0.1 copy.40
  61.0 0.6 convolution_bitcast_fusion
  61.5 0.1 broadcast_and_fusion
  61.6 0.4 fusion.26
  62.0 0.5 exponential_reduce_fusion
  62.6 0.6 convolution_bitcast_fusion.1
  63.2 0.1 fusion.23
  63.3 0.1 copy.29
  63.4 4.8 %convolution_convert_fusion = bf16[64,4,3,512]{3,0,2,1:T(8,128)(2,1)S(1)} fusion(bf16[4,3,512,512]{3,2,1,0:T(8,128)(2,1)} %bitcast.123, bf16[64,512,1,1]{1,0,2,3:T(8,128)(2,1)S(1)} %reshape.153), kind=kOutput, calls=%fused_computation.7 | convolution fusion | flops 403046400 | bytes 7143424 | tf_op jit(solution)/shard_map/dot_general | solution.py:85
  68.3 4.3 %collective-permute-start.6 = (bf16[4,64,512]{2,1,0:T(8,128)(2,1)S(1)}, bf16[4,64,512]{2,1,0:T(8,128)(2,1)S(1)}, u32[]{:S(2)}, u32[]{:S(2)}) collective-permute-start(bf16[4,64,512]{2,1,0:T(8,128)(2,1)S(1)} %get-tuple-element.21), channel_id=1, source_target_pairs={{0,1},{1,2},{2,0},{3,4},{4,5},{5,3},{6,7},{7,8},{8,6},{9,10},{10,1... | collective-permute-start | bytes 786440 | tf_op jit(solution)/shard_map/ppermute | solution.py:98
  72.5 1.9 %collective-permute-start.7 = (bf16[4,64,512]{2,1,0:T(8,128)(2,1)S(1)}, bf16[4,64,512]{2,1,0:T(8,128)(2,1)S(1)}, u32[]{:S(2)}, u32[]{:S(2)}) collective-permute-start(bf16[4,64,512]{2,1,0:T(8,128)(2,1)S(1)} %get-tuple-element.22), channel_id=1, source_target_pairs={{0,2},{1,0},{2,1},{3,5},{4,3},{5,4},{6,8},{7,6},{8,7},{9,11},{10,9... | collective-permute-start | bytes 786440 | tf_op jit(solution)/shard_map/ppermute | solution.py:98
  74.6 9.8 %collective-permute-done.6 = bf16[4,64,512]{2,1,0:T(8,128)(2,1)S(1)} collective-permute-done((bf16[4,64,512]{2,1,0:T(8,128)(2,1)S(1)}, bf16[4,64,512]{2,1,0:T(8,128)(2,1)S(1)}, u32[]{:S(2)}, u32[]{:S(2)}) %collective-permute-start.6) | collective-permute-done | bytes 262176 | tf_op jit(solution)/shard_map/ppermute | solution.py:98
  84.4 0.8 collective-permute-done.7
  85.1 0.1 fusion.10
  85.3 13.0 %collective-permute-start.10 = (bf16[64,512]{1,0:T(8,128)(2,1)S(1)}, bf16[64,512]{1,0:T(8,128)(2,1)S(1)}, u32[]{:S(2)}, u32[]{:S(2)}) collective-permute-start(bf16[64,512]{1,0:T(8,128)(2,1)S(1)} %get-tuple-element.24), channel_id=1, source_target_pairs={{0,9},{1,10},{2,11},{3,0},{4,1},{5,2},{6,3},{7,4},{8,5},{9,6},{10,... | collective-permute-start | bytes 196616 | tf_op jit(solution)/shard_map/ppermute | solution.py:106
  98.3 1.9 %collective-permute-start.8 = (bf16[64,512]{1,0:T(8,128)(2,1)S(1)}, bf16[64,512]{1,0:T(8,128)(2,1)S(1)}, u32[]{:S(2)}, u32[]{:S(2)}) collective-permute-start(bf16[64,512]{1,0:T(8,128)(2,1)S(1)} %get-tuple-element.23), channel_id=1, source_target_pairs={{0,3},{1,4},{2,5},{3,6},{4,7},{5,8},{6,9},{7,10},{8,11},{9,0},{10,... | collective-permute-start | bytes 196616 | tf_op jit(solution)/shard_map/ppermute | solution.py:106
  100.2 8.1 %collective-permute-start.9 = (bf16[64,512]{1,0:T(8,128)(2,1)S(1)}, bf16[64,512]{1,0:T(8,128)(2,1)S(1)}, u32[]{:S(2)}, u32[]{:S(2)}) collective-permute-start(bf16[64,512]{1,0:T(8,128)(2,1)S(1)} %get-tuple-element.25), channel_id=1, source_target_pairs={{0,6},{1,7},{2,8},{3,9},{4,10},{5,11},{6,0},{7,1},{8,2},{9,3},{10,... | collective-permute-start | bytes 196616 | tf_op jit(solution)/shard_map/ppermute | solution.py:106
  108.4 0.0 collective-permute-done.10
  108.4 1.4 %collective-permute-done.8 = bf16[64,512]{1,0:T(8,128)(2,1)S(1)} collective-permute-done((bf16[64,512]{1,0:T(8,128)(2,1)S(1)}, bf16[64,512]{1,0:T(8,128)(2,1)S(1)}, u32[]{:S(2)}, u32[]{:S(2)}) %collective-permute-start.8) | collective-permute-done | bytes 65568 | tf_op jit(solution)/shard_map/ppermute | solution.py:106
  109.7 5.8 %collective-permute-done.9 = bf16[64,512]{1,0:T(8,128)(2,1)S(1)} collective-permute-done((bf16[64,512]{1,0:T(8,128)(2,1)S(1)}, bf16[64,512]{1,0:T(8,128)(2,1)S(1)}, u32[]{:S(2)}, u32[]{:S(2)}) %collective-permute-start.9) | collective-permute-done | bytes 65568 | tf_op jit(solution)/shard_map/ppermute | solution.py:106
  115.5 0.7 fusion.19
  (9 shorter events, 0.2 us)
Async XLA Ops:
  0.0 44.0 %copy-start.3 = (bf16[1,64,512]{2,1,0:T(8,128)(2,1)S(1)}, bf16[1,64,512]{2,1,0:T(8,128)(2,1)}, u32[]{:S(2)}) copy-start(bf16[1,64,512]{2,1,0:T(8,128)(2,1)} %param.8) | copy-start | bytes 196612
  0.8 8.7 %collective-permute-start = (bf16[64,512]{1,0:T(8,128)(2,1)S(1)}, bf16[64,512]{1,0:T(8,128)(2,1)S(1)}, u32[]{:S(2)}, u32[]{:S(2)}) collective-permute-start(bf16[64,512]{1,0:T(8,128)(2,1)S(1)} %pad_maximum_fusion.1), channel_id=1, source_target_pairs={{0,96},{96,192},{192,288},{288,384},{384,480},{480,576},{576,672},... | collective-permute-start | bytes 196616 | tf_op jit(solution)/shard_map/ppermute | solution.py:16
  4.2 6.5 %collective-permute-start.1 = (bf16[64,512]{1,0:T(8,128)(2,1)S(1)}, bf16[64,512]{1,0:T(8,128)(2,1)S(1)}, u32[]{:S(2)}, u32[]{:S(2)}) collective-permute-start(bf16[64,512]{1,0:T(8,128)(2,1)S(1)} %pad_maximum_fusion.1), channel_id=1, source_target_pairs={{0,192},{96,288},{192,384},{288,480},{384,576},{480,672},{1,193},{... | collective-permute-start | bytes 196616 | tf_op jit(solution)/shard_map/ppermute | solution.py:16
  10.8 19.1 %collective-permute-start.2 = (bf16[208,512]{1,0:T(8,128)(2,1)S(1)}, bf16[208,512]{1,0:T(8,128)(2,1)S(1)}, u32[]{:S(2)}, u32[]{:S(2)}) collective-permute-start(bf16[208,512]{1,0:T(8,128)(2,1)S(1)} %get-tuple-element.18), channel_id=1, source_target_pairs={{0,24},{12,36},{24,48},{36,60},{48,72},{60,84},{72,0},{84,12},{1,2... | collective-permute-start | bytes 638984 | tf_op jit(solution)/shard_map/ppermute | solution.py:50
  15.3 18.4 %collective-permute-start.3 = (bf16[208,512]{1,0:T(8,128)(2,1)S(1)}, bf16[208,512]{1,0:T(8,128)(2,1)S(1)}, u32[]{:S(2)}, u32[]{:S(2)}) collective-permute-start(bf16[208,512]{1,0:T(8,128)(2,1)S(1)} %get-tuple-element.18), channel_id=1, source_target_pairs={{0,48},{12,60},{24,72},{36,84},{48,0},{60,12},{72,24},{84,36},{1,4... | collective-permute-start | bytes 638984 | tf_op jit(solution)/shard_map/ppermute | solution.py:50
  21.2 19.9 %collective-permute-start.4 = (bf16[208,512]{1,0:T(8,128)(2,1)S(1)}, bf16[208,512]{1,0:T(8,128)(2,1)S(1)}, u32[]{:S(2)}, u32[]{:S(2)}) collective-permute-start(bf16[208,512]{1,0:T(8,128)(2,1)S(1)} %get-tuple-element.18), channel_id=1, source_target_pairs={{0,72},{12,84},{24,0},{36,12},{48,24},{60,36},{72,48},{84,60},{1,7... | collective-permute-start | bytes 638984 | tf_op jit(solution)/shard_map/ppermute | solution.py:50
  29.9 11.3 %copy-start = (bf16[208,512]{1,0:T(8,128)(2,1)}, bf16[208,512]{1,0:T(8,128)(2,1)S(1)}, u32[]{:S(2)}) copy-start(bf16[208,512]{1,0:T(8,128)(2,1)S(1)} %collective-permute-done.2) | copy-start | bytes 638980
  33.7 7.5 %copy-start.1 = (bf16[208,512]{1,0:T(8,128)(2,1)}, bf16[208,512]{1,0:T(8,128)(2,1)S(1)}, u32[]{:S(2)}) copy-start(bf16[208,512]{1,0:T(8,128)(2,1)S(1)} %collective-permute-done.3) | copy-start | bytes 638980
  41.1 0.7 copy-start.2
  41.9 13.7 %collective-permute-start.5 = (bf16[4,208,512]{2,1,0:T(8,128)(2,1)S(1)}, bf16[4,208,512]{2,1,0:T(8,128)(2,1)S(1)}, u32[]{:S(2)}, u32[]{:S(2)}) collective-permute-start(bf16[4,208,512]{2,1,0:T(8,128)(2,1)S(1)} %pad_maximum_fusion), channel_id=1, source_target_pairs={{0,12},{12,0},{24,36},{36,24},{48,60},{60,48},{72,84},{84,72},{1,1... | collective-permute-start | bytes 2555912 | tf_op jit(solution)/shard_map/ppermute | solution.py:52
  68.3 16.1 %collective-permute-start.6 = (bf16[4,64,512]{2,1,0:T(8,128)(2,1)S(1)}, bf16[4,64,512]{2,1,0:T(8,128)(2,1)S(1)}, u32[]{:S(2)}, u32[]{:S(2)}) collective-permute-start(bf16[4,64,512]{2,1,0:T(8,128)(2,1)S(1)} %get-tuple-element.21), channel_id=1, source_target_pairs={{0,1},{1,2},{2,0},{3,4},{4,5},{5,3},{6,7},{7,8},{8,6},{9,10},{10,1... | collective-permute-start | bytes 786440 | tf_op jit(solution)/shard_map/ppermute | solution.py:98
  72.5 12.6 %collective-permute-start.7 = (bf16[4,64,512]{2,1,0:T(8,128)(2,1)S(1)}, bf16[4,64,512]{2,1,0:T(8,128)(2,1)S(1)}, u32[]{:S(2)}, u32[]{:S(2)}) collective-permute-start(bf16[4,64,512]{2,1,0:T(8,128)(2,1)S(1)} %get-tuple-element.22), channel_id=1, source_target_pairs={{0,2},{1,0},{2,1},{3,5},{4,3},{5,4},{6,8},{7,6},{8,7},{9,11},{10,9... | collective-permute-start | bytes 786440 | tf_op jit(solution)/shard_map/ppermute | solution.py:98
  85.3 23.1 %collective-permute-start.10 = (bf16[64,512]{1,0:T(8,128)(2,1)S(1)}, bf16[64,512]{1,0:T(8,128)(2,1)S(1)}, u32[]{:S(2)}, u32[]{:S(2)}) collective-permute-start(bf16[64,512]{1,0:T(8,128)(2,1)S(1)} %get-tuple-element.24), channel_id=1, source_target_pairs={{0,9},{1,10},{2,11},{3,0},{4,1},{5,2},{6,3},{7,4},{8,5},{9,6},{10,... | collective-permute-start | bytes 196616 | tf_op jit(solution)/shard_map/ppermute | solution.py:106
  98.3 11.4 %collective-permute-start.8 = (bf16[64,512]{1,0:T(8,128)(2,1)S(1)}, bf16[64,512]{1,0:T(8,128)(2,1)S(1)}, u32[]{:S(2)}, u32[]{:S(2)}) collective-permute-start(bf16[64,512]{1,0:T(8,128)(2,1)S(1)} %get-tuple-element.23), channel_id=1, source_target_pairs={{0,3},{1,4},{2,5},{3,6},{4,7},{5,8},{6,9},{7,10},{8,11},{9,0},{10,... | collective-permute-start | bytes 196616 | tf_op jit(solution)/shard_map/ppermute | solution.py:106
  100.2 15.3 %collective-permute-start.9 = (bf16[64,512]{1,0:T(8,128)(2,1)S(1)}, bf16[64,512]{1,0:T(8,128)(2,1)S(1)}, u32[]{:S(2)}, u32[]{:S(2)}) collective-permute-start(bf16[64,512]{1,0:T(8,128)(2,1)S(1)} %get-tuple-element.25), channel_id=1, source_target_pairs={{0,6},{1,7},{2,8},{3,9},{4,10},{5,11},{6,0},{7,1},{8,2},{9,3},{10,... | collective-permute-start | bytes 196616 | tf_op jit(solution)/shard_map/ppermute | solution.py:106

commit v5 on v3

--- a/solution.py
+++ b/solution.py
@@ -6,7 +6,7 @@
 HEAD_DIM = 128
 WINDOW = 3
 GROUP = 6
-KV_SLOTS = 2
+LENT_HEADS = 2
 CLIP_PAD = 16
 
 
@@ -14,6 +14,18 @@
     size = lax.axis_size(axis)
     pairs = [(i, i + by) for i in range(size) if 0 <= i + by < size]
     return lax.ppermute(x, axis, pairs)
+
+
+def lending_pairs(mp_count, head_count, lent):
+    pairs = []
+    for i in range(mp_count):
+        groups = [(i * head_count + h) // GROUP for h in range(head_count)]
+        if len(set(groups)) == 1:
+            continue
+        assert len(set(groups[:lent])) == 1 and len(set(groups[lent:])) == 1
+        assert i + 1 < mp_count and groups[lent] == ((i + 1) * head_count) // GROUP
+        pairs.append((i, i + 1))
+    return pairs
 
 
 def on_device(queries, keys, values, clip_ids, block_mask, out_weight):
@@ -24,13 +36,18 @@
     score_scale = HEAD_DIM ** (-0.5)
     span_index = lax.axis_index("span")
     first_head = lax.axis_index("mp") * head_count
-    first_kv = jnp.minimum(first_head // GROUP, kv_count - KV_SLOTS)
-    kv_slot = (first_head + jnp.arange(head_count, dtype=jnp.int32)) // GROUP - first_kv
-    kv_start = first_kv * HEAD_DIM
-    slot_width = KV_SLOTS * HEAD_DIM
-    own_keys = lax.dynamic_slice_in_dim(keys[0], kv_start, slot_width, 1)
-    own_values = lax.dynamic_slice_in_dim(values[0], kv_start, slot_width, 1)
+    mp_index = lax.axis_index("mp")
+    mp_count = lax.axis_size("mp")
+    kv_start = (first_head // GROUP) * HEAD_DIM
+    own_keys = lax.dynamic_slice_in_dim(keys[0], kv_start, HEAD_DIM, 1)
+    own_values = lax.dynamic_slice_in_dim(values[0], kv_start, HEAD_DIM, 1)
     packed = jnp.concatenate([own_keys, own_values], axis=1)
+    lent = head_count - LENT_HEADS
+    lends = lending_pairs(mp_count, head_count, lent)
+    borrowed = lax.ppermute(queries[0][:, lent * HEAD_DIM :], "mp", lends)
+    lender = jnp.zeros((), jnp.bool_)
+    for i, _ in lends:
+        lender = lender | (mp_index == i)
     mask_row = lax.dynamic_index_in_dim(block_mask, span_index, 0, keepdims=False)
     visible = []
     for j in range(WINDOW):
@@ -55,15 +72,13 @@
     key_clips = gathered[:, WINDOW * row_count, :row_count].reshape(-1)
     piece_rows = seq_count * row_count
     window_rows = WINDOW * piece_rows
-    kv = jnp.transpose(kv_rows, (1, 0, 2, 3)).reshape(window_rows, 2, KV_SLOTS, HEAD_DIM)
+    kv = jnp.transpose(kv_rows, (1, 0, 2, 3)).reshape(window_rows, 2, HEAD_DIM)
     key_all = kv[:, 0]
     value_all = kv[:, 1]
-    query_heads = queries[0].reshape(row_count, head_count, HEAD_DIM)
-    s_both = jnp.einsum(
-        "qhd,kad->ahqk", query_heads, key_all, preferred_element_type=jnp.float32
-    )
-    pick = kv_slot[:, None, None] == 0
-    s = jnp.where(pick, s_both[0], s_both[1]) * score_scale
+    all_queries = jnp.concatenate([queries[0], borrowed], axis=1)
+    query_heads = all_queries.reshape(row_count, head_count + LENT_HEADS, HEAD_DIM)
+    s = jnp.einsum("qhd,kd->hqk", query_heads, key_all, preferred_element_type=jnp.float32)
+    s = s * score_scale
     span_ok = jnp.stack(visible) == 1
     query_clips = clip_ids.astype(jnp.bfloat16)
     allowed = span_ok[None, :, None] & (query_clips[:, None, None] == key_clips[None, None, :])
@@ -72,15 +87,14 @@
     top = jnp.max(s, axis=2, keepdims=True)
     p = jnp.exp(s - top)
     total = jnp.sum(p, axis=2, keepdims=True)
-    acc_both = jnp.einsum(
-        "hqk,kad->ahqd", p.astype(jnp.bfloat16), value_all, preferred_element_type=jnp.float32
+    acc = jnp.einsum(
+        "hqk,kd->hqd", p.astype(jnp.bfloat16), value_all, preferred_element_type=jnp.float32
     )
-    acc = jnp.where(pick, acc_both[0], acc_both[1])
-    attended = acc / total
-    attended = (
-        jnp.transpose(attended, (1, 0, 2)).reshape(row_count, local_width).astype(jnp.bfloat16)
-    )
-    mp_count = lax.axis_size("mp")
+    attended = (acc / total).astype(jnp.bfloat16)
+    returned = lax.ppermute(attended[head_count:], "mp", [(j, i) for i, j in lends])
+    mine = attended[:head_count]
+    mine = jnp.concatenate([mine[:lent], jnp.where(lender, returned, mine[lent:])], axis=0)
+    attended = jnp.transpose(mine, (1, 0, 2)).reshape(row_count, local_width)
     out_width = out_weight.shape[1] // mp_count
     partial_sum = jnp.dot(attended, out_weight, preferred_element_type=jnp.float32)
     partial_sum = jnp.transpose(

time: 102 us -> 104 us (1.020)
  the two profiles are of different devices: /device:TPU:60 before, /device:TPU:6 now
where the time goes in v5:
time: 104 us
  blocking collectives  55.4 us (53%)
  starting transfers between devices  25.1 us (24%)
  waiting for transfers between devices  7.98 us (8%)
  local copies, waits for them, and re-layouts  5.82 us (6%)
  matrix products  5.17 us (5%)
  between operations  2.25 us (2%)
  other arithmetic  2.17 us (2%)
    all_to_all x1, blocking collectives, on_device(): received = lax.all_to_all(partial_sum, 'mp', 0, 0, tiled=True)  55.4 us
    ppermute x3, starting transfers between devices, on_device(): held.append(lax.ppermute(outgoing, 'seq', pairs))  13.6 us
    ppermute x2, starting transfers between devices, passed_along(): return lax.ppermute(x, axis, pairs)  8.33 us
    ppermute x3, waiting for transfers between devices, on_device(): held.append(lax.ppermute(outgoing, 'seq', pairs))  6.29 us
    dot_general x1, matrix products, on_device(): jnp.dot(attended, out_weight, preferred_element_type=jnp.float32)  4.02 us
  transfers between devices with their start and end apart: 8, of which 2 were waited for; matrix products, arithmetic and copies ran while one was open for 5% of the time, Pallas kernels for 0%

profile of v5, /device:TPU:6, one launch (start us, length us, event | category | flops | bytes accessed | tf_op | source)
XLA Modules:
  0.0 104.0 jit_solution(2200482175416412871)
XLA Ops:
  0.0 0.7 dynamic-slice_bitcast_fusion
  0.7 4.3 %collective-permute-start.1 = (bf16[64,256]{1,0:T(8,128)(2,1)S(1)}, bf16[64,256]{1,0:T(8,128)(2,1)S(1)}, u32[]{:S(2)}, u32[]{:S(2)}) collective-permute-start(bf16[64,256]{1,0:T(8,128)(2,1)S(1)} %pad_maximum_fusion.1), channel_id=1, source_target_pairs={{0,192},{96,288},{192,384},{288,480},{384,576},{480,672},{1,193},{... | collective-permute-start | bytes 98312 | tf_op jit(solution)/shard_map/ppermute | solution.py:16
  5.1 4.0 %collective-permute-start = (bf16[64,256]{1,0:T(8,128)(2,1)S(1)}, bf16[64,256]{1,0:T(8,128)(2,1)S(1)}, u32[]{:S(2)}, u32[]{:S(2)}) collective-permute-start(bf16[64,256]{1,0:T(8,128)(2,1)S(1)} %pad_maximum_fusion.1), channel_id=1, source_target_pairs={{0,96},{96,192},{192,288},{288,384},{384,480},{480,576},{576,672},... | collective-permute-start | bytes 98312 | tf_op jit(solution)/shard_map/ppermute | solution.py:16
  9.1 0.8 slice.54
  9.9 0.7 collective-permute-start.6
  10.5 0.7 fusion.23
  11.2 1.5 %fusion.22 = (s32[1,1]{1,0:T(1,128)}, s32[1,1]{1,0:T(1,128)}, s32[1,1]{1,0:T(1,128)}) fusion(s32[8,8]{1,0:T(8,128)} %param.12, s32[]{:T(128)S(6)} %select_n.42, s32[]{:T(128)S(6)} %max.16, s32[]{:T(128)S(6)} %max.20, s32[]{:T(128)S(6)} %max.18), kind=kLoop, calls=%fused_computation.39 | loop fusion | bytes 40 | tf_op jit(solution)/shard_map/jit(dynamic_index_in_dim)/dynamic_slice | solution.py:55
  14.6 0.0 collective-permute-done.1
  14.6 0.0 collective-permute-done
  14.7 5.3 %collective-permute-start.4 = (bf16[208,256]{1,0:T(8,128)(2,1)S(1)}, bf16[208,256]{1,0:T(8,128)(2,1)S(1)}, u32[]{:S(2)}, u32[]{:S(2)}) collective-permute-start(bf16[208,256]{1,0:T(8,128)(2,1)S(1)} %get-tuple-element.18), channel_id=1, source_target_pairs={{0,72},{12,84},{24,0},{36,12},{48,24},{60,36},{72,48},{84,60},{1,7... | collective-permute-start | bytes 319496 | tf_op jit(solution)/shard_map/ppermute | solution.py:67
  19.9 4.7 %collective-permute-start.3 = (bf16[208,256]{1,0:T(8,128)(2,1)S(1)}, bf16[208,256]{1,0:T(8,128)(2,1)S(1)}, u32[]{:S(2)}, u32[]{:S(2)}) collective-permute-start(bf16[208,256]{1,0:T(8,128)(2,1)S(1)} %get-tuple-element.18), channel_id=1, source_target_pairs={{0,48},{12,60},{24,72},{36,84},{48,0},{60,12},{72,24},{84,36},{1,4... | collective-permute-start | bytes 319496 | tf_op jit(solution)/shard_map/ppermute | solution.py:67
  24.6 3.6 %collective-permute-start.2 = (bf16[208,256]{1,0:T(8,128)(2,1)S(1)}, bf16[208,256]{1,0:T(8,128)(2,1)S(1)}, u32[]{:S(2)}, u32[]{:S(2)}) collective-permute-start(bf16[208,256]{1,0:T(8,128)(2,1)S(1)} %get-tuple-element.18), channel_id=1, source_target_pairs={{0,24},{12,36},{24,48},{36,60},{48,72},{60,84},{72,0},{84,12},{1,2... | collective-permute-start | bytes 319496 | tf_op jit(solution)/shard_map/ppermute | solution.py:67
  28.3 0.1 add_compare_fusion
  28.3 0.1 and.31
  28.4 0.0 collective-permute-done.4
  28.4 6.3 %collective-permute-done.3 = bf16[208,256]{1,0:T(8,128)(2,1)S(1)} collective-permute-done((bf16[208,256]{1,0:T(8,128)(2,1)S(1)}, bf16[208,256]{1,0:T(8,128)(2,1)S(1)}, u32[]{:S(2)}, u32[]{:S(2)}) %collective-permute-start.3) | collective-permute-done | bytes 106528 | tf_op jit(solution)/shard_map/ppermute | solution.py:67
  34.7 0.0 collective-permute-done.2
  34.7 0.1 pad_maximum_fusion
  34.8 1.9 %collective-permute-start.5 = (bf16[4,208,256]{2,1,0:T(8,128)(2,1)S(1)}, bf16[4,208,256]{2,1,0:T(8,128)(2,1)S(1)}, u32[]{:S(2)}, u32[]{:S(2)}) collective-permute-start(bf16[4,208,256]{2,1,0:T(8,128)(2,1)S(1)} %pad_maximum_fusion), channel_id=1, source_target_pairs={{0,12},{12,0},{24,36},{36,24},{48,60},{60,48},{72,84},{84,72},{1,1... | collective-permute-start | bytes 1277960 | tf_op jit(solution)/shard_map/ppermute | solution.py:69
  36.8 1.7 %collective-permute-done.5 = bf16[4,208,256]{2,1,0:T(8,128)(2,1)S(1)} collective-permute-done((bf16[4,208,256]{2,1,0:T(8,128)(2,1)S(1)}, bf16[4,208,256]{2,1,0:T(8,128)(2,1)S(1)}, u32[]{:S(2)}, u32[]{:S(2)}) %collective-permute-start.5) | collective-permute-done | bytes 426016 | tf_op jit(solution)/shard_map/ppermute | solution.py:69
  38.5 0.1 slice.52
  38.6 0.1 eq.41
  38.6 0.1 copy.22
  38.7 0.0 copy-start
  38.7 0.2 reshape.132
  38.9 0.1 broadcast_compare_fusion
  39.0 0.1 and.35
  39.2 0.1 copy.32
  39.2 0.1 broadcast_and_fusion
  39.3 1.1 %fusion.20 = (bf16[1536,1,128]{2,1,0:T(2,128)(2,1)S(1)}, bf16[1536,1,128]{2,1,0:T(2,128)(2,1)S(1)}) fusion(bf16[1536,2,128]{2,1,0:T(2,128)(2,1)S(1)} %reshape.132), kind=kLoop, calls=%fused_computation.37 | loop fusion | bytes 1572864 | tf_op jit(solution)/shard_map/slice | solution.py:77
  40.4 0.0 collective-permute-done.6
  40.4 0.0 copy-done
  40.4 0.6 fusion.24
  41.0 0.4 fusion.2
  41.5 0.5 fusion.10
  42.1 0.7 collective-permute-start.7
  42.7 0.0 collective-permute-done.7
  42.8 4.0 %convolution_convert_fusion = bf16[64,6144]{1,0:T(8,128)(2,1)S(1)} fusion(bf16[512,6144]{1,0:T(8,128)(2,1)} %param.13, bf16[2,64,128]{2,1,0:T(8,128)(2,1)S(1)} %get-tuple-element.22, bf16[2,64,128]{2,1,0:T(8,128)(2,1)S(1)} %get-tuple-element.21), kind=kOutput, calls=%fused_computation | convolution fusion | flops 403079168 | bytes 7143424 | tf_op jit(solution)/shard_map/dot_general | solution.py:99
  46.8 0.5 reshape.135
  47.3 0.4 copy.27
  47.8 55.4 %all_to_all.5 = bf16[12,64,512]{2,1,0:T(8,128)(2,1)S(1)} all-to-all(bf16[12,64,512]{2,1,0:T(8,128)(2,1)S(1)} %copy.27), channel_id=1, replica_groups=mesh['span'=8,'seq'=8,'mp'=12] {'mp'}, dimensions={0} | all-to-all | bytes 1572864 | tf_op jit(solution)/shard_map/all_to_all | solution.py:103
  103.2 0.7 reduce_sum.22
  (10 shorter events, 0.1 us)
Async XLA Ops:
  0.7 13.9 %collective-permute-start.1 = (bf16[64,256]{1,0:T(8,128)(2,1)S(1)}, bf16[64,256]{1,0:T(8,128)(2,1)S(1)}, u32[]{:S(2)}, u32[]{:S(2)}) collective-permute-start(bf16[64,256]{1,0:T(8,128)(2,1)S(1)} %pad_maximum_fusion.1), channel_id=1, source_target_pairs={{0,192},{96,288},{192,384},{288,480},{384,576},{480,672},{1,193},{... | collective-permute-start | bytes 98312 | tf_op jit(solution)/shard_map/ppermute | solution.py:16
  5.1 9.5 %collective-permute-start = (bf16[64,256]{1,0:T(8,128)(2,1)S(1)}, bf16[64,256]{1,0:T(8,128)(2,1)S(1)}, u32[]{:S(2)}, u32[]{:S(2)}) collective-permute-start(bf16[64,256]{1,0:T(8,128)(2,1)S(1)} %pad_maximum_fusion.1), channel_id=1, source_target_pairs={{0,96},{96,192},{192,288},{288,384},{384,480},{480,576},{576,672},... | collective-permute-start | bytes 98312 | tf_op jit(solution)/shard_map/ppermute | solution.py:16
  9.9 30.6 %collective-permute-start.6 = (bf16[64,256]{1,0:T(8,128)(2,1)S(1)}, bf16[64,256]{1,0:T(8,128)(2,1)S(1)}, u32[]{:S(2)}, u32[]{:S(2)}) collective-permute-start(bf16[64,256]{1,0:T(8,128)(2,1)S(1)} %slice.54), channel_id=1, source_target_pairs={{1,2},{4,5},{7,8},{10,11},{13,14},{16,17},{19,20},{22,23},{25,26},... | collective-permute-start | bytes 98312 | tf_op jit(solution)/shard_map/ppermute | solution.py:47
  14.7 13.8 %collective-permute-start.4 = (bf16[208,256]{1,0:T(8,128)(2,1)S(1)}, bf16[208,256]{1,0:T(8,128)(2,1)S(1)}, u32[]{:S(2)}, u32[]{:S(2)}) collective-permute-start(bf16[208,256]{1,0:T(8,128)(2,1)S(1)} %get-tuple-element.18), channel_id=1, source_target_pairs={{0,72},{12,84},{24,0},{36,12},{48,24},{60,36},{72,48},{84,60},{1,7... | collective-permute-start | bytes 319496 | tf_op jit(solution)/shard_map/ppermute | solution.py:67
  19.9 14.8 %collective-permute-start.3 = (bf16[208,256]{1,0:T(8,128)(2,1)S(1)}, bf16[208,256]{1,0:T(8,128)(2,1)S(1)}, u32[]{:S(2)}, u32[]{:S(2)}) collective-permute-start(bf16[208,256]{1,0:T(8,128)(2,1)S(1)} %get-tuple-element.18), channel_id=1, source_target_pairs={{0,48},{12,60},{24,72},{36,84},{48,0},{60,12},{72,24},{84,36},{1,4... | collective-permute-start | bytes 319496 | tf_op jit(solution)/shard_map/ppermute | solution.py:67
  24.6 10.1 %collective-permute-start.2 = (bf16[208,256]{1,0:T(8,128)(2,1)S(1)}, bf16[208,256]{1,0:T(8,128)(2,1)S(1)}, u32[]{:S(2)}, u32[]{:S(2)}) collective-permute-start(bf16[208,256]{1,0:T(8,128)(2,1)S(1)} %get-tuple-element.18), channel_id=1, source_target_pairs={{0,24},{12,36},{24,48},{36,60},{48,72},{60,84},{72,0},{84,12},{1,2... | collective-permute-start | bytes 319496 | tf_op jit(solution)/shard_map/ppermute | solution.py:67
  34.8 3.7 %collective-permute-start.5 = (bf16[4,208,256]{2,1,0:T(8,128)(2,1)S(1)}, bf16[4,208,256]{2,1,0:T(8,128)(2,1)S(1)}, u32[]{:S(2)}, u32[]{:S(2)}) collective-permute-start(bf16[4,208,256]{2,1,0:T(8,128)(2,1)S(1)} %pad_maximum_fusion), channel_id=1, source_target_pairs={{0,12},{12,0},{24,36},{36,24},{48,60},{60,48},{72,84},{84,72},{1,1... | collective-permute-start | bytes 1277960 | tf_op jit(solution)/shard_map/ppermute | solution.py:69
  38.7 1.7 %copy-start = (bf16[1,64,512]{2,1,0:T(8,128)(2,1)S(1)}, bf16[1,64,512]{2,1,0:T(8,128)(2,1)}, u32[]{:S(2)}) copy-start(bf16[1,64,512]{2,1,0:T(8,128)(2,1)} %param.8) | copy-start | bytes 196612
  42.1 0.7 collective-permute-start.7

commit v6 on v3

--- a/solution.py
+++ b/solution.py
@@ -23,7 +23,8 @@
     kv_count = keys.shape[2] // HEAD_DIM
     score_scale = HEAD_DIM ** (-0.5)
     span_index = lax.axis_index("span")
-    first_head = lax.axis_index("mp") * head_count
+    trio = lax.axis_size("mp_lo")
+    first_head = (lax.axis_index("mp_hi") * trio + lax.axis_index("mp_lo")) * head_count
     first_kv = jnp.minimum(first_head // GROUP, kv_count - KV_SLOTS)
     kv_slot = (first_head + jnp.arange(head_count, dtype=jnp.int32)) // GROUP - first_kv
     kv_start = first_kv * HEAD_DIM
@@ -80,27 +81,36 @@
     attended = (
         jnp.transpose(attended, (1, 0, 2)).reshape(row_count, local_width).astype(jnp.bfloat16)
     )
-    mp_count = lax.axis_size("mp")
-    out_width = out_weight.shape[1] // mp_count
+    trios = lax.axis_size("mp_hi")
+    out_width = out_weight.shape[1] // (trios * trio)
     partial_sum = jnp.dot(attended, out_weight, preferred_element_type=jnp.float32)
     partial_sum = jnp.transpose(
-        partial_sum.astype(jnp.bfloat16).reshape(row_count, mp_count, out_width), (1, 0, 2)
+        partial_sum.astype(jnp.bfloat16).reshape(row_count, trios, trio, out_width), (2, 1, 0, 3)
     )
-    received = lax.all_to_all(partial_sum, "mp", 0, 0, tiled=True)
+    received = lax.all_to_all(partial_sum, "mp_lo", 0, 0, tiled=True)
+    partial_trio = jnp.sum(received.astype(jnp.float32), axis=0).astype(jnp.bfloat16)
+    received = lax.all_to_all(partial_trio, "mp_hi", 0, 0, tiled=True)
     projected = jnp.sum(received.astype(jnp.float32), axis=0)
     return projected.astype(jnp.bfloat16)[None]
 
 
 def solution(mesh):
+    shape = dict(mesh.shape)
+    trio = 3
+    split = jax.sharding.Mesh(
+        mesh.devices.reshape(shape["span"], shape["seq"], shape["mp"] // trio, trio),
+        ("span", "seq", "mp_hi", "mp_lo"),
+    )
+    mp = ("mp_hi", "mp_lo")
     in_specs = (
-        P("span", "seq", "mp"),
+        P("span", "seq", mp),
         P("span", "seq", None),
         P("span", "seq", None),
         P("seq"),
         P(),
-        P("mp", None),
+        P(mp, None),
     )
-    out_specs = P("span", "seq", "mp")
+    out_specs = P("span", "seq", mp)
     return jax.shard_map(
-        on_device, mesh=mesh, in_specs=in_specs, out_specs=out_specs, check_vma=False
+        on_device, mesh=split, in_specs=in_specs, out_specs=out_specs, check_vma=False
     )

time: 102 us -> 103 us (level)
    all_to_all x1 -> x2, blocking collectives: 47.6 us -> 47.7 us  [the longest x1 27.9 us: on_device(): received = lax.all_to_all(partial_trio, 'mp_hi', 0, 0, tiled=True)]
where the time goes in v6:
time: 103 us; the launch traced here: 102 us
  blocking collectives  47.7 us (46%)
  waiting for transfers between devices  19.3 us (19%)
  starting transfers between devices  19 us (18%)
  local copies, waits for them, and re-layouts  8.88 us (9%)
  other arithmetic  2.82 us (3%)
  matrix products  2.45 us (2%)
  between operations  2.16 us (2%)
    all_to_all x1, blocking collectives, on_device(): received = lax.all_to_all(partial_trio, 'mp_hi', 0, 0, tiled=True)  27.9 us
    all_to_all x1, blocking collectives, on_device(): received = lax.all_to_all(partial_sum, 'mp_lo', 0, 0, tiled=True)  19.7 us
    ppermute x3, waiting for transfers between devices, on_device(): held.append(lax.ppermute(outgoing, 'seq', pairs))  13.3 us
    ppermute x3, starting transfers between devices, on_device(): held.append(lax.ppermute(outgoing, 'seq', pairs))  12.7 us
    ppermute x2, starting transfers between devices, passed_along(): return lax.ppermute(x, axis, pairs)  4.4 us
    ppermute x2, waiting for transfers between devices, passed_along(): return lax.ppermute(x, axis, pairs)  3.91 us
    ppermute x1, waiting for transfers between devices, on_device(): partner = lax.ppermute(held, 'seq', [(i, i ^ 1) for i in range(seq_count)])  2.17 us
  transfers between devices with their start and end apart: 6, of which 6 were waited for; matrix products, arithmetic and copies ran while one was open for 2% of the time, Pallas kernels for 0%

profile of v6, /device:TPU:60, one launch (start us, length us, event | category | flops | bytes accessed | tf_op | source)
XLA Modules:
  0.0 102.3 jit_solution(17669969987749827122)
XLA Ops:
  0.0 0.0 copy-start
  0.0 0.8 dynamic-slice_bitcast_fusion
  0.8 1.3 %collective-permute-start.1 = (bf16[64,512]{1,0:T(8,128)(2,1)S(1)}, bf16[64,512]{1,0:T(8,128)(2,1)S(1)}, u32[]{:S(2)}, u32[]{:S(2)}) collective-permute-start(bf16[64,512]{1,0:T(8,128)(2,1)S(1)} %pad_maximum_fusion.1), channel_id=1, source_target_pairs={{0,192},{96,288},{192,384},{288,480},{384,576},{480,672},{1,193},{... | collective-permute-start | bytes 196616 | tf_op jit(solution)/shard_map/ppermute | solution.py:16
  2.1 3.1 %collective-permute-start = (bf16[64,512]{1,0:T(8,128)(2,1)S(1)}, bf16[64,512]{1,0:T(8,128)(2,1)S(1)}, u32[]{:S(2)}, u32[]{:S(2)}) collective-permute-start(bf16[64,512]{1,0:T(8,128)(2,1)S(1)} %pad_maximum_fusion.1), channel_id=1, source_target_pairs={{0,96},{96,192},{192,288},{288,384},{384,480},{480,576},{576,672},... | collective-permute-start | bytes 196616 | tf_op jit(solution)/shard_map/ppermute | solution.py:16
  5.2 0.7 fusion.25
  5.9 2.7 %collective-permute-done.1 = bf16[64,512]{1,0:T(8,128)(2,1)S(1)} collective-permute-done((bf16[64,512]{1,0:T(8,128)(2,1)S(1)}, bf16[64,512]{1,0:T(8,128)(2,1)S(1)}, u32[]{:S(2)}, u32[]{:S(2)}) %collective-permute-start.1) | collective-permute-done | bytes 65568 | tf_op jit(solution)/shard_map/ppermute | solution.py:16
  8.6 1.2 %collective-permute-done = bf16[64,512]{1,0:T(8,128)(2,1)S(1)} collective-permute-done((bf16[64,512]{1,0:T(8,128)(2,1)S(1)}, bf16[64,512]{1,0:T(8,128)(2,1)S(1)}, u32[]{:S(2)}, u32[]{:S(2)}) %collective-permute-start) | collective-permute-done | bytes 65568 | tf_op jit(solution)/shard_map/ppermute | solution.py:16
  9.8 4.0 %collective-permute-start.4 = (bf16[208,512]{1,0:T(8,128)(2,1)S(1)}, bf16[208,512]{1,0:T(8,128)(2,1)S(1)}, u32[]{:S(2)}, u32[]{:S(2)}) collective-permute-start(bf16[208,512]{1,0:T(8,128)(2,1)S(1)} %get-tuple-element.18), channel_id=1, source_target_pairs={{0,72},{12,84},{24,0},{36,12},{48,24},{60,36},{72,48},{84,60},{1,7... | collective-permute-start | bytes 638984 | tf_op jit(solution)/shard_map/ppermute | solution.py:51
  13.9 2.9 %collective-permute-start.3 = (bf16[208,512]{1,0:T(8,128)(2,1)S(1)}, bf16[208,512]{1,0:T(8,128)(2,1)S(1)}, u32[]{:S(2)}, u32[]{:S(2)}) collective-permute-start(bf16[208,512]{1,0:T(8,128)(2,1)S(1)} %get-tuple-element.18), channel_id=1, source_target_pairs={{0,48},{12,60},{24,72},{36,84},{48,0},{60,12},{72,24},{84,36},{1,4... | collective-permute-start | bytes 638984 | tf_op jit(solution)/shard_map/ppermute | solution.py:51
  16.8 5.7 %collective-permute-start.2 = (bf16[208,512]{1,0:T(8,128)(2,1)S(1)}, bf16[208,512]{1,0:T(8,128)(2,1)S(1)}, u32[]{:S(2)}, u32[]{:S(2)}) collective-permute-start(bf16[208,512]{1,0:T(8,128)(2,1)S(1)} %get-tuple-element.18), channel_id=1, source_target_pairs={{0,24},{12,36},{24,48},{36,60},{48,72},{60,84},{72,0},{84,12},{1,2... | collective-permute-start | bytes 638984 | tf_op jit(solution)/shard_map/ppermute | solution.py:51
  22.6 1.5 %fusion.24 = (s32[1,1]{1,0:T(1,128)}, s32[1,1]{1,0:T(1,128)}, s32[1,1]{1,0:T(1,128)}) fusion(s32[8,8]{1,0:T(8,128)} %param.12, s32[]{:T(128)S(6)} %select_n.60, s32[]{:T(128)S(6)} %max.16, s32[]{:T(128)S(6)} %max.20, s32[]{:T(128)S(6)} %max.18), kind=kLoop, calls=%fused_computation.50 | loop fusion | bytes 40 | tf_op jit(solution)/shard_map/jit(dynamic_index_in_dim)/dynamic_slice | solution.py:39
  25.9 1.8 %collective-permute-done.4 = bf16[208,512]{1,0:T(8,128)(2,1)S(1)} collective-permute-done((bf16[208,512]{1,0:T(8,128)(2,1)S(1)}, bf16[208,512]{1,0:T(8,128)(2,1)S(1)}, u32[]{:S(2)}, u32[]{:S(2)}) %collective-permute-start.4) | collective-permute-done | bytes 213024 | tf_op jit(solution)/shard_map/ppermute | solution.py:51
  27.7 2.3 %collective-permute-done.3 = bf16[208,512]{1,0:T(8,128)(2,1)S(1)} collective-permute-done((bf16[208,512]{1,0:T(8,128)(2,1)S(1)}, bf16[208,512]{1,0:T(8,128)(2,1)S(1)}, u32[]{:S(2)}, u32[]{:S(2)}) %collective-permute-start.3) | collective-permute-done | bytes 213024 | tf_op jit(solution)/shard_map/ppermute | solution.py:51
  30.0 9.2 %collective-permute-done.2 = bf16[208,512]{1,0:T(8,128)(2,1)S(1)} collective-permute-done((bf16[208,512]{1,0:T(8,128)(2,1)S(1)}, bf16[208,512]{1,0:T(8,128)(2,1)S(1)}, u32[]{:S(2)}, u32[]{:S(2)}) %collective-permute-start.2) | collective-permute-done | bytes 213024 | tf_op jit(solution)/shard_map/ppermute | solution.py:51
  39.2 0.1 pad_maximum_fusion
  39.3 1.9 %collective-permute-start.5 = (bf16[4,208,512]{2,1,0:T(8,128)(2,1)S(1)}, bf16[4,208,512]{2,1,0:T(8,128)(2,1)}, u32[]{:S(2)}, u32[]{:S(2)}) collective-permute-start(bf16[4,208,512]{2,1,0:T(8,128)(2,1)S(1)} %pad_maximum_fusion), channel_id=1, source_target_pairs={{0,12},{12,0},{24,36},{36,24},{48,60},{60,48},{72,84},{84,72},{1,1... | collective-permute-start | bytes 2555912 | tf_op jit(solution)/shard_map/ppermute | solution.py:53
  41.2 0.1 add_compare_fusion
  41.3 0.1 and.42
  41.4 0.0 copy-done
  41.5 2.2 %collective-permute-done.5 = bf16[4,208,512]{2,1,0:T(8,128)(2,1)} collective-permute-done((bf16[4,208,512]{2,1,0:T(8,128)(2,1)S(1)}, bf16[4,208,512]{2,1,0:T(8,128)(2,1)}, u32[]{:S(2)}, u32[]{:S(2)}) %collective-permute-start.5) | collective-permute-done | bytes 852000 | tf_op jit(solution)/shard_map/ppermute | solution.py:53
  43.7 1.2 %constant_dynamic-update-slice_fusion = bf16[8,208,512]{2,1,0:T(8,128)(2,1)S(1)} fusion(bf16[8,208,512]{2,1,0:T(8,128)(2,1)S(1)} %constant_dynamic-update-slice_fusion.1, bf16[4,208,512]{2,1,0:T(8,128)(2,1)} %collective-permute-done.5), kind=kLoop, calls=%fused_computation.36 | loop fusion | bytes 1703936 | tf_op jit(solution)/shard_map/concatenate | solution.py:54
  45.0 0.1 slice.48
  45.1 0.1 eq.38
  45.2 0.1 copy.59
  45.3 0.4 reshape.144
  45.8 1.1 %fusion.23 = (bf16[1536,1,2,128]{3,2,1,0:T(2,128)(2,1)S(1)}, bf16[1536,1,2,128]{3,2,1,0:T(2,128)(2,1)S(1)}) fusion(bf16[1536,2,2,128]{3,2,1,0:T(2,128)(2,1)S(1)} %reshape.144), kind=kLoop, calls=%fused_computation.49 | loop fusion | bytes 3145728 | tf_op jit(solution)/shard_map/slice | solution.py:61
  46.9 0.1 broadcast_compare_fusion
  47.0 0.1 and.45
  47.1 0.1 copy.45
  47.2 0.1 broadcast_and_fusion
  47.3 0.6 convolution_bitcast_fusion
  47.8 0.0 slice-start
  47.8 0.4 fusion.21
  48.3 0.0 slice-start.1
  48.3 0.5 exponential_reduce_fusion
  48.8 0.6 convolution_bitcast_fusion.1
  49.4 0.6 slice-done
  50.0 0.8 slice-done.1
  50.8 1.3 %convolution_convert_fusion = bf16[64,6144]{1,0:T(8,128)(2,1)S(1)} fusion(bf16[512,6144]{1,0:T(8,128)(2,1)S(1)} %bitcast.101, f32[4,64]{1,0:T(4,128)S(1)} %exponential_reduce_fusion, f32[2,4,64,128]{3,2,1,0:T(8,128)S(1)} %convolution_bitcast_fusion.1, pred[4]{0:T(512)(128)(4,1)S(1)} %subtract_compare_fusion), kind=kOutput, calls=%fused_computation | convolution fusion | flops 403144704 | bytes 7341060 | tf_op jit(solution)/shard_map/dot_general | solution.py:86
  52.1 1.2 %reshape.145 = bf16[64,4,3,512]{3,2,1,0:T(4,128)(2,1)S(1)} reshape(bf16[64,6144]{1,0:T(8,128)(2,1)S(1)} %convolution_convert_fusion) | data formatting | bytes 1572864 | tf_op jit(solution)/shard_map/reshape | solution.py:88
  53.3 0.6 copy.36
  53.8 19.7 %all_to_all.10 = bf16[3,4,64,512]{3,2,1,0:T(8,128)(2,1)S(1)} all-to-all(bf16[3,4,64,512]{3,2,1,0:T(8,128)(2,1)S(1)} %copy.36), channel_id=1, replica_groups=mesh['span'=8,'seq'=8,'mp_hi'=4,'mp_lo'=3] {'mp_lo'}, dimensions={0} | all-to-all | bytes 1572864 | tf_op jit(solution)/shard_map/all_to_all | solution.py:90
  73.6 0.1 reduce_sum.34
  73.7 27.9 %all_to_all.11 = bf16[4,64,512]{2,1,0:T(8,128)(2,1)S(1)} all-to-all(bf16[4,64,512]{2,1,0:T(8,128)(2,1)S(1)} %reduce_sum.34), channel_id=1, replica_groups=mesh['span'=8,'seq'=8,'mp_hi'=4,'mp_lo'=3] {'mp_hi'}, dimensions={0} | all-to-all | bytes 524288 | tf_op jit(solution)/shard_map/all_to_all | solution.py:92
  101.6 0.7 reduce_sum.35
  (10 shorter events, 0.2 us)
Async XLA Ops:
  0.0 41.4 %copy-start = (bf16[1,64,512]{2,1,0:T(8,128)(2,1)S(1)}, bf16[1,64,512]{2,1,0:T(8,128)(2,1)}, u32[]{:S(2)}) copy-start(bf16[1,64,512]{2,1,0:T(8,128)(2,1)} %param.8) | copy-start | bytes 196612
  0.8 7.8 %collective-permute-start.1 = (bf16[64,512]{1,0:T(8,128)(2,1)S(1)}, bf16[64,512]{1,0:T(8,128)(2,1)S(1)}, u32[]{:S(2)}, u32[]{:S(2)}) collective-permute-start(bf16[64,512]{1,0:T(8,128)(2,1)S(1)} %pad_maximum_fusion.1), channel_id=1, source_target_pairs={{0,192},{96,288},{192,384},{288,480},{384,576},{480,672},{1,193},{... | collective-permute-start | bytes 196616 | tf_op jit(solution)/shard_map/ppermute | solution.py:16
  2.1 7.7 %collective-permute-start = (bf16[64,512]{1,0:T(8,128)(2,1)S(1)}, bf16[64,512]{1,0:T(8,128)(2,1)S(1)}, u32[]{:S(2)}, u32[]{:S(2)}) collective-permute-start(bf16[64,512]{1,0:T(8,128)(2,1)S(1)} %pad_maximum_fusion.1), channel_id=1, source_target_pairs={{0,96},{96,192},{192,288},{288,384},{384,480},{480,576},{576,672},... | collective-permute-start | bytes 196616 | tf_op jit(solution)/shard_map/ppermute | solution.py:16
  9.8 17.9 %collective-permute-start.4 = (bf16[208,512]{1,0:T(8,128)(2,1)S(1)}, bf16[208,512]{1,0:T(8,128)(2,1)S(1)}, u32[]{:S(2)}, u32[]{:S(2)}) collective-permute-start(bf16[208,512]{1,0:T(8,128)(2,1)S(1)} %get-tuple-element.18), channel_id=1, source_target_pairs={{0,72},{12,84},{24,0},{36,12},{48,24},{60,36},{72,48},{84,60},{1,7... | collective-permute-start | bytes 638984 | tf_op jit(solution)/shard_map/ppermute | solution.py:51
  13.9 16.1 %collective-permute-start.3 = (bf16[208,512]{1,0:T(8,128)(2,1)S(1)}, bf16[208,512]{1,0:T(8,128)(2,1)S(1)}, u32[]{:S(2)}, u32[]{:S(2)}) collective-permute-start(bf16[208,512]{1,0:T(8,128)(2,1)S(1)} %get-tuple-element.18), channel_id=1, source_target_pairs={{0,48},{12,60},{24,72},{36,84},{48,0},{60,12},{72,24},{84,36},{1,4... | collective-permute-start | bytes 638984 | tf_op jit(solution)/shard_map/ppermute | solution.py:51
  16.8 22.4 %collective-permute-start.2 = (bf16[208,512]{1,0:T(8,128)(2,1)S(1)}, bf16[208,512]{1,0:T(8,128)(2,1)S(1)}, u32[]{:S(2)}, u32[]{:S(2)}) collective-permute-start(bf16[208,512]{1,0:T(8,128)(2,1)S(1)} %get-tuple-element.18), channel_id=1, source_target_pairs={{0,24},{12,36},{24,48},{36,60},{48,72},{60,84},{72,0},{84,12},{1,2... | collective-permute-start | bytes 638984 | tf_op jit(solution)/shard_map/ppermute | solution.py:51
  39.3 4.4 %collective-permute-start.5 = (bf16[4,208,512]{2,1,0:T(8,128)(2,1)S(1)}, bf16[4,208,512]{2,1,0:T(8,128)(2,1)}, u32[]{:S(2)}, u32[]{:S(2)}) collective-permute-start(bf16[4,208,512]{2,1,0:T(8,128)(2,1)S(1)} %pad_maximum_fusion), channel_id=1, source_target_pairs={{0,12},{12,0},{24,36},{36,24},{48,60},{60,48},{72,84},{84,72},{1,1... | collective-permute-start | bytes 2555912 | tf_op jit(solution)/shard_map/ppermute | solution.py:53
  47.8 2.2 %slice-start = ((s8[6291456]{0:T(1024)(128)(4,1)}), s8[4194304]{0:T(1024)(128)(4,1)S(1)}, s32[]{:S(2)}) async-start(s8[6291456]{0:T(1024)(128)(4,1)} %bitcast.100), calls=%async_computation.2 | async-start | bytes 8388608
  48.3 2.5 %slice-start.1 = ((s8[6291456]{0:T(1024)(128)(4,1)}), s8[2097152]{0:T(1024)(128)(4,1)S(1)}, s32[]{:S(2)}) async-start(s8[6291456]{0:T(1024)(128)(4,1)} %bitcast.100), calls=%async_computation.3 | async-start | bytes 4194304

commit v7 on v3

--- a/solution.py
+++ b/solution.py
@@ -37,25 +37,29 @@
         earlier = span_index - j
         entry = lax.dynamic_index_in_dim(mask_row, jnp.maximum(earlier, 0), 0, keepdims=False)
         visible.append(jnp.where(earlier >= 0, entry, 0))
-    stacked = [packed]
-    for j in range(1, WINDOW):
-        stacked.append(passed_along(packed, "span", j))
     clip_row = jnp.zeros((CLIP_PAD, packed.shape[1]), jnp.bfloat16)
     clip_row = clip_row.at[0, :row_count].set(clip_ids.astype(jnp.bfloat16))
-    outgoing = jnp.concatenate(stacked + [clip_row], axis=0)
+    outgoing = jnp.concatenate([packed, clip_row], axis=0)
+    span_count = lax.axis_size("span")
     seq_count = lax.axis_size("seq")
-    held = [outgoing]
-    for shift in range(2, seq_count, 2):
-        pairs = [(i, (i + shift) % seq_count) for i in range(seq_count)]
-        held.append(lax.ppermute(outgoing, "seq", pairs))
-    held = jnp.stack(held, axis=0)
+    held = []
+    for j in range(WINDOW):
+        for shift in range(0, seq_count, 2):
+            if j == 0 and shift == 0:
+                held.append(outgoing)
+                continue
+            pairs = [
+                (c * seq_count + s, (c + j) * seq_count + (s + shift) % seq_count)
+                for c in range(span_count - j)
+                for s in range(seq_count)
+            ]
+            held.append(lax.ppermute(outgoing, ("span", "seq"), pairs))
+    held = jnp.stack(held, axis=0).reshape(WINDOW, seq_count // 2, *outgoing.shape)
     partner = lax.ppermute(held, "seq", [(i, i ^ 1) for i in range(seq_count)])
-    gathered = jnp.concatenate([held, partner], axis=0)
-    kv_rows = gathered[:, : WINDOW * row_count].reshape(seq_count, WINDOW, row_count, -1)
-    key_clips = gathered[:, WINDOW * row_count, :row_count].reshape(-1)
-    piece_rows = seq_count * row_count
-    window_rows = WINDOW * piece_rows
-    kv = jnp.transpose(kv_rows, (1, 0, 2, 3)).reshape(window_rows, 2, KV_SLOTS, HEAD_DIM)
+    gathered = jnp.concatenate([held, partner], axis=1)
+    key_clips = gathered[0, :, row_count, :row_count].reshape(-1)
+    window_rows = WINDOW * seq_count * row_count
+    kv = gathered[:, :, :row_count].reshape(window_rows, 2, KV_SLOTS, HEAD_DIM)
     key_all = kv[:, 0]
     value_all = kv[:, 1]
     query_heads = queries[0].reshape(row_count, head_count, HEAD_DIM)

time: 102 us -> 150 us (1.47)
  the two profiles are of different devices: /device:TPU:60 before, /device:TPU:6 now
where the time goes in v7:
time: 150 us; the launch traced here: 148 us
  starting transfers between devices  48.9 us (33%)
  blocking collectives  47.7 us (32%)
  waiting for transfers between devices  35 us (23%)
  local copies, waits for them, and re-layouts  7.48 us (5%)
  other arithmetic  3.95 us (3%)
  matrix products  2.45 us (2%)
  between operations  2.29 us (2%)
    all_to_all x1, blocking collectives, on_device(): received = lax.all_to_all(partial_sum, 'mp', 0, 0, tiled=True)  47.7 us
    ppermute x11, starting transfers between devices, on_device(): held.append(lax.ppermute(outgoing, ('span', 'seq'), pairs))  47 us
    ppermute x11, waiting for transfers between devices, on_device(): held.append(lax.ppermute(outgoing, ('span', 'seq'), pairs))  35 us
  transfers between devices with their start and end apart: 12, of which 7 were waited for; matrix products, arithmetic and copies ran while one was open for 1% of the time, Pallas kernels for 0%

profile of v7, /device:TPU:6, one launch (start us, length us, event | category | flops | bytes accessed | tf_op | source)
XLA Modules:
  0.0 147.7 jit_solution(13189033554957501681)
XLA Ops:
  0.0 0.0 copy-start.1
  0.0 0.7 fusion.26
  0.7 0.8 dynamic-slice_bitcast_fusion
  1.5 7.8 %collective-permute-start.9 = (bf16[80,512]{1,0:T(8,128)(2,1)S(1)}, bf16[80,512]{1,0:T(8,128)(2,1)S(1)}, u32[]{:S(2)}, u32[]{:S(2)}) collective-permute-start(bf16[80,512]{1,0:T(8,128)(2,1)S(1)} %fusion.14), channel_id=1, source_target_pairs={{0,240},{12,252},{24,264},{36,276},{48,192},{60,204},{72,216},{84,... | collective-permute-start | bytes 245768 | tf_op jit(solution)/shard_map/ppermute | solution.py:56
  9.3 5.2 %collective-permute-start.8 = (bf16[80,512]{1,0:T(8,128)(2,1)S(1)}, bf16[80,512]{1,0:T(8,128)(2,1)S(1)}, u32[]{:S(2)}, u32[]{:S(2)}) collective-permute-start(bf16[80,512]{1,0:T(8,128)(2,1)S(1)} %fusion.14), channel_id=1, source_target_pairs={{0,216},{12,228},{24,240},{36,252},{48,264},{60,276},{72,192},{84,... | collective-permute-start | bytes 245768 | tf_op jit(solution)/shard_map/ppermute | solution.py:56
  14.4 1.9 %collective-permute-start.7 = (bf16[80,512]{1,0:T(8,128)(2,1)S(1)}, bf16[80,512]{1,0:T(8,128)(2,1)S(1)}, u32[]{:S(2)}, u32[]{:S(2)}) collective-permute-start(bf16[80,512]{1,0:T(8,128)(2,1)S(1)} %fusion.14), channel_id=1, source_target_pairs={{0,192},{12,204},{24,216},{36,228},{48,240},{60,252},{72,264},{84,... | collective-permute-start | bytes 245768 | tf_op jit(solution)/shard_map/ppermute | solution.py:56
  16.4 1.9 %collective-permute-start.6 = (bf16[80,512]{1,0:T(8,128)(2,1)S(1)}, bf16[80,512]{1,0:T(8,128)(2,1)S(1)}, u32[]{:S(2)}, u32[]{:S(2)}) collective-permute-start(bf16[80,512]{1,0:T(8,128)(2,1)S(1)} %fusion.14), channel_id=1, source_target_pairs={{0,168},{12,180},{24,96},{36,108},{48,120},{60,132},{72,144},{84,1... | collective-permute-start | bytes 245768 | tf_op jit(solution)/shard_map/ppermute | solution.py:56
  18.3 3.1 %collective-permute-start = (bf16[80,512]{1,0:T(8,128)(2,1)S(1)}, bf16[80,512]{1,0:T(8,128)(2,1)S(1)}, u32[]{:S(2)}, u32[]{:S(2)}) collective-permute-start(bf16[80,512]{1,0:T(8,128)(2,1)S(1)} %fusion.14), channel_id=1, source_target_pairs={{0,24},{12,36},{24,48},{36,60},{48,72},{60,84},{72,0},{84,12},{96,... | collective-permute-start | bytes 245768 | tf_op jit(solution)/shard_map/ppermute | solution.py:56
  21.4 5.3 %collective-permute-done = bf16[80,512]{1,0:T(8,128)(2,1)S(1)} collective-permute-done((bf16[80,512]{1,0:T(8,128)(2,1)S(1)}, bf16[80,512]{1,0:T(8,128)(2,1)S(1)}, u32[]{:S(2)}, u32[]{:S(2)}) %collective-permute-start) | collective-permute-done | bytes 81952 | tf_op jit(solution)/shard_map/ppermute | solution.py:56
  26.7 4.7 %collective-permute-start.1 = (bf16[80,512]{1,0:T(8,128)(2,1)S(1)}, bf16[80,512]{1,0:T(8,128)(2,1)S(1)}, u32[]{:S(2)}, u32[]{:S(2)}) collective-permute-start(bf16[80,512]{1,0:T(8,128)(2,1)S(1)} %fusion.14), channel_id=1, source_target_pairs={{0,48},{12,60},{24,72},{36,84},{48,0},{60,12},{72,24},{84,36},{96,... | collective-permute-start | bytes 245768 | tf_op jit(solution)/shard_map/ppermute | solution.py:56
  31.5 5.5 %collective-permute-done.1 = bf16[80,512]{1,0:T(8,128)(2,1)S(1)} collective-permute-done((bf16[80,512]{1,0:T(8,128)(2,1)S(1)}, bf16[80,512]{1,0:T(8,128)(2,1)S(1)}, u32[]{:S(2)}, u32[]{:S(2)}) %collective-permute-start.1) | collective-permute-done | bytes 81952 | tf_op jit(solution)/shard_map/ppermute | solution.py:56
  37.0 4.7 %collective-permute-start.2 = (bf16[80,512]{1,0:T(8,128)(2,1)S(1)}, bf16[80,512]{1,0:T(8,128)(2,1)S(1)}, u32[]{:S(2)}, u32[]{:S(2)}) collective-permute-start(bf16[80,512]{1,0:T(8,128)(2,1)S(1)} %fusion.14), channel_id=1, source_target_pairs={{0,72},{12,84},{24,0},{36,12},{48,24},{60,36},{72,48},{84,60},{96,... | collective-permute-start | bytes 245768 | tf_op jit(solution)/shard_map/ppermute | solution.py:56
  41.7 2.5 %collective-permute-done.2 = bf16[80,512]{1,0:T(8,128)(2,1)S(1)} collective-permute-done((bf16[80,512]{1,0:T(8,128)(2,1)S(1)}, bf16[80,512]{1,0:T(8,128)(2,1)S(1)}, u32[]{:S(2)}, u32[]{:S(2)}) %collective-permute-start.2) | collective-permute-done | bytes 81952 | tf_op jit(solution)/shard_map/ppermute | solution.py:56
  44.2 3.0 %collective-permute-start.3 = (bf16[80,512]{1,0:T(8,128)(2,1)S(1)}, bf16[80,512]{1,0:T(8,128)(2,1)S(1)}, u32[]{:S(2)}, u32[]{:S(2)}) collective-permute-start(bf16[80,512]{1,0:T(8,128)(2,1)S(1)} %fusion.14), channel_id=1, source_target_pairs={{0,96},{12,108},{24,120},{36,132},{48,144},{60,156},{72,168},{84,1... | collective-permute-start | bytes 245768 | tf_op jit(solution)/shard_map/ppermute | solution.py:56
  47.2 6.1 %collective-permute-done.3 = bf16[80,512]{1,0:T(8,128)(2,1)S(1)} collective-permute-done((bf16[80,512]{1,0:T(8,128)(2,1)S(1)}, bf16[80,512]{1,0:T(8,128)(2,1)S(1)}, u32[]{:S(2)}, u32[]{:S(2)}) %collective-permute-start.3) | collective-permute-done | bytes 81952 | tf_op jit(solution)/shard_map/ppermute | solution.py:56
  53.3 4.8 %collective-permute-start.4 = (bf16[80,512]{1,0:T(8,128)(2,1)S(1)}, bf16[80,512]{1,0:T(8,128)(2,1)S(1)}, u32[]{:S(2)}, u32[]{:S(2)}) collective-permute-start(bf16[80,512]{1,0:T(8,128)(2,1)S(1)} %fusion.14), channel_id=1, source_target_pairs={{0,120},{12,132},{24,144},{36,156},{48,168},{60,180},{72,96},{84,1... | collective-permute-start | bytes 245768 | tf_op jit(solution)/shard_map/ppermute | solution.py:56
  58.2 4.5 %collective-permute-done.4 = bf16[80,512]{1,0:T(8,128)(2,1)S(1)} collective-permute-done((bf16[80,512]{1,0:T(8,128)(2,1)S(1)}, bf16[80,512]{1,0:T(8,128)(2,1)S(1)}, u32[]{:S(2)}, u32[]{:S(2)}) %collective-permute-start.4) | collective-permute-done | bytes 81952 | tf_op jit(solution)/shard_map/ppermute | solution.py:56
  62.6 6.1 %collective-permute-start.5 = (bf16[80,512]{1,0:T(8,128)(2,1)S(1)}, bf16[80,512]{1,0:T(8,128)(2,1)S(1)}, u32[]{:S(2)}, u32[]{:S(2)}) collective-permute-start(bf16[80,512]{1,0:T(8,128)(2,1)S(1)} %fusion.14), channel_id=1, source_target_pairs={{0,144},{12,156},{24,168},{36,180},{48,96},{60,108},{72,120},{84,1... | collective-permute-start | bytes 245768 | tf_op jit(solution)/shard_map/ppermute | solution.py:56
  68.7 5.4 %collective-permute-done.5 = bf16[80,512]{1,0:T(8,128)(2,1)S(1)} collective-permute-done((bf16[80,512]{1,0:T(8,128)(2,1)S(1)}, bf16[80,512]{1,0:T(8,128)(2,1)S(1)}, u32[]{:S(2)}, u32[]{:S(2)}) %collective-permute-start.5) | collective-permute-done | bytes 81952 | tf_op jit(solution)/shard_map/ppermute | solution.py:56
  74.1 3.7 %collective-permute-start.10 = (bf16[80,512]{1,0:T(8,128)(2,1)S(1)}, bf16[80,512]{1,0:T(8,128)(2,1)S(1)}, u32[]{:S(2)}, u32[]{:S(2)}) collective-permute-start(bf16[80,512]{1,0:T(8,128)(2,1)S(1)} %fusion.14), channel_id=1, source_target_pairs={{0,264},{12,276},{24,192},{36,204},{48,216},{60,228},{72,240},{84,... | collective-permute-start | bytes 245768 | tf_op jit(solution)/shard_map/ppermute | solution.py:56
  77.8 0.0 collective-permute-done.6
  77.9 0.0 collective-permute-done.7
  77.9 0.0 collective-permute-done.8
  77.9 0.0 collective-permute-done.9
  77.9 5.8 %collective-permute-done.10 = bf16[80,512]{1,0:T(8,128)(2,1)S(1)} collective-permute-done((bf16[80,512]{1,0:T(8,128)(2,1)S(1)}, bf16[80,512]{1,0:T(8,128)(2,1)S(1)}, u32[]{:S(2)}, u32[]{:S(2)}) %collective-permute-start.10) | collective-permute-done | bytes 81952 | tf_op jit(solution)/shard_map/ppermute | solution.py:56
  83.8 1.9 %collective-permute-start.11 = (bf16[3,4,80,512]{3,2,1,0:T(8,128)(2,1)S(1)}, bf16[3,4,80,512]{3,2,1,0:T(8,128)(2,1)S(1)}, u32[]{:S(2)}, u32[]{:S(2)}) collective-permute-start(bf16[3,4,80,512]{3,2,1,0:T(8,128)(2,1)S(1)} %bitcast.113), channel_id=1, source_target_pairs={{0,12},{12,0},{24,36},{36,24},{48,60},{60,48},{72,84},{84,72},{1,1... | collective-permute-start | bytes 2949128 | tf_op jit(solution)/shard_map/ppermute | solution.py:58
  85.7 1.4 fusion.25
  89.0 0.1 add_compare_fusion
  89.1 0.1 and.41
  89.2 0.0 copy-done.1
  89.3 0.0 collective-permute-done.11
  89.3 0.0 copy-start
  89.3 0.9 copy-done
  90.2 0.1 eq.38
  90.3 1.3 fusion
  91.6 0.4 reshape.144
  92.0 1.1 fusion.24
  93.2 0.1 broadcast_compare_fusion
  93.3 0.1 and.44
  93.4 0.1 copy.27
  93.4 0.1 broadcast_and_fusion
  93.5 0.6 convolution_bitcast_fusion
  94.1 0.0 slice-start
  94.1 0.4 fusion.23
  94.5 0.0 slice-start.1
  94.5 0.5 exponential_reduce_fusion
  95.1 0.6 convolution_bitcast_fusion.1
  95.7 0.6 slice-done
  96.3 0.8 slice-done.1
  97.1 1.3 convolution_convert_fusion
  98.3 0.5 reshape.145
  98.9 0.4 copy.21
  99.3 47.7 %all_to_all.5 = bf16[12,64,512]{2,1,0:T(8,128)(2,1)S(1)} all-to-all(bf16[12,64,512]{2,1,0:T(8,128)(2,1)S(1)} %copy.21), channel_id=1, replica_groups=mesh['span'=8,'seq'=8,'mp'=12] {'mp'}, dimensions={0} | all-to-all | bytes 1572864 | tf_op jit(solution)/shard_map/all_to_all | solution.py:93
  147.0 0.7 reduce_sum.22
  (18 shorter events, 0.2 us)
Async XLA Ops:
  0.0 89.2 %copy-start.1 = (bf16[1,64,512]{2,1,0:T(8,128)(2,1)S(1)}, bf16[1,64,512]{2,1,0:T(8,128)(2,1)}, u32[]{:S(2)}) copy-start(bf16[1,64,512]{2,1,0:T(8,128)(2,1)} %param.8) | copy-start | bytes 196612
  1.5 76.4 %collective-permute-start.9 = (bf16[80,512]{1,0:T(8,128)(2,1)S(1)}, bf16[80,512]{1,0:T(8,128)(2,1)S(1)}, u32[]{:S(2)}, u32[]{:S(2)}) collective-permute-start(bf16[80,512]{1,0:T(8,128)(2,1)S(1)} %fusion.14), channel_id=1, source_target_pairs={{0,240},{12,252},{24,264},{36,276},{48,192},{60,204},{72,216},{84,... | collective-permute-start | bytes 245768 | tf_op jit(solution)/shard_map/ppermute | solution.py:56
  9.3 68.6 %collective-permute-start.8 = (bf16[80,512]{1,0:T(8,128)(2,1)S(1)}, bf16[80,512]{1,0:T(8,128)(2,1)S(1)}, u32[]{:S(2)}, u32[]{:S(2)}) collective-permute-start(bf16[80,512]{1,0:T(8,128)(2,1)S(1)} %fusion.14), channel_id=1, source_target_pairs={{0,216},{12,228},{24,240},{36,252},{48,264},{60,276},{72,192},{84,... | collective-permute-start | bytes 245768 | tf_op jit(solution)/shard_map/ppermute | solution.py:56
  14.4 63.4 %collective-permute-start.7 = (bf16[80,512]{1,0:T(8,128)(2,1)S(1)}, bf16[80,512]{1,0:T(8,128)(2,1)S(1)}, u32[]{:S(2)}, u32[]{:S(2)}) collective-permute-start(bf16[80,512]{1,0:T(8,128)(2,1)S(1)} %fusion.14), channel_id=1, source_target_pairs={{0,192},{12,204},{24,216},{36,228},{48,240},{60,252},{72,264},{84,... | collective-permute-start | bytes 245768 | tf_op jit(solution)/shard_map/ppermute | solution.py:56
  16.4 61.5 %collective-permute-start.6 = (bf16[80,512]{1,0:T(8,128)(2,1)S(1)}, bf16[80,512]{1,0:T(8,128)(2,1)S(1)}, u32[]{:S(2)}, u32[]{:S(2)}) collective-permute-start(bf16[80,512]{1,0:T(8,128)(2,1)S(1)} %fusion.14), channel_id=1, source_target_pairs={{0,168},{12,180},{24,96},{36,108},{48,120},{60,132},{72,144},{84,1... | collective-permute-start | bytes 245768 | tf_op jit(solution)/shard_map/ppermute | solution.py:56
  18.3 8.4 %collective-permute-start = (bf16[80,512]{1,0:T(8,128)(2,1)S(1)}, bf16[80,512]{1,0:T(8,128)(2,1)S(1)}, u32[]{:S(2)}, u32[]{:S(2)}) collective-permute-start(bf16[80,512]{1,0:T(8,128)(2,1)S(1)} %fusion.14), channel_id=1, source_target_pairs={{0,24},{12,36},{24,48},{36,60},{48,72},{60,84},{72,0},{84,12},{96,... | collective-permute-start | bytes 245768 | tf_op jit(solution)/shard_map/ppermute | solution.py:56
  26.7 10.2 %collective-permute-start.1 = (bf16[80,512]{1,0:T(8,128)(2,1)S(1)}, bf16[80,512]{1,0:T(8,128)(2,1)S(1)}, u32[]{:S(2)}, u32[]{:S(2)}) collective-permute-start(bf16[80,512]{1,0:T(8,128)(2,1)S(1)} %fusion.14), channel_id=1, source_target_pairs={{0,48},{12,60},{24,72},{36,84},{48,0},{60,12},{72,24},{84,36},{96,... | collective-permute-start | bytes 245768 | tf_op jit(solution)/shard_map/ppermute | solution.py:56
  37.0 7.2 %collective-permute-start.2 = (bf16[80,512]{1,0:T(8,128)(2,1)S(1)}, bf16[80,512]{1,0:T(8,128)(2,1)S(1)}, u32[]{:S(2)}, u32[]{:S(2)}) collective-permute-start(bf16[80,512]{1,0:T(8,128)(2,1)S(1)} %fusion.14), channel_id=1, source_target_pairs={{0,72},{12,84},{24,0},{36,12},{48,24},{60,36},{72,48},{84,60},{96,... | collective-permute-start | bytes 245768 | tf_op jit(solution)/shard_map/ppermute | solution.py:56
  44.2 9.1 %collective-permute-start.3 = (bf16[80,512]{1,0:T(8,128)(2,1)S(1)}, bf16[80,512]{1,0:T(8,128)(2,1)S(1)}, u32[]{:S(2)}, u32[]{:S(2)}) collective-permute-start(bf16[80,512]{1,0:T(8,128)(2,1)S(1)} %fusion.14), channel_id=1, source_target_pairs={{0,96},{12,108},{24,120},{36,132},{48,144},{60,156},{72,168},{84,1... | collective-permute-start | bytes 245768 | tf_op jit(solution)/shard_map/ppermute | solution.py:56
  53.3 9.3 %collective-permute-start.4 = (bf16[80,512]{1,0:T(8,128)(2,1)S(1)}, bf16[80,512]{1,0:T(8,128)(2,1)S(1)}, u32[]{:S(2)}, u32[]{:S(2)}) collective-permute-start(bf16[80,512]{1,0:T(8,128)(2,1)S(1)} %fusion.14), channel_id=1, source_target_pairs={{0,120},{12,132},{24,144},{36,156},{48,168},{60,180},{72,96},{84,1... | collective-permute-start | bytes 245768 | tf_op jit(solution)/shard_map/ppermute | solution.py:56
  62.6 11.5 %collective-permute-start.5 = (bf16[80,512]{1,0:T(8,128)(2,1)S(1)}, bf16[80,512]{1,0:T(8,128)(2,1)S(1)}, u32[]{:S(2)}, u32[]{:S(2)}) collective-permute-start(bf16[80,512]{1,0:T(8,128)(2,1)S(1)} %fusion.14), channel_id=1, source_target_pairs={{0,144},{12,156},{24,168},{36,180},{48,96},{60,108},{72,120},{84,1... | collective-permute-start | bytes 245768 | tf_op jit(solution)/shard_map/ppermute | solution.py:56
  74.1 9.6 %collective-permute-start.10 = (bf16[80,512]{1,0:T(8,128)(2,1)S(1)}, bf16[80,512]{1,0:T(8,128)(2,1)S(1)}, u32[]{:S(2)}, u32[]{:S(2)}) collective-permute-start(bf16[80,512]{1,0:T(8,128)(2,1)S(1)} %fusion.14), channel_id=1, source_target_pairs={{0,264},{12,276},{24,192},{36,204},{48,216},{60,228},{72,240},{84,... | collective-permute-start | bytes 245768 | tf_op jit(solution)/shard_map/ppermute | solution.py:56
  83.8 5.5 %collective-permute-start.11 = (bf16[3,4,80,512]{3,2,1,0:T(8,128)(2,1)S(1)}, bf16[3,4,80,512]{3,2,1,0:T(8,128)(2,1)S(1)}, u32[]{:S(2)}, u32[]{:S(2)}) collective-permute-start(bf16[3,4,80,512]{3,2,1,0:T(8,128)(2,1)S(1)} %bitcast.113), channel_id=1, source_target_pairs={{0,12},{12,0},{24,36},{36,24},{48,60},{60,48},{72,84},{84,72},{1,1... | collective-permute-start | bytes 2949128 | tf_op jit(solution)/shard_map/ppermute | solution.py:58
  89.3 1.0 copy-start
  94.1 2.2 %slice-start = ((s8[6291456]{0:T(1024)(128)(4,1)}), s8[4194304]{0:T(1024)(128)(4,1)S(1)}, s32[]{:S(2)}) async-start(s8[6291456]{0:T(1024)(128)(4,1)} %bitcast.111), calls=%async_computation.1 | async-start | bytes 8388608
  94.5 2.5 %slice-start.1 = ((s8[6291456]{0:T(1024)(128)(4,1)}), s8[2097152]{0:T(1024)(128)(4,1)S(1)}, s32[]{:S(2)}) async-start(s8[6291456]{0:T(1024)(128)(4,1)} %bitcast.111), calls=%async_computation.2 | async-start | bytes 4194304

commit v8 on v3

--- a/solution.py
+++ b/solution.py
@@ -50,32 +50,42 @@
         held.append(lax.ppermute(outgoing, "seq", pairs))
     held = jnp.stack(held, axis=0)
     partner = lax.ppermute(held, "seq", [(i, i ^ 1) for i in range(seq_count)])
-    gathered = jnp.concatenate([held, partner], axis=0)
-    kv_rows = gathered[:, : WINDOW * row_count].reshape(seq_count, WINDOW, row_count, -1)
-    key_clips = gathered[:, WINDOW * row_count, :row_count].reshape(-1)
-    piece_rows = seq_count * row_count
-    window_rows = WINDOW * piece_rows
-    kv = jnp.transpose(kv_rows, (1, 0, 2, 3)).reshape(window_rows, 2, KV_SLOTS, HEAD_DIM)
-    key_all = kv[:, 0]
-    value_all = kv[:, 1]
     query_heads = queries[0].reshape(row_count, head_count, HEAD_DIM)
-    s_both = jnp.einsum(
-        "qhd,kad->ahqk", query_heads, key_all, preferred_element_type=jnp.float32
-    )
     pick = kv_slot[:, None, None] == 0
-    s = jnp.where(pick, s_both[0], s_both[1]) * score_scale
     span_ok = jnp.stack(visible) == 1
     query_clips = clip_ids.astype(jnp.bfloat16)
-    allowed = span_ok[None, :, None] & (query_clips[:, None, None] == key_clips[None, None, :])
-    allowed = allowed.reshape(row_count, window_rows)
-    s = jnp.where(allowed[None], s, -jnp.inf)
-    top = jnp.max(s, axis=2, keepdims=True)
+
+    def piece_scores(piece):
+        blocks = piece.shape[0]
+        kv_rows = piece[:, : WINDOW * row_count].reshape(blocks, WINDOW, row_count, -1)
+        key_clips = piece[:, WINDOW * row_count, :row_count].reshape(-1)
+        rows = WINDOW * blocks * row_count
+        kv = jnp.transpose(kv_rows, (1, 0, 2, 3)).reshape(rows, 2, KV_SLOTS, HEAD_DIM)
+        s_both = jnp.einsum(
+            "qhd,kad->ahqk", query_heads, kv[:, 0], preferred_element_type=jnp.float32
+        )
+        s = jnp.where(pick, s_both[0], s_both[1]) * score_scale
+        same = query_clips[:, None, None] == key_clips[None, None, :]
+        allowed = (span_ok[None, :, None] & same).reshape(row_count, rows)
+        return jnp.where(allowed[None], s, -jnp.inf), kv[:, 1]
+
+    def weighted(p, value_all):
+        acc_both = jnp.einsum(
+            "hqk,kad->ahqd", p.astype(jnp.bfloat16), value_all, preferred_element_type=jnp.float32
+        )
+        return jnp.where(pick, acc_both[0], acc_both[1])
+
+    s, value_all = piece_scores(held)
+    first_top = jnp.max(s, axis=2, keepdims=True)
+    p = jnp.exp(s - first_top)
+    first_total = jnp.sum(p, axis=2, keepdims=True)
+    first_acc = weighted(p, value_all)
+    s, value_all = piece_scores(partner)
+    top = jnp.maximum(first_top, jnp.max(s, axis=2, keepdims=True))
     p = jnp.exp(s - top)
-    total = jnp.sum(p, axis=2, keepdims=True)
-    acc_both = jnp.einsum(
-        "hqk,kad->ahqd", p.astype(jnp.bfloat16), value_all, preferred_element_type=jnp.float32
-    )
-    acc = jnp.where(pick, acc_both[0], acc_both[1])
+    factor = jnp.exp(first_top - top)
+    total = first_total * factor + jnp.sum(p, axis=2, keepdims=True)
+    acc = first_acc * factor + weighted(p, value_all)
     attended = acc / total
     attended = (
         jnp.transpose(attended, (1, 0, 2)).reshape(row_count, local_width).astype(jnp.bfloat16)

time: 102 us -> 100 us (0.980)
  the two profiles are of different devices: /device:TPU:60 before, /device:TPU:64 now
where the time goes in v8:
time: 100 us; the launch traced here: 99.8 us
  blocking collectives  47.7 us (48%)
  starting transfers between devices  25 us (25%)
  waiting for transfers between devices  12 us (12%)
  local copies, waits for them, and re-layouts  7.22 us (7%)
  matrix products  2.85 us (3%)
  other arithmetic  2.82 us (3%)
  between operations  2.2 us (2%)
    all_to_all x1, blocking collectives, on_device(): received = lax.all_to_all(partial_sum, 'mp', 0, 0, tiled=True)  47.7 us
    ppermute x3, starting transfers between devices, on_device(): held.append(lax.ppermute(outgoing, 'seq', pairs))  15.7 us
    ppermute x3, waiting for transfers between devices, on_device(): held.append(lax.ppermute(outgoing, 'seq', pairs))  10.7 us
    ppermute x2, starting transfers between devices, passed_along(): return lax.ppermute(x, axis, pairs)  7.43 us
  transfers between devices with their start and end apart: 6, of which 3 were waited for; matrix products, arithmetic and copies ran while one was open for 4% of the time, Pallas kernels for 0%

profile of v8, /device:TPU:64, one launch (start us, length us, event | category | flops | bytes accessed | tf_op | source)
XLA Modules:
  0.0 99.8 jit_solution(7476103434693052590)
XLA Ops:
  0.0 0.0 copy-start.1
  0.0 0.8 dynamic-slice_bitcast_fusion
  0.8 4.9 %collective-permute-start.1 = (bf16[64,512]{1,0:T(8,128)(2,1)S(1)}, bf16[64,512]{1,0:T(8,128)(2,1)S(1)}, u32[]{:S(2)}, u32[]{:S(2)}) collective-permute-start(bf16[64,512]{1,0:T(8,128)(2,1)S(1)} %pad_maximum_fusion.1), channel_id=1, source_target_pairs={{0,192},{96,288},{192,384},{288,480},{384,576},{480,672},{1,193},{... | collective-permute-start | bytes 196616 | tf_op jit(solution)/shard_map/ppermute | solution.py:16
  5.8 2.5 %collective-permute-start = (bf16[64,512]{1,0:T(8,128)(2,1)S(1)}, bf16[64,512]{1,0:T(8,128)(2,1)S(1)}, u32[]{:S(2)}, u32[]{:S(2)}) collective-permute-start(bf16[64,512]{1,0:T(8,128)(2,1)S(1)} %pad_maximum_fusion.1), channel_id=1, source_target_pairs={{0,96},{96,192},{192,288},{288,384},{384,480},{480,576},{576,672},... | collective-permute-start | bytes 196616 | tf_op jit(solution)/shard_map/ppermute | solution.py:16
  8.3 0.7 fusion.42
  8.9 0.0 collective-permute-done.1
  8.9 1.2 %collective-permute-done = bf16[64,512]{1,0:T(8,128)(2,1)S(1)} collective-permute-done((bf16[64,512]{1,0:T(8,128)(2,1)S(1)}, bf16[64,512]{1,0:T(8,128)(2,1)S(1)}, u32[]{:S(2)}, u32[]{:S(2)}) %collective-permute-start) | collective-permute-done | bytes 65568 | tf_op jit(solution)/shard_map/ppermute | solution.py:16
  10.2 7.7 %collective-permute-start.3 = (bf16[208,512]{1,0:T(8,128)(2,1)S(1)}, bf16[208,512]{1,0:T(8,128)(2,1)S(1)}, u32[]{:S(2)}, u32[]{:S(2)}) collective-permute-start(bf16[208,512]{1,0:T(8,128)(2,1)S(1)} %fusion.19), channel_id=1, source_target_pairs={{0,48},{12,60},{24,72},{36,84},{48,0},{60,12},{72,24},{84,36},{1,4... | collective-permute-start | bytes 638984 | tf_op jit(solution)/shard_map/ppermute | solution.py:50
  17.9 2.7 %collective-permute-start.2 = (bf16[208,512]{1,0:T(8,128)(2,1)S(1)}, bf16[208,512]{1,0:T(8,128)(2,1)S(1)}, u32[]{:S(2)}, u32[]{:S(2)}) collective-permute-start(bf16[208,512]{1,0:T(8,128)(2,1)S(1)} %fusion.19), channel_id=1, source_target_pairs={{0,24},{12,36},{24,48},{36,60},{48,72},{60,84},{72,0},{84,12},{1,2... | collective-permute-start | bytes 638984 | tf_op jit(solution)/shard_map/ppermute | solution.py:50
  20.6 5.3 %collective-permute-start.4 = (bf16[208,512]{1,0:T(8,128)(2,1)S(1)}, bf16[208,512]{1,0:T(8,128)(2,1)S(1)}, u32[]{:S(2)}, u32[]{:S(2)}) collective-permute-start(bf16[208,512]{1,0:T(8,128)(2,1)S(1)} %fusion.19), channel_id=1, source_target_pairs={{0,72},{12,84},{24,0},{36,12},{48,24},{60,36},{72,48},{84,60},{1,7... | collective-permute-start | bytes 638984 | tf_op jit(solution)/shard_map/ppermute | solution.py:50
  25.9 1.4 %fusion.41 = (s32[1,1]{1,0:T(1,128)}, s32[1,1]{1,0:T(1,128)}, s32[1,1]{1,0:T(1,128)}) fusion(s32[8,8]{1,0:T(8,128)} %param.12, s32[]{:T(128)S(6)} %select_n.75, s32[]{:T(128)S(6)} %max.30, s32[]{:T(128)S(6)} %max.34, s32[]{:T(128)S(6)} %max.32), kind=kLoop, calls=%fused_computation.76 | loop fusion | bytes 40 | tf_op jit(solution)/shard_map/jit(dynamic_index_in_dim)/dynamic_slice | solution.py:38
  29.3 0.0 collective-permute-done.3
  29.3 2.0 %collective-permute-done.2 = bf16[208,512]{1,0:T(8,128)(2,1)S(1)} collective-permute-done((bf16[208,512]{1,0:T(8,128)(2,1)S(1)}, bf16[208,512]{1,0:T(8,128)(2,1)S(1)}, u32[]{:S(2)}, u32[]{:S(2)}) %collective-permute-start.2) | collective-permute-done | bytes 213024 | tf_op jit(solution)/shard_map/ppermute | solution.py:50
  31.3 8.7 %collective-permute-done.4 = bf16[208,512]{1,0:T(8,128)(2,1)S(1)} collective-permute-done((bf16[208,512]{1,0:T(8,128)(2,1)S(1)}, bf16[208,512]{1,0:T(8,128)(2,1)S(1)}, u32[]{:S(2)}, u32[]{:S(2)}) %collective-permute-start.4) | collective-permute-done | bytes 213024 | tf_op jit(solution)/shard_map/ppermute | solution.py:50
  40.0 0.1 pad_maximum_fusion
  40.1 1.9 %collective-permute-start.5 = (bf16[4,208,512]{2,1,0:T(8,128)(2,1)S(1)}, bf16[4,208,512]{2,1,0:T(8,128)(2,1)S(1)}, u32[]{:S(2)}, u32[]{:S(2)}) collective-permute-start(bf16[4,208,512]{2,1,0:T(8,128)(2,1)S(1)} %pad_maximum_fusion), channel_id=1, source_target_pairs={{0,12},{12,0},{24,36},{36,24},{48,60},{60,48},{72,84},{84,72},{1,1... | collective-permute-start | bytes 2555912 | tf_op jit(solution)/shard_map/ppermute | solution.py:52
  42.0 0.1 add_compare_fusion
  42.1 0.1 and.58
  42.2 0.0 copy-done.1
  42.2 0.1 slice.80
  42.3 0.1 eq.56
  42.4 0.1 copy.71
  42.5 0.2 reshape.222
  42.7 1.3 %fusion.39 = (bf16[768,1,2,128]{3,2,1,0:T(2,128)(2,1)}, bf16[768,1,2,128]{3,2,1,0:T(2,128)(2,1)S(1)}) fusion(bf16[768,2,2,128]{3,2,1,0:T(2,128)(2,1)S(1)} %reshape.222), kind=kLoop, calls=%fused_computation.74 | loop fusion | bytes 1572864 | tf_op jit(solution)/shard_map/slice | solution.py:70
  44.0 0.4 convolution_bitcast_fusion.1
  44.3 0.0 collective-permute-done.5
  44.4 0.1 eq.59
  44.5 0.1 slice.89
  44.5 0.1 copy.33
  44.6 0.2 reshape.224
  44.8 0.5 fusion.40
  45.4 0.1 broadcast_compare_fusion.1
  45.5 0.1 and.61
  45.6 0.1 and.64
  45.7 0.0 slice-start
  45.7 0.4 convolution_bitcast_fusion
  46.1 0.1 broadcast_and_fusion.1
  46.1 0.0 copy-start
  46.1 0.4 fusion.38
  46.6 0.8 copy-done
  47.4 0.0 slice-start.1
  47.4 0.4 convolution_bitcast_fusion.3
  47.8 0.6 exponential_reduce_fusion.1
  48.4 0.4 convolution_bitcast_fusion.2
  48.8 0.0 slice-done
  48.8 0.3 slice-done.1
  49.1 1.3 %convolution_convert_fusion = bf16[64,6144]{1,0:T(8,128)(2,1)S(1)} fusion(bf16[512,6144]{1,0:T(8,128)(2,1)S(1)} %bitcast.170, f32[4,64]{1,0:T(4,128)S(1)} %get-tuple-element.21, f32[2,4,64,128]{3,2,1,0:T(8,128)S(1)} %convolution_bitcast_fusion.2, f32[4,64]{1,0:T(4,128)S(1)} %get-tuple-element.22, f32[2,4,64,128]{3,2,1,0:T(8,128)S(1)} %convolution_bitcast_fusion.3, ...), kind=kOutput, calls=%fused_computation | convolution fusion | flops 403243008 | bytes 7604228 | tf_op jit(solution)/shard_map/dot_general | solution.py:95
  50.4 0.5 reshape.225
  50.9 0.4 copy.38
  51.4 47.7 %all_to_all.5 = bf16[12,64,512]{2,1,0:T(8,128)(2,1)S(1)} all-to-all(bf16[12,64,512]{2,1,0:T(8,128)(2,1)S(1)} %copy.38), channel_id=1, replica_groups=mesh['span'=8,'seq'=8,'mp'=12] {'mp'}, dimensions={0} | all-to-all | bytes 1572864 | tf_op jit(solution)/shard_map/all_to_all | solution.py:99
  99.1 0.7 reduce_sum.32
  (13 shorter events, 0.2 us)
Async XLA Ops:
  0.0 42.2 %copy-start.1 = (bf16[1,64,512]{2,1,0:T(8,128)(2,1)S(1)}, bf16[1,64,512]{2,1,0:T(8,128)(2,1)}, u32[]{:S(2)}) copy-start(bf16[1,64,512]{2,1,0:T(8,128)(2,1)} %param.8) | copy-start | bytes 196612
  0.8 8.1 %collective-permute-start.1 = (bf16[64,512]{1,0:T(8,128)(2,1)S(1)}, bf16[64,512]{1,0:T(8,128)(2,1)S(1)}, u32[]{:S(2)}, u32[]{:S(2)}) collective-permute-start(bf16[64,512]{1,0:T(8,128)(2,1)S(1)} %pad_maximum_fusion.1), channel_id=1, source_target_pairs={{0,192},{96,288},{192,384},{288,480},{384,576},{480,672},{1,193},{... | collective-permute-start | bytes 196616 | tf_op jit(solution)/shard_map/ppermute | solution.py:16
  5.8 4.4 %collective-permute-start = (bf16[64,512]{1,0:T(8,128)(2,1)S(1)}, bf16[64,512]{1,0:T(8,128)(2,1)S(1)}, u32[]{:S(2)}, u32[]{:S(2)}) collective-permute-start(bf16[64,512]{1,0:T(8,128)(2,1)S(1)} %pad_maximum_fusion.1), channel_id=1, source_target_pairs={{0,96},{96,192},{192,288},{288,384},{384,480},{480,576},{576,672},... | collective-permute-start | bytes 196616 | tf_op jit(solution)/shard_map/ppermute | solution.py:16
  10.2 19.1 %collective-permute-start.3 = (bf16[208,512]{1,0:T(8,128)(2,1)S(1)}, bf16[208,512]{1,0:T(8,128)(2,1)S(1)}, u32[]{:S(2)}, u32[]{:S(2)}) collective-permute-start(bf16[208,512]{1,0:T(8,128)(2,1)S(1)} %fusion.19), channel_id=1, source_target_pairs={{0,48},{12,60},{24,72},{36,84},{48,0},{60,12},{72,24},{84,36},{1,4... | collective-permute-start | bytes 638984 | tf_op jit(solution)/shard_map/ppermute | solution.py:50
  17.9 13.4 %collective-permute-start.2 = (bf16[208,512]{1,0:T(8,128)(2,1)S(1)}, bf16[208,512]{1,0:T(8,128)(2,1)S(1)}, u32[]{:S(2)}, u32[]{:S(2)}) collective-permute-start(bf16[208,512]{1,0:T(8,128)(2,1)S(1)} %fusion.19), channel_id=1, source_target_pairs={{0,24},{12,36},{24,48},{36,60},{48,72},{60,84},{72,0},{84,12},{1,2... | collective-permute-start | bytes 638984 | tf_op jit(solution)/shard_map/ppermute | solution.py:50
  20.6 19.4 %collective-permute-start.4 = (bf16[208,512]{1,0:T(8,128)(2,1)S(1)}, bf16[208,512]{1,0:T(8,128)(2,1)S(1)}, u32[]{:S(2)}, u32[]{:S(2)}) collective-permute-start(bf16[208,512]{1,0:T(8,128)(2,1)S(1)} %fusion.19), channel_id=1, source_target_pairs={{0,72},{12,84},{24,0},{36,12},{48,24},{60,36},{72,48},{84,60},{1,7... | collective-permute-start | bytes 638984 | tf_op jit(solution)/shard_map/ppermute | solution.py:50
  40.1 4.3 %collective-permute-start.5 = (bf16[4,208,512]{2,1,0:T(8,128)(2,1)S(1)}, bf16[4,208,512]{2,1,0:T(8,128)(2,1)S(1)}, u32[]{:S(2)}, u32[]{:S(2)}) collective-permute-start(bf16[4,208,512]{2,1,0:T(8,128)(2,1)S(1)} %pad_maximum_fusion), channel_id=1, source_target_pairs={{0,12},{12,0},{24,36},{36,24},{48,60},{60,48},{72,84},{84,72},{1,1... | collective-permute-start | bytes 2555912 | tf_op jit(solution)/shard_map/ppermute | solution.py:52
  45.7 3.1 %slice-start = ((s8[6291456]{0:T(1024)(128)(4,1)}), s8[4194304]{0:T(1024)(128)(4,1)S(1)}, s32[]{:S(2)}) async-start(s8[6291456]{0:T(1024)(128)(4,1)} %bitcast.169), calls=%async_computation.1 | async-start | bytes 8388608
  46.1 1.2 %copy-start = (bf16[768,1,2,128]{3,2,1,0:T(2,128)(2,1)S(1)}, bf16[768,1,2,128]{3,2,1,0:T(2,128)(2,1)}, u32[]{:S(2)}) copy-start(bf16[768,1,2,128]{3,2,1,0:T(2,128)(2,1)} %get-tuple-element.23) | copy-start | bytes 1179652
  47.4 1.7 %slice-start.1 = ((s8[6291456]{0:T(1024)(128)(4,1)}), s8[2097152]{0:T(1024)(128)(4,1)S(1)}, s32[]{:S(2)}) async-start(s8[6291456]{0:T(1024)(128)(4,1)} %bitcast.169), calls=%async_computation.2 | async-start | bytes 4194304

commit v9 on v8

--- a/solution.py
+++ b/solution.py
@@ -23,7 +23,8 @@
     kv_count = keys.shape[2] // HEAD_DIM
     score_scale = HEAD_DIM ** (-0.5)
     span_index = lax.axis_index("span")
-    first_head = lax.axis_index("mp") * head_count
+    trio = lax.axis_size("mp_lo")
+    first_head = (lax.axis_index("mp_hi") * trio + lax.axis_index("mp_lo")) * head_count
     first_kv = jnp.minimum(first_head // GROUP, kv_count - KV_SLOTS)
     kv_slot = (first_head + jnp.arange(head_count, dtype=jnp.int32)) // GROUP - first_kv
     kv_start = first_kv * HEAD_DIM
@@ -90,27 +91,36 @@
     attended = (
         jnp.transpose(attended, (1, 0, 2)).reshape(row_count, local_width).astype(jnp.bfloat16)
     )
-    mp_count = lax.axis_size("mp")
-    out_width = out_weight.shape[1] // mp_count
+    trios = lax.axis_size("mp_hi")
+    out_width = out_weight.shape[1] // (trios * trio)
     partial_sum = jnp.dot(attended, out_weight, preferred_element_type=jnp.float32)
     partial_sum = jnp.transpose(
-        partial_sum.astype(jnp.bfloat16).reshape(row_count, mp_count, out_width), (1, 0, 2)
+        partial_sum.astype(jnp.bfloat16).reshape(row_count, trios, trio, out_width), (2, 1, 0, 3)
     )
-    received = lax.all_to_all(partial_sum, "mp", 0, 0, tiled=True)
+    received = lax.all_to_all(partial_sum, "mp_lo", 0, 0, tiled=True)
+    partial_trio = jnp.sum(received.astype(jnp.float32), axis=0).astype(jnp.bfloat16)
+    received = lax.all_to_all(partial_trio, "mp_hi", 0, 0, tiled=True)
     projected = jnp.sum(received.astype(jnp.float32), axis=0)
     return projected.astype(jnp.bfloat16)[None]
 
 
 def solution(mesh):
+    shape = dict(mesh.shape)
+    trio = 3
+    split = jax.sharding.Mesh(
+        mesh.devices.reshape(shape["span"], shape["seq"], shape["mp"] // trio, trio),
+        ("span", "seq", "mp_hi", "mp_lo"),
+    )
+    mp = ("mp_hi", "mp_lo")
     in_specs = (
-        P("span", "seq", "mp"),
+        P("span", "seq", mp),
         P("span", "seq", None),
         P("span", "seq", None),
         P("seq"),
         P(),
-        P("mp", None),
+        P(mp, None),
     )
-    out_specs = P("span", "seq", "mp")
+    out_specs = P("span", "seq", mp)
     return jax.shard_map(
-        on_device, mesh=mesh, in_specs=in_specs, out_specs=out_specs, check_vma=False
+        on_device, mesh=split, in_specs=in_specs, out_specs=out_specs, check_vma=False
     )

time: 100 us -> 101 us (1.010)
    all_to_all x1 -> x2, blocking collectives: 47.7 us -> 47.3 us  [the longest x1 28.8 us: on_device(): received = lax.all_to_all(partial_trio, 'mp_hi', 0, 0, tiled=True)]
where the time goes in v9:
time: 101 us; the launch traced here: 100 us
  blocking collectives  47.3 us (47%)
  starting transfers between devices  25 us (25%)
  waiting for transfers between devices  11.8 us (12%)
  local copies, waits for them, and re-layouts  8.04 us (8%)
  other arithmetic  2.88 us (3%)
  matrix products  2.85 us (3%)
  between operations  2.28 us (2%)
    all_to_all x1, blocking collectives, on_device(): received = lax.all_to_all(partial_trio, 'mp_hi', 0, 0, tiled=True)  28.8 us
    all_to_all x1, blocking collectives, on_device(): received = lax.all_to_all(partial_sum, 'mp_lo', 0, 0, tiled=True)  18.6 us
    ppermute x3, starting transfers between devices, on_device(): held.append(lax.ppermute(outgoing, 'seq', pairs))  15.7 us
    ppermute x3, waiting for transfers between devices, on_device(): held.append(lax.ppermute(outgoing, 'seq', pairs))  10.6 us
    ppermute x2, starting transfers between devices, passed_along(): return lax.ppermute(x, axis, pairs)  7.43 us
  transfers between devices with their start and end apart: 6, of which 3 were waited for; matrix products, arithmetic and copies ran while one was open for 4% of the time, Pallas kernels for 0%

profile of v9, /device:TPU:64, one launch (start us, length us, event | category | flops | bytes accessed | tf_op | source)
XLA Modules:
  0.0 100.3 jit_solution(11581587658519936291)
XLA Ops:
  0.0 0.0 copy-start.1
  0.0 0.8 dynamic-slice_bitcast_fusion
  0.8 4.9 %collective-permute-start.1 = (bf16[64,512]{1,0:T(8,128)(2,1)S(1)}, bf16[64,512]{1,0:T(8,128)(2,1)S(1)}, u32[]{:S(2)}, u32[]{:S(2)}) collective-permute-start(bf16[64,512]{1,0:T(8,128)(2,1)S(1)} %pad_maximum_fusion.1), channel_id=1, source_target_pairs={{0,192},{96,288},{192,384},{288,480},{384,576},{480,672},{1,193},{... | collective-permute-start | bytes 196616 | tf_op jit(solution)/shard_map/ppermute | solution.py:16
  5.8 2.5 %collective-permute-start = (bf16[64,512]{1,0:T(8,128)(2,1)S(1)}, bf16[64,512]{1,0:T(8,128)(2,1)S(1)}, u32[]{:S(2)}, u32[]{:S(2)}) collective-permute-start(bf16[64,512]{1,0:T(8,128)(2,1)S(1)} %pad_maximum_fusion.1), channel_id=1, source_target_pairs={{0,96},{96,192},{192,288},{288,384},{384,480},{480,576},{576,672},... | collective-permute-start | bytes 196616 | tf_op jit(solution)/shard_map/ppermute | solution.py:16
  8.3 0.7 fusion.42
  8.9 0.0 collective-permute-done.1
  8.9 1.2 %collective-permute-done = bf16[64,512]{1,0:T(8,128)(2,1)S(1)} collective-permute-done((bf16[64,512]{1,0:T(8,128)(2,1)S(1)}, bf16[64,512]{1,0:T(8,128)(2,1)S(1)}, u32[]{:S(2)}, u32[]{:S(2)}) %collective-permute-start) | collective-permute-done | bytes 65568 | tf_op jit(solution)/shard_map/ppermute | solution.py:16
  10.2 7.7 %collective-permute-start.3 = (bf16[208,512]{1,0:T(8,128)(2,1)S(1)}, bf16[208,512]{1,0:T(8,128)(2,1)S(1)}, u32[]{:S(2)}, u32[]{:S(2)}) collective-permute-start(bf16[208,512]{1,0:T(8,128)(2,1)S(1)} %fusion.19), channel_id=1, source_target_pairs={{0,48},{12,60},{24,72},{36,84},{48,0},{60,12},{72,24},{84,36},{1,4... | collective-permute-start | bytes 638984 | tf_op jit(solution)/shard_map/ppermute | solution.py:51
  17.9 2.7 %collective-permute-start.2 = (bf16[208,512]{1,0:T(8,128)(2,1)S(1)}, bf16[208,512]{1,0:T(8,128)(2,1)S(1)}, u32[]{:S(2)}, u32[]{:S(2)}) collective-permute-start(bf16[208,512]{1,0:T(8,128)(2,1)S(1)} %fusion.19), channel_id=1, source_target_pairs={{0,24},{12,36},{24,48},{36,60},{48,72},{60,84},{72,0},{84,12},{1,2... | collective-permute-start | bytes 638984 | tf_op jit(solution)/shard_map/ppermute | solution.py:51
  20.6 5.3 %collective-permute-start.4 = (bf16[208,512]{1,0:T(8,128)(2,1)S(1)}, bf16[208,512]{1,0:T(8,128)(2,1)S(1)}, u32[]{:S(2)}, u32[]{:S(2)}) collective-permute-start(bf16[208,512]{1,0:T(8,128)(2,1)S(1)} %fusion.19), channel_id=1, source_target_pairs={{0,72},{12,84},{24,0},{36,12},{48,24},{60,36},{72,48},{84,60},{1,7... | collective-permute-start | bytes 638984 | tf_op jit(solution)/shard_map/ppermute | solution.py:51
  25.9 1.5 %fusion.41 = (s32[1,1]{1,0:T(1,128)}, s32[1,1]{1,0:T(1,128)}, s32[1,1]{1,0:T(1,128)}) fusion(s32[8,8]{1,0:T(8,128)} %param.12, s32[]{:T(128)S(6)} %select_n.75, s32[]{:T(128)S(6)} %max.30, s32[]{:T(128)S(6)} %max.34, s32[]{:T(128)S(6)} %max.32), kind=kLoop, calls=%fused_computation.76 | loop fusion | bytes 40 | tf_op jit(solution)/shard_map/jit(dynamic_index_in_dim)/dynamic_slice | solution.py:39
  29.4 0.0 collective-permute-done.3
  29.4 1.9 %collective-permute-done.2 = bf16[208,512]{1,0:T(8,128)(2,1)S(1)} collective-permute-done((bf16[208,512]{1,0:T(8,128)(2,1)S(1)}, bf16[208,512]{1,0:T(8,128)(2,1)S(1)}, u32[]{:S(2)}, u32[]{:S(2)}) %collective-permute-start.2) | collective-permute-done | bytes 213024 | tf_op jit(solution)/shard_map/ppermute | solution.py:51
  31.3 8.7 %collective-permute-done.4 = bf16[208,512]{1,0:T(8,128)(2,1)S(1)} collective-permute-done((bf16[208,512]{1,0:T(8,128)(2,1)S(1)}, bf16[208,512]{1,0:T(8,128)(2,1)S(1)}, u32[]{:S(2)}, u32[]{:S(2)}) %collective-permute-start.4) | collective-permute-done | bytes 213024 | tf_op jit(solution)/shard_map/ppermute | solution.py:51
  40.0 0.1 pad_maximum_fusion
  40.1 1.9 %collective-permute-start.5 = (bf16[4,208,512]{2,1,0:T(8,128)(2,1)S(1)}, bf16[4,208,512]{2,1,0:T(8,128)(2,1)S(1)}, u32[]{:S(2)}, u32[]{:S(2)}) collective-permute-start(bf16[4,208,512]{2,1,0:T(8,128)(2,1)S(1)} %pad_maximum_fusion), channel_id=1, source_target_pairs={{0,12},{12,0},{24,36},{36,24},{48,60},{60,48},{72,84},{84,72},{1,1... | collective-permute-start | bytes 2555912 | tf_op jit(solution)/shard_map/ppermute | solution.py:53
  42.0 0.1 add_compare_fusion
  42.1 0.1 and.59
  42.2 0.0 copy-done.1
  42.2 0.1 slice.80
  42.3 0.1 eq.56
  42.4 0.1 copy.85
  42.5 0.2 reshape.222
  42.7 1.3 %fusion.39 = (bf16[768,1,2,128]{3,2,1,0:T(2,128)(2,1)}, bf16[768,1,2,128]{3,2,1,0:T(2,128)(2,1)S(1)}) fusion(bf16[768,2,2,128]{3,2,1,0:T(2,128)(2,1)S(1)} %reshape.222), kind=kLoop, calls=%fused_computation.74 | loop fusion | bytes 1572864 | tf_op jit(solution)/shard_map/slice | solution.py:71
  44.0 0.4 convolution_bitcast_fusion.1
  44.3 0.0 collective-permute-done.5
  44.4 0.1 eq.59
  44.5 0.1 slice.89
  44.5 0.1 copy.44
  44.6 0.2 reshape.224
  44.8 0.5 fusion.40
  45.4 0.1 broadcast_compare_fusion.1
  45.5 0.1 and.62
  45.6 0.1 and.65
  45.7 0.0 slice-start
  45.7 0.4 convolution_bitcast_fusion
  46.1 0.1 broadcast_and_fusion.1
  46.1 0.0 copy-start
  46.1 0.4 fusion.38
  46.6 0.8 copy-done
  47.4 0.0 slice-start.1
  47.4 0.4 convolution_bitcast_fusion.3
  47.8 0.6 exponential_reduce_fusion.1
  48.4 0.4 convolution_bitcast_fusion.2
  48.8 0.0 slice-done
  48.8 0.3 slice-done.1
  49.1 1.3 %convolution_convert_fusion = bf16[64,6144]{1,0:T(8,128)(2,1)S(1)} fusion(bf16[512,6144]{1,0:T(8,128)(2,1)S(1)} %bitcast.170, f32[4,64]{1,0:T(4,128)S(1)} %get-tuple-element.21, f32[2,4,64,128]{3,2,1,0:T(8,128)S(1)} %convolution_bitcast_fusion.2, f32[4,64]{1,0:T(4,128)S(1)} %get-tuple-element.22, f32[2,4,64,128]{3,2,1,0:T(8,128)S(1)} %convolution_bitcast_fusion.3, ...), kind=kOutput, calls=%fused_computation | convolution fusion | flops 403243008 | bytes 7604228 | tf_op jit(solution)/shard_map/dot_general | solution.py:96
  50.4 1.2 %reshape.225 = bf16[64,4,3,512]{3,2,1,0:T(4,128)(2,1)S(1)} reshape(bf16[64,6144]{1,0:T(8,128)(2,1)S(1)} %convolution_convert_fusion) | data formatting | bytes 1572864 | tf_op jit(solution)/shard_map/reshape | solution.py:98
  51.5 0.6 copy.49
  52.1 18.6 %all_to_all.10 = bf16[3,4,64,512]{3,2,1,0:T(8,128)(2,1)S(1)} all-to-all(bf16[3,4,64,512]{3,2,1,0:T(8,128)(2,1)S(1)} %copy.49), channel_id=1, replica_groups=mesh['span'=8,'seq'=8,'mp_hi'=4,'mp_lo'=3] {'mp_lo'}, dimensions={0} | all-to-all | bytes 1572864 | tf_op jit(solution)/shard_map/all_to_all | solution.py:100
  70.7 0.1 reduce_sum.44
  70.8 28.8 %all_to_all.11 = bf16[4,64,512]{2,1,0:T(8,128)(2,1)S(1)} all-to-all(bf16[4,64,512]{2,1,0:T(8,128)(2,1)S(1)} %reduce_sum.44), channel_id=1, replica_groups=mesh['span'=8,'seq'=8,'mp_hi'=4,'mp_lo'=3] {'mp_hi'}, dimensions={0} | all-to-all | bytes 524288 | tf_op jit(solution)/shard_map/all_to_all | solution.py:102
  99.6 0.7 reduce_sum.45
  (13 shorter events, 0.2 us)
Async XLA Ops:
  0.0 42.2 %copy-start.1 = (bf16[1,64,512]{2,1,0:T(8,128)(2,1)S(1)}, bf16[1,64,512]{2,1,0:T(8,128)(2,1)}, u32[]{:S(2)}) copy-start(bf16[1,64,512]{2,1,0:T(8,128)(2,1)} %param.8) | copy-start | bytes 196612
  0.8 8.1 %collective-permute-start.1 = (bf16[64,512]{1,0:T(8,128)(2,1)S(1)}, bf16[64,512]{1,0:T(8,128)(2,1)S(1)}, u32[]{:S(2)}, u32[]{:S(2)}) collective-permute-start(bf16[64,512]{1,0:T(8,128)(2,1)S(1)} %pad_maximum_fusion.1), channel_id=1, source_target_pairs={{0,192},{96,288},{192,384},{288,480},{384,576},{480,672},{1,193},{... | collective-permute-start | bytes 196616 | tf_op jit(solution)/shard_map/ppermute | solution.py:16
  5.8 4.4 %collective-permute-start = (bf16[64,512]{1,0:T(8,128)(2,1)S(1)}, bf16[64,512]{1,0:T(8,128)(2,1)S(1)}, u32[]{:S(2)}, u32[]{:S(2)}) collective-permute-start(bf16[64,512]{1,0:T(8,128)(2,1)S(1)} %pad_maximum_fusion.1), channel_id=1, source_target_pairs={{0,96},{96,192},{192,288},{288,384},{384,480},{480,576},{576,672},... | collective-permute-start | bytes 196616 | tf_op jit(solution)/shard_map/ppermute | solution.py:16
  10.2 19.2 %collective-permute-start.3 = (bf16[208,512]{1,0:T(8,128)(2,1)S(1)}, bf16[208,512]{1,0:T(8,128)(2,1)S(1)}, u32[]{:S(2)}, u32[]{:S(2)}) collective-permute-start(bf16[208,512]{1,0:T(8,128)(2,1)S(1)} %fusion.19), channel_id=1, source_target_pairs={{0,48},{12,60},{24,72},{36,84},{48,0},{60,12},{72,24},{84,36},{1,4... | collective-permute-start | bytes 638984 | tf_op jit(solution)/shard_map/ppermute | solution.py:51
  17.9 13.4 %collective-permute-start.2 = (bf16[208,512]{1,0:T(8,128)(2,1)S(1)}, bf16[208,512]{1,0:T(8,128)(2,1)S(1)}, u32[]{:S(2)}, u32[]{:S(2)}) collective-permute-start(bf16[208,512]{1,0:T(8,128)(2,1)S(1)} %fusion.19), channel_id=1, source_target_pairs={{0,24},{12,36},{24,48},{36,60},{48,72},{60,84},{72,0},{84,12},{1,2... | collective-permute-start | bytes 638984 | tf_op jit(solution)/shard_map/ppermute | solution.py:51
  20.6 19.4 %collective-permute-start.4 = (bf16[208,512]{1,0:T(8,128)(2,1)S(1)}, bf16[208,512]{1,0:T(8,128)(2,1)S(1)}, u32[]{:S(2)}, u32[]{:S(2)}) collective-permute-start(bf16[208,512]{1,0:T(8,128)(2,1)S(1)} %fusion.19), channel_id=1, source_target_pairs={{0,72},{12,84},{24,0},{36,12},{48,24},{60,36},{72,48},{84,60},{1,7... | collective-permute-start | bytes 638984 | tf_op jit(solution)/shard_map/ppermute | solution.py:51
  40.1 4.3 %collective-permute-start.5 = (bf16[4,208,512]{2,1,0:T(8,128)(2,1)S(1)}, bf16[4,208,512]{2,1,0:T(8,128)(2,1)S(1)}, u32[]{:S(2)}, u32[]{:S(2)}) collective-permute-start(bf16[4,208,512]{2,1,0:T(8,128)(2,1)S(1)} %pad_maximum_fusion), channel_id=1, source_target_pairs={{0,12},{12,0},{24,36},{36,24},{48,60},{60,48},{72,84},{84,72},{1,1... | collective-permute-start | bytes 2555912 | tf_op jit(solution)/shard_map/ppermute | solution.py:53
  45.7 3.1 %slice-start = ((s8[6291456]{0:T(1024)(128)(4,1)}), s8[4194304]{0:T(1024)(128)(4,1)S(1)}, s32[]{:S(2)}) async-start(s8[6291456]{0:T(1024)(128)(4,1)} %bitcast.169), calls=%async_computation.2 | async-start | bytes 8388608
  46.1 1.2 %copy-start = (bf16[768,1,2,128]{3,2,1,0:T(2,128)(2,1)S(1)}, bf16[768,1,2,128]{3,2,1,0:T(2,128)(2,1)}, u32[]{:S(2)}) copy-start(bf16[768,1,2,128]{3,2,1,0:T(2,128)(2,1)} %get-tuple-element.23) | copy-start | bytes 1179652
  47.4 1.7 %slice-start.1 = ((s8[6291456]{0:T(1024)(128)(4,1)}), s8[2097152]{0:T(1024)(128)(4,1)S(1)}, s32[]{:S(2)}) async-start(s8[6291456]{0:T(1024)(128)(4,1)} %bitcast.169), calls=%async_computation.3 | async-start | bytes 4194304

commit v10 on v8

--- a/solution.py
+++ b/solution.py
@@ -80,6 +80,9 @@
     p = jnp.exp(s - first_top)
     first_total = jnp.sum(p, axis=2, keepdims=True)
     first_acc = weighted(p, value_all)
+    partner, first_top, first_total, first_acc = lax.optimization_barrier(
+        (partner, first_top, first_total, first_acc)
+    )
     s, value_all = piece_scores(partner)
     top = jnp.maximum(first_top, jnp.max(s, axis=2, keepdims=True))
     p = jnp.exp(s - top)

time: 100 us -> 105 us (1.050)
  the two profiles are of different devices: /device:TPU:64 before, /device:TPU:6 now
where the time goes in v10:
time: 105 us; the launch traced here: 103 us
  blocking collectives  47.7 us (45%)
  starting transfers between devices  25 us (24%)
  local copies, waits for them, and re-layouts  11.9 us (11%)
  waiting for transfers between devices  10.3 us (10%)
  other arithmetic  3.2 us (3%)
  matrix products  2.83 us (3%)
  between operations  2.31 us (2%)
    all_to_all x1, blocking collectives, on_device(): received = lax.all_to_all(partial_sum, 'mp', 0, 0, tiled=True)  47.7 us
    ppermute x3, starting transfers between devices, on_device(): held.append(lax.ppermute(outgoing, 'seq', pairs))  14.8 us
    ppermute x3, waiting for transfers between devices, on_device(): held.append(lax.ppermute(outgoing, 'seq', pairs))  10.3 us
    ppermute x2, starting transfers between devices, passed_along(): return lax.ppermute(x, axis, pairs)  8.33 us
    reshape x2, local copies, waits for them, and re-layouts, piece_scores(): jnp.transpose(kv_rows, (1, 0, 2, 3)).reshape(rows, 2, KV_SLOTS, HEAD_DIM)  2.4 us
  transfers between devices with their start and end apart: 6, of which 2 were waited for; matrix products, arithmetic and copies ran while one was open for 6% of the time, Pallas kernels for 0%

profile of v10, /device:TPU:6, one launch (start us, length us, event | category | flops | bytes accessed | tf_op | source)
XLA Modules:
  0.0 103.3 jit_solution(1435594866525179456)
XLA Ops:
  0.0 0.8 dynamic-slice_bitcast_fusion
  0.8 4.3 %collective-permute-start.1 = (bf16[64,512]{1,0:T(8,128)(2,1)S(1)}, bf16[64,512]{1,0:T(8,128)(2,1)S(1)}, u32[]{:S(2)}, u32[]{:S(2)}) collective-permute-start(bf16[64,512]{1,0:T(8,128)(2,1)S(1)} %pad_maximum_fusion.1), channel_id=1, source_target_pairs={{0,192},{96,288},{192,384},{288,480},{384,576},{480,672},{1,193},{... | collective-permute-start | bytes 196616 | tf_op jit(solution)/shard_map/ppermute | solution.py:16
  5.1 4.0 %collective-permute-start = (bf16[64,512]{1,0:T(8,128)(2,1)S(1)}, bf16[64,512]{1,0:T(8,128)(2,1)S(1)}, u32[]{:S(2)}, u32[]{:S(2)}) collective-permute-start(bf16[64,512]{1,0:T(8,128)(2,1)S(1)} %pad_maximum_fusion.1), channel_id=1, source_target_pairs={{0,96},{96,192},{192,288},{288,384},{384,480},{480,576},{576,672},... | collective-permute-start | bytes 196616 | tf_op jit(solution)/shard_map/ppermute | solution.py:16
  9.2 0.7 fusion.44
  9.8 1.5 %fusion.43 = (s32[1,1]{1,0:T(1,128)}, s32[1,1]{1,0:T(1,128)}, s32[1,1]{1,0:T(1,128)}) fusion(s32[8,8]{1,0:T(8,128)} %param.12, s32[]{:T(128)S(6)} %select_n.74, s32[]{:T(128)S(6)} %max.19, s32[]{:T(128)S(6)} %max.23, s32[]{:T(128)S(6)} %max.21), kind=kLoop, calls=%fused_computation.79 | loop fusion | bytes 40 | tf_op jit(solution)/shard_map/jit(dynamic_index_in_dim)/dynamic_slice | solution.py:38
  13.3 0.1 add_compare_fusion
  13.3 0.1 and.57
  13.4 0.9 reshape_squeeze.3
  14.3 0.0 collective-permute-done.1
  14.3 0.0 collective-permute-done
  14.3 6.8 %collective-permute-start.3 = (bf16[208,512]{1,0:T(8,128)(2,1)S(1)}, bf16[208,512]{1,0:T(8,128)(2,1)S(1)}, u32[]{:S(2)}, u32[]{:S(2)}) collective-permute-start(bf16[208,512]{1,0:T(8,128)(2,1)S(1)} %fusion.19), channel_id=1, source_target_pairs={{0,48},{12,60},{24,72},{36,84},{48,0},{60,12},{72,24},{84,36},{1,4... | collective-permute-start | bytes 638984 | tf_op jit(solution)/shard_map/ppermute | solution.py:50
  21.2 2.7 %collective-permute-start.2 = (bf16[208,512]{1,0:T(8,128)(2,1)S(1)}, bf16[208,512]{1,0:T(8,128)(2,1)S(1)}, u32[]{:S(2)}, u32[]{:S(2)}) collective-permute-start(bf16[208,512]{1,0:T(8,128)(2,1)S(1)} %fusion.19), channel_id=1, source_target_pairs={{0,24},{12,36},{24,48},{36,60},{48,72},{60,84},{72,0},{84,12},{1,2... | collective-permute-start | bytes 638984 | tf_op jit(solution)/shard_map/ppermute | solution.py:50
  23.9 5.3 %collective-permute-start.4 = (bf16[208,512]{1,0:T(8,128)(2,1)S(1)}, bf16[208,512]{1,0:T(8,128)(2,1)S(1)}, u32[]{:S(2)}, u32[]{:S(2)}) collective-permute-start(bf16[208,512]{1,0:T(8,128)(2,1)S(1)} %fusion.19), channel_id=1, source_target_pairs={{0,72},{12,84},{24,0},{36,12},{48,24},{60,36},{72,48},{84,60},{1,7... | collective-permute-start | bytes 638984 | tf_op jit(solution)/shard_map/ppermute | solution.py:50
  29.2 6.8 %collective-permute-done.3 = bf16[208,512]{1,0:T(8,128)(2,1)S(1)} collective-permute-done((bf16[208,512]{1,0:T(8,128)(2,1)S(1)}, bf16[208,512]{1,0:T(8,128)(2,1)S(1)}, u32[]{:S(2)}, u32[]{:S(2)}) %collective-permute-start.3) | collective-permute-done | bytes 213024 | tf_op jit(solution)/shard_map/ppermute | solution.py:50
  36.0 3.5 %collective-permute-done.2 = bf16[208,512]{1,0:T(8,128)(2,1)S(1)} collective-permute-done((bf16[208,512]{1,0:T(8,128)(2,1)S(1)}, bf16[208,512]{1,0:T(8,128)(2,1)S(1)}, u32[]{:S(2)}, u32[]{:S(2)}) %collective-permute-start.2) | collective-permute-done | bytes 213024 | tf_op jit(solution)/shard_map/ppermute | solution.py:50
  39.5 0.0 collective-permute-done.4
  39.5 0.1 pad_maximum_fusion
  39.7 0.1 slice.81
  39.7 1.9 %collective-permute-start.5 = (bf16[4,208,512]{2,1,0:T(8,128)(2,1)S(1)}, bf16[4,208,512]{2,1,0:T(8,128)(2,1)S(1)}, u32[]{:S(2)}, u32[]{:S(2)}) collective-permute-start(bf16[4,208,512]{2,1,0:T(8,128)(2,1)S(1)} %pad_maximum_fusion), channel_id=1, source_target_pairs={{0,12},{12,0},{24,36},{36,24},{48,60},{60,48},{72,84},{84,72},{1,1... | collective-permute-start | bytes 2555912 | tf_op jit(solution)/shard_map/ppermute | solution.py:52
  41.7 0.1 eq.55
  41.7 0.1 broadcast_compare_fusion.1
  41.8 0.1 and.60
  41.9 0.1 copy.71
  42.0 0.2 reshape.196
  42.2 0.5 fusion.42
  42.7 0.4 convolution_bitcast_fusion.1
  43.2 0.3 fusion.39
  43.4 0.3 exponential_reduce_fusion.1
  43.8 0.4 convolution_bitcast_fusion.3
  44.2 0.1 fusion.23
  44.3 0.0 collective-permute-done.5
  44.3 0.0 copy-start
  44.3 0.9 copy-done
  45.2 1.2 %slice.73 = bf16[4,192,512]{2,1,0:T(8,128)(2,1)S(1)} slice(bf16[4,208,512]{2,1,0:T(8,128)(2,1)} %copy-done), slice={[0:4], [0:192], [0:512]} | slice | bytes 1572864 | tf_op jit(solution)/shard_map/slice | solution.py:60
  46.4 0.1 eq.59
  46.5 0.0 slice-start
  46.5 1.0 copy.33
  47.5 2.2 %reshape.198 = bf16[768,2,2,128]{3,2,1,0:T(2,128)(2,1)S(1)} reshape(bf16[3,4,64,512]{3,2,1,0:T(8,128)(2,1)} %copy.33) | data formatting | bytes 1572864 | tf_op jit(solution)/shard_map/reshape | solution.py:63
  49.7 0.5 fusion.41
  50.2 0.1 broadcast_compare_fusion
  50.3 0.1 and.64
  50.5 0.0 slice-start.1
  50.5 0.4 convolution_bitcast_fusion
  50.9 0.3 fusion.40
  51.1 0.3 exponential_reduce_fusion
  51.5 0.4 convolution_bitcast_fusion.2
  51.9 0.0 slice-done
  51.9 0.7 slice-done.1
  52.7 1.3 %convolution_convert_fusion = bf16[64,6144]{1,0:T(8,128)(2,1)S(1)} fusion(bf16[512,6144]{1,0:T(8,128)(2,1)S(1)} %bitcast.176, f32[4,64]{1,0:T(4,128)S(1)} %get-tuple-element.30, f32[2,4,64,128]{3,2,1,0:T(8,128)S(1)} %convolution_bitcast_fusion.2, pred[4]{0:T(512)(128)(4,1)S(1)} %subtract_compare_fusion, f32[4,64,128]{2,1,0:T(8,128)S(1)} %fusion.23, ...), kind=kOutput, calls=%fused_computation | convolution fusion | flops 403210240 | bytes 7473156 | tf_op jit(solution)/shard_map/dot_general | solution.py:98
  53.9 0.5 reshape.199
  54.5 0.4 copy.38
  54.9 47.7 %all_to_all.5 = bf16[12,64,512]{2,1,0:T(8,128)(2,1)S(1)} all-to-all(bf16[12,64,512]{2,1,0:T(8,128)(2,1)S(1)} %copy.38), channel_id=1, replica_groups=mesh['span'=8,'seq'=8,'mp'=12] {'mp'}, dimensions={0} | all-to-all | bytes 1572864 | tf_op jit(solution)/shard_map/all_to_all | solution.py:102
  102.6 0.7 reduce_sum.32
  (14 shorter events, 0.3 us)
Async XLA Ops:
  0.8 13.5 %collective-permute-start.1 = (bf16[64,512]{1,0:T(8,128)(2,1)S(1)}, bf16[64,512]{1,0:T(8,128)(2,1)S(1)}, u32[]{:S(2)}, u32[]{:S(2)}) collective-permute-start(bf16[64,512]{1,0:T(8,128)(2,1)S(1)} %pad_maximum_fusion.1), channel_id=1, source_target_pairs={{0,192},{96,288},{192,384},{288,480},{384,576},{480,672},{1,193},{... | collective-permute-start | bytes 196616 | tf_op jit(solution)/shard_map/ppermute | solution.py:16
  5.1 9.2 %collective-permute-start = (bf16[64,512]{1,0:T(8,128)(2,1)S(1)}, bf16[64,512]{1,0:T(8,128)(2,1)S(1)}, u32[]{:S(2)}, u32[]{:S(2)}) collective-permute-start(bf16[64,512]{1,0:T(8,128)(2,1)S(1)} %pad_maximum_fusion.1), channel_id=1, source_target_pairs={{0,96},{96,192},{192,288},{288,384},{384,480},{480,576},{576,672},... | collective-permute-start | bytes 196616 | tf_op jit(solution)/shard_map/ppermute | solution.py:16
  14.3 21.7 %collective-permute-start.3 = (bf16[208,512]{1,0:T(8,128)(2,1)S(1)}, bf16[208,512]{1,0:T(8,128)(2,1)S(1)}, u32[]{:S(2)}, u32[]{:S(2)}) collective-permute-start(bf16[208,512]{1,0:T(8,128)(2,1)S(1)} %fusion.19), channel_id=1, source_target_pairs={{0,48},{12,60},{24,72},{36,84},{48,0},{60,12},{72,24},{84,36},{1,4... | collective-permute-start | bytes 638984 | tf_op jit(solution)/shard_map/ppermute | solution.py:50
  21.2 18.3 %collective-permute-start.2 = (bf16[208,512]{1,0:T(8,128)(2,1)S(1)}, bf16[208,512]{1,0:T(8,128)(2,1)S(1)}, u32[]{:S(2)}, u32[]{:S(2)}) collective-permute-start(bf16[208,512]{1,0:T(8,128)(2,1)S(1)} %fusion.19), channel_id=1, source_target_pairs={{0,24},{12,36},{24,48},{36,60},{48,72},{60,84},{72,0},{84,12},{1,2... | collective-permute-start | bytes 638984 | tf_op jit(solution)/shard_map/ppermute | solution.py:50
  23.9 15.6 %collective-permute-start.4 = (bf16[208,512]{1,0:T(8,128)(2,1)S(1)}, bf16[208,512]{1,0:T(8,128)(2,1)S(1)}, u32[]{:S(2)}, u32[]{:S(2)}) collective-permute-start(bf16[208,512]{1,0:T(8,128)(2,1)S(1)} %fusion.19), channel_id=1, source_target_pairs={{0,72},{12,84},{24,0},{36,12},{48,24},{60,36},{72,48},{84,60},{1,7... | collective-permute-start | bytes 638984 | tf_op jit(solution)/shard_map/ppermute | solution.py:50
  39.7 4.6 %collective-permute-start.5 = (bf16[4,208,512]{2,1,0:T(8,128)(2,1)S(1)}, bf16[4,208,512]{2,1,0:T(8,128)(2,1)S(1)}, u32[]{:S(2)}, u32[]{:S(2)}) collective-permute-start(bf16[4,208,512]{2,1,0:T(8,128)(2,1)S(1)} %pad_maximum_fusion), channel_id=1, source_target_pairs={{0,12},{12,0},{24,36},{36,24},{48,60},{60,48},{72,84},{84,72},{1,1... | collective-permute-start | bytes 2555912 | tf_op jit(solution)/shard_map/ppermute | solution.py:52
  44.3 0.9 copy-start
  46.5 5.4 %slice-start = ((s8[6291456]{0:T(1024)(128)(4,1)}), s8[2097152]{0:T(1024)(128)(4,1)S(1)}, s32[]{:S(2)}) async-start(s8[6291456]{0:T(1024)(128)(4,1)} %bitcast.175), calls=%async_computation.1 | async-start | bytes 4194304
  50.5 2.2 %slice-start.1 = ((s8[6291456]{0:T(1024)(128)(4,1)}), s8[4194304]{0:T(1024)(128)(4,1)S(1)}, s32[]{:S(2)}) async-start(s8[6291456]{0:T(1024)(128)(4,1)} %bitcast.175), calls=%async_computation.2 | async-start | bytes 8388608

commit v11 on v8

--- a/solution.py
+++ b/solution.py
@@ -92,12 +92,12 @@
     )
     mp_count = lax.axis_size("mp")
     out_width = out_weight.shape[1] // mp_count
-    partial_sum = jnp.dot(attended, out_weight, preferred_element_type=jnp.float32)
-    partial_sum = jnp.transpose(
-        partial_sum.astype(jnp.bfloat16).reshape(row_count, mp_count, out_width), (1, 0, 2)
-    )
-    received = lax.all_to_all(partial_sum, "mp", 0, 0, tiled=True)
-    projected = jnp.sum(received.astype(jnp.float32), axis=0)
+    weight_parts = out_weight.reshape(local_width, mp_count, out_width)
+    partial_sum = jnp.einsum(
+        "qi,icj->qcj", attended, weight_parts, preferred_element_type=jnp.float32
+    ).astype(jnp.bfloat16)
+    received = lax.all_to_all(partial_sum, "mp", 1, 1, tiled=True)
+    projected = jnp.sum(received.astype(jnp.float32), axis=1)
     return projected.astype(jnp.bfloat16)[None]
 
 

time: 100 us -> 111 us (1.11)
  local copies, waits for them, and re-layouts: 7.22 us -> 14.6 us
  matrix products: 2.85 us -> 6.37 us
    unnamed x10 -> x7, local copies, waits for them, and re-layouts: 1.12 us -> 9.31 us
    dot_general x1, matrix products: 1.26 us -> 4.79 us  [on_device(): jnp.einsum('qi,icj->qcj', attended, weight_parts, preferred_element_type=...]
  transfers between devices with their start and end apart: 6 -> 6, of which waited for: 3 -> 3; matrix products, arithmetic and copies ran while one was open for 4% -> 12% of each run, Pallas kernels for 0% -> 0%
where the time goes in v11:
time: 111 us
  blocking collectives  47.7 us (43%)
  starting transfers between devices  25 us (23%)
  local copies, waits for them, and re-layouts  14.6 us (13%)
  waiting for transfers between devices  11.8 us (11%)
  matrix products  6.37 us (6%)
  other arithmetic  2.96 us (3%)
  between operations  2.26 us (2%)
    all_to_all x1, blocking collectives, on_device(): received = lax.all_to_all(partial_sum, 'mp', 1, 1, tiled=True)  47.7 us
    ppermute x3, starting transfers between devices, on_device(): held.append(lax.ppermute(outgoing, 'seq', pairs))  15.7 us
    ppermute x3, waiting for transfers between devices, on_device(): held.append(lax.ppermute(outgoing, 'seq', pairs))  10.6 us
    unnamed x7, local copies, waits for them, and re-layouts  9.31 us
    ppermute x2, starting transfers between devices, passed_along(): return lax.ppermute(x, axis, pairs)  7.43 us
    dot_general x1, matrix products, on_device(): jnp.einsum('qi,icj->qcj', attended, weight_parts, preferred_element_type=...  4.79 us
  transfers between devices with their start and end apart: 6, of which 3 were waited for; matrix products, arithmetic and copies ran while one was open for 12% of the time, Pallas kernels for 0%

profile of v11, /device:TPU:64, one launch (start us, length us, event | category | flops | bytes accessed | tf_op | source)
XLA Modules:
  0.0 110.8 jit_solution(17919151175081991041)
XLA Ops:
  0.0 0.0 copy-start.1
  0.0 0.8 dynamic-slice_bitcast_fusion
  0.8 4.9 %collective-permute-start.1 = (bf16[64,512]{1,0:T(8,128)(2,1)S(1)}, bf16[64,512]{1,0:T(8,128)(2,1)S(1)}, u32[]{:S(2)}, u32[]{:S(2)}) collective-permute-start(bf16[64,512]{1,0:T(8,128)(2,1)S(1)} %pad_maximum_fusion.1), channel_id=1, source_target_pairs={{0,192},{96,288},{192,384},{288,480},{384,576},{480,672},{1,193},{... | collective-permute-start | bytes 196616 | tf_op jit(solution)/shard_map/ppermute | solution.py:16
  5.8 2.5 %collective-permute-start = (bf16[64,512]{1,0:T(8,128)(2,1)S(1)}, bf16[64,512]{1,0:T(8,128)(2,1)S(1)}, u32[]{:S(2)}, u32[]{:S(2)}) collective-permute-start(bf16[64,512]{1,0:T(8,128)(2,1)S(1)} %pad_maximum_fusion.1), channel_id=1, source_target_pairs={{0,96},{96,192},{192,288},{288,384},{384,480},{480,576},{576,672},... | collective-permute-start | bytes 196616 | tf_op jit(solution)/shard_map/ppermute | solution.py:16
  8.3 0.7 fusion.40
  8.9 0.0 collective-permute-done.1
  8.9 1.2 %collective-permute-done = bf16[64,512]{1,0:T(8,128)(2,1)S(1)} collective-permute-done((bf16[64,512]{1,0:T(8,128)(2,1)S(1)}, bf16[64,512]{1,0:T(8,128)(2,1)S(1)}, u32[]{:S(2)}, u32[]{:S(2)}) %collective-permute-start) | collective-permute-done | bytes 65568 | tf_op jit(solution)/shard_map/ppermute | solution.py:16
  10.2 7.7 %collective-permute-start.3 = (bf16[208,512]{1,0:T(8,128)(2,1)S(1)}, bf16[208,512]{1,0:T(8,128)(2,1)S(1)}, u32[]{:S(2)}, u32[]{:S(2)}) collective-permute-start(bf16[208,512]{1,0:T(8,128)(2,1)S(1)} %fusion.19), channel_id=1, source_target_pairs={{0,48},{12,60},{24,72},{36,84},{48,0},{60,12},{72,24},{84,36},{1,4... | collective-permute-start | bytes 638984 | tf_op jit(solution)/shard_map/ppermute | solution.py:50
  17.9 2.7 %collective-permute-start.2 = (bf16[208,512]{1,0:T(8,128)(2,1)S(1)}, bf16[208,512]{1,0:T(8,128)(2,1)S(1)}, u32[]{:S(2)}, u32[]{:S(2)}) collective-permute-start(bf16[208,512]{1,0:T(8,128)(2,1)S(1)} %fusion.19), channel_id=1, source_target_pairs={{0,24},{12,36},{24,48},{36,60},{48,72},{60,84},{72,0},{84,12},{1,2... | collective-permute-start | bytes 638984 | tf_op jit(solution)/shard_map/ppermute | solution.py:50
  20.6 5.3 %collective-permute-start.4 = (bf16[208,512]{1,0:T(8,128)(2,1)S(1)}, bf16[208,512]{1,0:T(8,128)(2,1)S(1)}, u32[]{:S(2)}, u32[]{:S(2)}) collective-permute-start(bf16[208,512]{1,0:T(8,128)(2,1)S(1)} %fusion.19), channel_id=1, source_target_pairs={{0,72},{12,84},{24,0},{36,12},{48,24},{60,36},{72,48},{84,60},{1,7... | collective-permute-start | bytes 638984 | tf_op jit(solution)/shard_map/ppermute | solution.py:50
  25.9 1.5 %fusion.39 = (s32[1,1]{1,0:T(1,128)}, s32[1,1]{1,0:T(1,128)}, s32[1,1]{1,0:T(1,128)}) fusion(s32[8,8]{1,0:T(8,128)} %param.12, s32[]{:T(128)S(6)} %select_n.75, s32[]{:T(128)S(6)} %max.30, s32[]{:T(128)S(6)} %max.34, s32[]{:T(128)S(6)} %max.32), kind=kLoop, calls=%fused_computation.74 | loop fusion | bytes 40 | tf_op jit(solution)/shard_map/jit(dynamic_index_in_dim)/dynamic_slice | solution.py:38
  29.4 0.0 collective-permute-done.3
  29.4 1.9 %collective-permute-done.2 = bf16[208,512]{1,0:T(8,128)(2,1)S(1)} collective-permute-done((bf16[208,512]{1,0:T(8,128)(2,1)S(1)}, bf16[208,512]{1,0:T(8,128)(2,1)S(1)}, u32[]{:S(2)}, u32[]{:S(2)}) %collective-permute-start.2) | collective-permute-done | bytes 213024 | tf_op jit(solution)/shard_map/ppermute | solution.py:50
  31.3 8.7 %collective-permute-done.4 = bf16[208,512]{1,0:T(8,128)(2,1)S(1)} collective-permute-done((bf16[208,512]{1,0:T(8,128)(2,1)S(1)}, bf16[208,512]{1,0:T(8,128)(2,1)S(1)}, u32[]{:S(2)}, u32[]{:S(2)}) %collective-permute-start.4) | collective-permute-done | bytes 213024 | tf_op jit(solution)/shard_map/ppermute | solution.py:50
  40.0 0.1 pad_maximum_fusion
  40.1 1.9 %collective-permute-start.5 = (bf16[4,208,512]{2,1,0:T(8,128)(2,1)S(1)}, bf16[4,208,512]{2,1,0:T(8,128)(2,1)S(1)}, u32[]{:S(2)}, u32[]{:S(2)}) collective-permute-start(bf16[4,208,512]{2,1,0:T(8,128)(2,1)S(1)} %pad_maximum_fusion), channel_id=1, source_target_pairs={{0,12},{12,0},{24,36},{36,24},{48,60},{60,48},{72,84},{84,72},{1,1... | collective-permute-start | bytes 2555912 | tf_op jit(solution)/shard_map/ppermute | solution.py:52
  42.0 0.1 add_compare_fusion
  42.1 0.1 and.58
  42.2 0.0 copy-done.1
  42.2 8.7 %copy.32 = bf16[512,6144]{0,1:T(8,128)(2,1)} copy(bf16[512,6144]{1,0:T(8,128)(2,1)} %param.13) | data formatting | bytes 12582912 | tf_op args[5]
  50.9 0.1 slice.80
  51.0 0.1 eq.56
  51.1 0.1 copy.62
  51.2 0.2 reshape.222
  51.4 1.3 %fusion.37 = (bf16[768,1,2,128]{3,2,1,0:T(2,128)(2,1)}, bf16[768,1,2,128]{3,2,1,0:T(2,128)(2,1)S(1)}) fusion(bf16[768,2,2,128]{3,2,1,0:T(2,128)(2,1)S(1)} %reshape.222), kind=kLoop, calls=%fused_computation.72 | loop fusion | bytes 1572864 | tf_op jit(solution)/shard_map/slice | solution.py:70
  52.7 0.4 convolution_bitcast_fusion.1
  53.0 0.0 collective-permute-done.5
  53.1 0.1 eq.59
  53.2 0.1 slice.89
  53.2 0.1 copy.27
  53.3 0.2 reshape.224
  53.5 0.5 fusion.38
  54.1 0.1 broadcast_compare_fusion.1
  54.2 0.1 and.61
  54.3 0.1 and.64
  54.4 0.4 convolution_bitcast_fusion
  54.8 0.1 broadcast_and_fusion.1
  54.8 0.0 copy-start
  54.8 0.4 fusion.36
  55.3 0.6 copy-done
  55.8 0.4 convolution_bitcast_fusion.3
  56.2 0.6 exponential_reduce_fusion.1
  56.8 0.4 convolution_bitcast_fusion.2
  57.3 0.1 fusion.28
  57.4 0.1 copy.31
  57.5 4.8 %convolution_convert_fusion = bf16[64,12,512]{2,0,1:T(8,128)(2,1)S(1)} fusion(bf16[64,512,1]{1,0,2:T(8,128)(2,1)S(1)} %reshape.234, bf16[512,12,512]{0,2,1:T(8,128)(2,1)} %bitcast.156), kind=kOutput, calls=%fused_computation.2 | convolution fusion | flops 403046400 | bytes 7143424 | tf_op jit(solution)/shard_map/qi,icj->qcj/dot_general | solution.py:96
  62.3 47.7 %all_to_all.5 = bf16[64,12,512]{2,0,1:T(8,128)(2,1)S(1)} all-to-all(bf16[64,12,512]{2,0,1:T(8,128)(2,1)S(1)} %convolution_convert_fusion), channel_id=1, replica_groups=mesh['span'=8,'seq'=8,'mp'=12] {'mp'}, dimensions={1} | all-to-all | bytes 1572864 | tf_op jit(solution)/shard_map/all_to_all | solution.py:99
  110.0 0.7 reduce_sum.32
  (13 shorter events, 0.2 us)
Async XLA Ops:
  0.0 42.2 %copy-start.1 = (bf16[1,64,512]{2,1,0:T(8,128)(2,1)S(1)}, bf16[1,64,512]{2,1,0:T(8,128)(2,1)}, u32[]{:S(2)}) copy-start(bf16[1,64,512]{2,1,0:T(8,128)(2,1)} %param.8) | copy-start | bytes 196612
  0.8 8.1 %collective-permute-start.1 = (bf16[64,512]{1,0:T(8,128)(2,1)S(1)}, bf16[64,512]{1,0:T(8,128)(2,1)S(1)}, u32[]{:S(2)}, u32[]{:S(2)}) collective-permute-start(bf16[64,512]{1,0:T(8,128)(2,1)S(1)} %pad_maximum_fusion.1), channel_id=1, source_target_pairs={{0,192},{96,288},{192,384},{288,480},{384,576},{480,672},{1,193},{... | collective-permute-start | bytes 196616 | tf_op jit(solution)/shard_map/ppermute | solution.py:16
  5.8 4.4 %collective-permute-start = (bf16[64,512]{1,0:T(8,128)(2,1)S(1)}, bf16[64,512]{1,0:T(8,128)(2,1)S(1)}, u32[]{:S(2)}, u32[]{:S(2)}) collective-permute-start(bf16[64,512]{1,0:T(8,128)(2,1)S(1)} %pad_maximum_fusion.1), channel_id=1, source_target_pairs={{0,96},{96,192},{192,288},{288,384},{384,480},{480,576},{576,672},... | collective-permute-start | bytes 196616 | tf_op jit(solution)/shard_map/ppermute | solution.py:16
  10.2 19.2 %collective-permute-start.3 = (bf16[208,512]{1,0:T(8,128)(2,1)S(1)}, bf16[208,512]{1,0:T(8,128)(2,1)S(1)}, u32[]{:S(2)}, u32[]{:S(2)}) collective-permute-start(bf16[208,512]{1,0:T(8,128)(2,1)S(1)} %fusion.19), channel_id=1, source_target_pairs={{0,48},{12,60},{24,72},{36,84},{48,0},{60,12},{72,24},{84,36},{1,4... | collective-permute-start | bytes 638984 | tf_op jit(solution)/shard_map/ppermute | solution.py:50
  17.9 13.4 %collective-permute-start.2 = (bf16[208,512]{1,0:T(8,128)(2,1)S(1)}, bf16[208,512]{1,0:T(8,128)(2,1)S(1)}, u32[]{:S(2)}, u32[]{:S(2)}) collective-permute-start(bf16[208,512]{1,0:T(8,128)(2,1)S(1)} %fusion.19), channel_id=1, source_target_pairs={{0,24},{12,36},{24,48},{36,60},{48,72},{60,84},{72,0},{84,12},{1,2... | collective-permute-start | bytes 638984 | tf_op jit(solution)/shard_map/ppermute | solution.py:50
  20.6 19.4 %collective-permute-start.4 = (bf16[208,512]{1,0:T(8,128)(2,1)S(1)}, bf16[208,512]{1,0:T(8,128)(2,1)S(1)}, u32[]{:S(2)}, u32[]{:S(2)}) collective-permute-start(bf16[208,512]{1,0:T(8,128)(2,1)S(1)} %fusion.19), channel_id=1, source_target_pairs={{0,72},{12,84},{24,0},{36,12},{48,24},{60,36},{72,48},{84,60},{1,7... | collective-permute-start | bytes 638984 | tf_op jit(solution)/shard_map/ppermute | solution.py:50
  40.1 13.0 %collective-permute-start.5 = (bf16[4,208,512]{2,1,0:T(8,128)(2,1)S(1)}, bf16[4,208,512]{2,1,0:T(8,128)(2,1)S(1)}, u32[]{:S(2)}, u32[]{:S(2)}) collective-permute-start(bf16[4,208,512]{2,1,0:T(8,128)(2,1)S(1)} %pad_maximum_fusion), channel_id=1, source_target_pairs={{0,12},{12,0},{24,36},{36,24},{48,60},{60,48},{72,84},{84,72},{1,1... | collective-permute-start | bytes 2555912 | tf_op jit(solution)/shard_map/ppermute | solution.py:52
  54.8 1.0 copy-start

commit v12 on v8

--- a/solution.py
+++ b/solution.py
@@ -37,18 +37,19 @@
         earlier = span_index - j
         entry = lax.dynamic_index_in_dim(mask_row, jnp.maximum(earlier, 0), 0, keepdims=False)
         visible.append(jnp.where(earlier >= 0, entry, 0))
-    stacked = [packed]
-    for j in range(1, WINDOW):
-        stacked.append(passed_along(packed, "span", j))
     clip_row = jnp.zeros((CLIP_PAD, packed.shape[1]), jnp.bfloat16)
     clip_row = clip_row.at[0, :row_count].set(clip_ids.astype(jnp.bfloat16))
-    outgoing = jnp.concatenate(stacked + [clip_row], axis=0)
+    own_block = jnp.concatenate([packed, clip_row], axis=0)
+    shifted = jnp.concatenate([passed_along(packed, "span", j) for j in range(1, WINDOW)], axis=0)
     seq_count = lax.axis_size("seq")
-    held = [outgoing]
-    for shift in range(2, seq_count, 2):
-        pairs = [(i, (i + shift) % seq_count) for i in range(seq_count)]
-        held.append(lax.ppermute(outgoing, "seq", pairs))
-    held = jnp.stack(held, axis=0)
+    def same_core(block):
+        held = [block]
+        for shift in range(2, seq_count, 2):
+            pairs = [(i, (i + shift) % seq_count) for i in range(seq_count)]
+            held.append(lax.ppermute(block, "seq", pairs))
+        return jnp.stack(held, axis=0)
+
+    held = jnp.concatenate([same_core(own_block), same_core(shifted)], axis=1)
     partner = lax.ppermute(held, "seq", [(i, i ^ 1) for i in range(seq_count)])
     query_heads = queries[0].reshape(row_count, head_count, HEAD_DIM)
     pick = kv_slot[:, None, None] == 0
@@ -57,8 +58,10 @@
 
     def piece_scores(piece):
         blocks = piece.shape[0]
-        kv_rows = piece[:, : WINDOW * row_count].reshape(blocks, WINDOW, row_count, -1)
-        key_clips = piece[:, WINDOW * row_count, :row_count].reshape(-1)
+        own_rows = piece[:, None, :row_count]
+        later_rows = piece[:, row_count + CLIP_PAD :].reshape(blocks, WINDOW - 1, row_count, -1)
+        kv_rows = jnp.concatenate([own_rows, later_rows], axis=1)
+        key_clips = piece[:, row_count, :row_count].reshape(-1)
         rows = WINDOW * blocks * row_count
         kv = jnp.transpose(kv_rows, (1, 0, 2, 3)).reshape(rows, 2, KV_SLOTS, HEAD_DIM)
         s_both = jnp.einsum(

time: 100 us -> 109 us (1.090)
  the two profiles are of different devices: /device:TPU:64 before, /device:TPU:6 now
where the time goes in v12:
time: 109 us; the launch traced here: 107 us
  blocking collectives  47.6 us (44%)
  starting transfers between devices  34.1 us (31%)
  waiting for transfers between devices  9.06 us (8%)
  local copies, waits for them, and re-layouts  7.88 us (7%)
  other arithmetic  3.01 us (3%)
  matrix products  2.84 us (3%)
  between operations  2.35 us (2%)
    all_to_all x1, blocking collectives, on_device(): received = lax.all_to_all(partial_sum, 'mp', 0, 0, tiled=True)  47.6 us
    ppermute x6, starting transfers between devices, same_core(): held.append(lax.ppermute(block, 'seq', pairs))  24.4 us
    ppermute x6, waiting for transfers between devices, same_core(): held.append(lax.ppermute(block, 'seq', pairs))  8.7 us
    ppermute x2, starting transfers between devices, passed_along(): return lax.ppermute(x, axis, pairs)  7.73 us
  transfers between devices with their start and end apart: 9, of which 3 were waited for; matrix products, arithmetic and copies ran while one was open for 5% of the time, Pallas kernels for 0%

profile of v12, /device:TPU:6, one launch (start us, length us, event | category | flops | bytes accessed | tf_op | source)
XLA Modules:
  0.0 106.8 jit_solution(17723538023821253302)
XLA Ops:
  0.0 0.8 dynamic-slice_bitcast_fusion
  0.8 3.4 %collective-permute-start.3 = (bf16[64,512]{1,0:T(8,128)(2,1)S(1)}, bf16[64,512]{1,0:T(8,128)(2,1)S(1)}, u32[]{:S(2)}, u32[]{:S(2)}) collective-permute-start(bf16[64,512]{1,0:T(8,128)(2,1)S(1)} %pad_maximum_fusion.1), channel_id=1, source_target_pairs={{0,96},{96,192},{192,288},{288,384},{384,480},{480,576},{576,672},... | collective-permute-start | bytes 196616 | tf_op jit(solution)/shard_map/ppermute | solution.py:16
  4.2 4.3 %collective-permute-start.4 = (bf16[64,512]{1,0:T(8,128)(2,1)S(1)}, bf16[64,512]{1,0:T(8,128)(2,1)S(1)}, u32[]{:S(2)}, u32[]{:S(2)}) collective-permute-start(bf16[64,512]{1,0:T(8,128)(2,1)S(1)} %pad_maximum_fusion.1), channel_id=1, source_target_pairs={{0,192},{96,288},{192,384},{288,480},{384,576},{480,672},{1,193},{... | collective-permute-start | bytes 196616 | tf_op jit(solution)/shard_map/ppermute | solution.py:16
  8.5 0.7 fusion.43
  9.2 6.8 %collective-permute-start.1 = (bf16[80,512]{1,0:T(8,128)(2,1)S(1)}, bf16[80,512]{1,0:T(8,128)(2,1)S(1)}, u32[]{:S(2)}, u32[]{:S(2)}) collective-permute-start(bf16[80,512]{1,0:T(8,128)(2,1)S(1)} %get-tuple-element.28), channel_id=1, source_target_pairs={{0,48},{12,60},{24,72},{36,84},{48,0},{60,12},{72,24},{84,36},{1,4... | collective-permute-start | bytes 245768 | tf_op jit(solution)/shard_map/ppermute | solution.py:49
  16.1 2.7 %collective-permute-start = (bf16[80,512]{1,0:T(8,128)(2,1)S(1)}, bf16[80,512]{1,0:T(8,128)(2,1)S(1)}, u32[]{:S(2)}, u32[]{:S(2)}) collective-permute-start(bf16[80,512]{1,0:T(8,128)(2,1)S(1)} %get-tuple-element.28), channel_id=1, source_target_pairs={{0,24},{12,36},{24,48},{36,60},{48,72},{60,84},{72,0},{84,12},{1,2... | collective-permute-start | bytes 245768 | tf_op jit(solution)/shard_map/ppermute | solution.py:49
  18.8 5.3 %collective-permute-start.2 = (bf16[80,512]{1,0:T(8,128)(2,1)S(1)}, bf16[80,512]{1,0:T(8,128)(2,1)S(1)}, u32[]{:S(2)}, u32[]{:S(2)}) collective-permute-start(bf16[80,512]{1,0:T(8,128)(2,1)S(1)} %get-tuple-element.28), channel_id=1, source_target_pairs={{0,72},{12,84},{24,0},{36,12},{48,24},{60,36},{72,48},{84,60},{1,7... | collective-permute-start | bytes 245768 | tf_op jit(solution)/shard_map/ppermute | solution.py:49
  24.0 1.5 %fusion.42 = (s32[1,1]{1,0:T(1,128)}, s32[1,1]{1,0:T(1,128)}, s32[1,1]{1,0:T(1,128)}) fusion(s32[8,8]{1,0:T(8,128)} %param.12, s32[]{:T(128)S(6)} %select_n.75, s32[]{:T(128)S(6)} %max.30, s32[]{:T(128)S(6)} %max.34, s32[]{:T(128)S(6)} %max.32), kind=kLoop, calls=%fused_computation.83 | loop fusion | bytes 40 | tf_op jit(solution)/shard_map/jit(dynamic_index_in_dim)/dynamic_slice | solution.py:38
  27.5 0.0 collective-permute-done.3
  27.5 0.0 collective-permute-done.4
  27.6 1.9 %collective-permute-start.7 = (bf16[128,512]{1,0:T(8,128)(2,1)S(1)}, bf16[128,512]{1,0:T(8,128)(2,1)S(1)}, u32[]{:S(2)}, u32[]{:S(2)}) collective-permute-start(bf16[128,512]{1,0:T(8,128)(2,1)S(1)} %constant_dynamic-update-slice_fusion), channel_id=1, source_target_pairs={{0,72},{12,84},{24,0},{36,12},{48,24},{60,36},{72,48},{84,60},{1,7... | collective-permute-start | bytes 393224 | tf_op jit(solution)/shard_map/ppermute | solution.py:49
  29.5 5.0 %collective-permute-start.6 = (bf16[128,512]{1,0:T(8,128)(2,1)S(1)}, bf16[128,512]{1,0:T(8,128)(2,1)S(1)}, u32[]{:S(2)}, u32[]{:S(2)}) collective-permute-start(bf16[128,512]{1,0:T(8,128)(2,1)S(1)} %constant_dynamic-update-slice_fusion), channel_id=1, source_target_pairs={{0,48},{12,60},{24,72},{36,84},{48,0},{60,12},{72,24},{84,36},{1,4... | collective-permute-start | bytes 393224 | tf_op jit(solution)/shard_map/ppermute | solution.py:49
  34.5 0.0 collective-permute-done.1
  34.5 2.7 %collective-permute-start.5 = (bf16[128,512]{1,0:T(8,128)(2,1)S(1)}, bf16[128,512]{1,0:T(8,128)(2,1)S(1)}, u32[]{:S(2)}, u32[]{:S(2)}) collective-permute-start(bf16[128,512]{1,0:T(8,128)(2,1)S(1)} %constant_dynamic-update-slice_fusion), channel_id=1, source_target_pairs={{0,24},{12,36},{24,48},{36,60},{48,72},{60,84},{72,0},{84,12},{1,2... | collective-permute-start | bytes 393224 | tf_op jit(solution)/shard_map/ppermute | solution.py:49
  37.2 0.1 add_compare_fusion
  37.3 0.1 and.58
  37.4 0.9 reshape_squeeze.3
  38.3 0.0 collective-permute-done
  38.3 0.0 collective-permute-done.2
  38.3 0.1 eq.56
  38.5 0.0 collective-permute-done.7
  38.5 6.8 %collective-permute-done.6 = bf16[128,512]{1,0:T(8,128)(2,1)S(1)} collective-permute-done((bf16[128,512]{1,0:T(8,128)(2,1)S(1)}, bf16[128,512]{1,0:T(8,128)(2,1)S(1)}, u32[]{:S(2)}, u32[]{:S(2)}) %collective-permute-start.6) | collective-permute-done | bytes 131104 | tf_op jit(solution)/shard_map/ppermute | solution.py:49
  45.3 1.9 %collective-permute-done.5 = bf16[128,512]{1,0:T(8,128)(2,1)S(1)} collective-permute-done((bf16[128,512]{1,0:T(8,128)(2,1)S(1)}, bf16[128,512]{1,0:T(8,128)(2,1)S(1)}, u32[]{:S(2)}, u32[]{:S(2)}) %collective-permute-start.5) | collective-permute-done | bytes 131104 | tf_op jit(solution)/shard_map/ppermute | solution.py:49
  47.2 0.1 maximum_maximum_fusion
  47.2 1.9 %collective-permute-start.8 = (bf16[4,208,512]{2,1,0:T(8,128)(2,1)S(1)}, bf16[4,208,512]{2,1,0:T(8,128)(2,1)S(1)}, u32[]{:S(2)}, u32[]{:S(2)}) collective-permute-start(bf16[4,208,512]{2,1,0:T(8,128)(2,1)S(1)} %maximum_maximum_fusion), channel_id=1, source_target_pairs={{0,12},{12,0},{24,36},{36,24},{48,60},{60,48},{72,84},{84,72},{1,1... | collective-permute-start | bytes 2555912 | tf_op jit(solution)/shard_map/ppermute | solution.py:53
  49.2 0.1 maximum_bitcast_fusion
  49.3 0.2 reshape.227
  49.5 1.3 %fusion.40 = (bf16[768,1,2,128]{3,2,1,0:T(2,128)(2,1)}, bf16[768,1,2,128]{3,2,1,0:T(2,128)(2,1)S(1)}) fusion(bf16[768,2,2,128]{3,2,1,0:T(2,128)(2,1)S(1)} %reshape.227), kind=kLoop, calls=%fused_computation.81 | loop fusion | bytes 1572864 | tf_op jit(solution)/shard_map/slice | solution.py:73
  50.8 0.4 convolution_bitcast_fusion.1
  51.2 0.4 collective-permute-done.8
  51.5 0.1 eq.59
  51.6 0.1 broadcast_compare_fusion.1
  51.7 0.1 and.61
  51.8 0.1 and.64
  52.0 0.1 maximum_bitcast_fusion.1
  52.1 0.1 copy.40
  52.1 0.2 reshape.229
  52.3 0.5 fusion.41
  52.9 0.0 slice-start
  52.9 0.4 convolution_bitcast_fusion
  53.3 0.0 copy-start
  53.3 0.1 broadcast_and_fusion.1
  53.3 0.4 fusion.38
  53.8 0.7 copy-done
  54.5 0.0 slice-start.1
  54.5 0.4 convolution_bitcast_fusion.3
  54.9 0.6 exponential_reduce_fusion.1
  55.5 0.4 convolution_bitcast_fusion.2
  55.9 0.0 slice-done
  55.9 0.3 slice-done.1
  56.2 1.3 %convolution_convert_fusion = bf16[64,6144]{1,0:T(8,128)(2,1)S(1)} fusion(bf16[512,6144]{1,0:T(8,128)(2,1)S(1)} %bitcast.188, f32[4,64]{1,0:T(4,128)S(1)} %get-tuple-element.21, f32[2,4,64,128]{3,2,1,0:T(8,128)S(1)} %convolution_bitcast_fusion.2, f32[4,64]{1,0:T(4,128)S(1)} %get-tuple-element.22, f32[2,4,64,128]{3,2,1,0:T(8,128)S(1)} %convolution_bitcast_fusion.3, ...), kind=kOutput, calls=%fused_computation | convolution fusion | flops 403243008 | bytes 7604228 | tf_op jit(solution)/shard_map/dot_general | solution.py:98
  57.5 0.5 reshape.230
  58.0 0.4 copy.45
  58.5 47.6 %all_to_all.5 = bf16[12,64,512]{2,1,0:T(8,128)(2,1)S(1)} all-to-all(bf16[12,64,512]{2,1,0:T(8,128)(2,1)S(1)} %copy.45), channel_id=1, replica_groups=mesh['span'=8,'seq'=8,'mp'=12] {'mp'}, dimensions={0} | all-to-all | bytes 1572864 | tf_op jit(solution)/shard_map/all_to_all | solution.py:102
  106.1 0.7 reduce_sum.32
  (17 shorter events, 0.3 us)
Async XLA Ops:
  0.8 26.7 %collective-permute-start.3 = (bf16[64,512]{1,0:T(8,128)(2,1)S(1)}, bf16[64,512]{1,0:T(8,128)(2,1)S(1)}, u32[]{:S(2)}, u32[]{:S(2)}) collective-permute-start(bf16[64,512]{1,0:T(8,128)(2,1)S(1)} %pad_maximum_fusion.1), channel_id=1, source_target_pairs={{0,96},{96,192},{192,288},{288,384},{384,480},{480,576},{576,672},... | collective-permute-start | bytes 196616 | tf_op jit(solution)/shard_map/ppermute | solution.py:16
  4.2 23.3 %collective-permute-start.4 = (bf16[64,512]{1,0:T(8,128)(2,1)S(1)}, bf16[64,512]{1,0:T(8,128)(2,1)S(1)}, u32[]{:S(2)}, u32[]{:S(2)}) collective-permute-start(bf16[64,512]{1,0:T(8,128)(2,1)S(1)} %pad_maximum_fusion.1), channel_id=1, source_target_pairs={{0,192},{96,288},{192,384},{288,480},{384,576},{480,672},{1,193},{... | collective-permute-start | bytes 196616 | tf_op jit(solution)/shard_map/ppermute | solution.py:16
  9.2 25.3 %collective-permute-start.1 = (bf16[80,512]{1,0:T(8,128)(2,1)S(1)}, bf16[80,512]{1,0:T(8,128)(2,1)S(1)}, u32[]{:S(2)}, u32[]{:S(2)}) collective-permute-start(bf16[80,512]{1,0:T(8,128)(2,1)S(1)} %get-tuple-element.28), channel_id=1, source_target_pairs={{0,48},{12,60},{24,72},{36,84},{48,0},{60,12},{72,24},{84,36},{1,4... | collective-permute-start | bytes 245768 | tf_op jit(solution)/shard_map/ppermute | solution.py:49
  16.1 22.2 %collective-permute-start = (bf16[80,512]{1,0:T(8,128)(2,1)S(1)}, bf16[80,512]{1,0:T(8,128)(2,1)S(1)}, u32[]{:S(2)}, u32[]{:S(2)}) collective-permute-start(bf16[80,512]{1,0:T(8,128)(2,1)S(1)} %get-tuple-element.28), channel_id=1, source_target_pairs={{0,24},{12,36},{24,48},{36,60},{48,72},{60,84},{72,0},{84,12},{1,2... | collective-permute-start | bytes 245768 | tf_op jit(solution)/shard_map/ppermute | solution.py:49
  18.8 19.5 %collective-permute-start.2 = (bf16[80,512]{1,0:T(8,128)(2,1)S(1)}, bf16[80,512]{1,0:T(8,128)(2,1)S(1)}, u32[]{:S(2)}, u32[]{:S(2)}) collective-permute-start(bf16[80,512]{1,0:T(8,128)(2,1)S(1)} %get-tuple-element.28), channel_id=1, source_target_pairs={{0,72},{12,84},{24,0},{36,12},{48,24},{60,36},{72,48},{84,60},{1,7... | collective-permute-start | bytes 245768 | tf_op jit(solution)/shard_map/ppermute | solution.py:49
  27.6 10.9 %collective-permute-start.7 = (bf16[128,512]{1,0:T(8,128)(2,1)S(1)}, bf16[128,512]{1,0:T(8,128)(2,1)S(1)}, u32[]{:S(2)}, u32[]{:S(2)}) collective-permute-start(bf16[128,512]{1,0:T(8,128)(2,1)S(1)} %constant_dynamic-update-slice_fusion), channel_id=1, source_target_pairs={{0,72},{12,84},{24,0},{36,12},{48,24},{60,36},{72,48},{84,60},{1,7... | collective-permute-start | bytes 393224 | tf_op jit(solution)/shard_map/ppermute | solution.py:49
  29.5 15.8 %collective-permute-start.6 = (bf16[128,512]{1,0:T(8,128)(2,1)S(1)}, bf16[128,512]{1,0:T(8,128)(2,1)S(1)}, u32[]{:S(2)}, u32[]{:S(2)}) collective-permute-start(bf16[128,512]{1,0:T(8,128)(2,1)S(1)} %constant_dynamic-update-slice_fusion), channel_id=1, source_target_pairs={{0,48},{12,60},{24,72},{36,84},{48,0},{60,12},{72,24},{84,36},{1,4... | collective-permute-start | bytes 393224 | tf_op jit(solution)/shard_map/ppermute | solution.py:49
  34.5 12.6 %collective-permute-start.5 = (bf16[128,512]{1,0:T(8,128)(2,1)S(1)}, bf16[128,512]{1,0:T(8,128)(2,1)S(1)}, u32[]{:S(2)}, u32[]{:S(2)}) collective-permute-start(bf16[128,512]{1,0:T(8,128)(2,1)S(1)} %constant_dynamic-update-slice_fusion), channel_id=1, source_target_pairs={{0,24},{12,36},{24,48},{36,60},{48,72},{60,84},{72,0},{84,12},{1,2... | collective-permute-start | bytes 393224 | tf_op jit(solution)/shard_map/ppermute | solution.py:49
  47.2 4.3 %collective-permute-start.8 = (bf16[4,208,512]{2,1,0:T(8,128)(2,1)S(1)}, bf16[4,208,512]{2,1,0:T(8,128)(2,1)S(1)}, u32[]{:S(2)}, u32[]{:S(2)}) collective-permute-start(bf16[4,208,512]{2,1,0:T(8,128)(2,1)S(1)} %maximum_maximum_fusion), channel_id=1, source_target_pairs={{0,12},{12,0},{24,36},{36,24},{48,60},{60,48},{72,84},{84,72},{1,1... | collective-permute-start | bytes 2555912 | tf_op jit(solution)/shard_map/ppermute | solution.py:53
  52.9 3.0 %slice-start = ((s8[6291456]{0:T(1024)(128)(4,1)}), s8[4194304]{0:T(1024)(128)(4,1)S(1)}, s32[]{:S(2)}) async-start(s8[6291456]{0:T(1024)(128)(4,1)} %bitcast.187), calls=%async_computation.1 | async-start | bytes 8388608
  53.3 1.2 %copy-start = (bf16[768,1,2,128]{3,2,1,0:T(2,128)(2,1)S(1)}, bf16[768,1,2,128]{3,2,1,0:T(2,128)(2,1)}, u32[]{:S(2)}) copy-start(bf16[768,1,2,128]{3,2,1,0:T(2,128)(2,1)} %get-tuple-element.23) | copy-start | bytes 1179652
  54.5 1.8 %slice-start.1 = ((s8[6291456]{0:T(1024)(128)(4,1)}), s8[2097152]{0:T(1024)(128)(4,1)S(1)}, s32[]{:S(2)}) async-start(s8[6291456]{0:T(1024)(128)(4,1)} %bitcast.187), calls=%async_computation.2 | async-start | bytes 4194304

commit v13 on v8

--- a/solution.py
+++ b/solution.py
@@ -44,11 +44,12 @@
     clip_row = clip_row.at[0, :row_count].set(clip_ids.astype(jnp.bfloat16))
     outgoing = jnp.concatenate(stacked + [clip_row], axis=0)
     seq_count = lax.axis_size("seq")
-    held = [outgoing]
+    fetched = []
     for shift in range(2, seq_count, 2):
         pairs = [(i, (i + shift) % seq_count) for i in range(seq_count)]
-        held.append(lax.ppermute(outgoing, "seq", pairs))
-    held = jnp.stack(held, axis=0)
+        fetched.append(lax.ppermute(outgoing, "seq", pairs))
+    pieces = [outgoing[None]] + ([jnp.stack(fetched, axis=0)] if fetched else [])
+    held = jnp.concatenate(pieces, axis=0)
     partner = lax.ppermute(held, "seq", [(i, i ^ 1) for i in range(seq_count)])
     query_heads = queries[0].reshape(row_count, head_count, HEAD_DIM)
     pick = kv_slot[:, None, None] == 0
@@ -75,17 +76,22 @@
         )
         return jnp.where(pick, acc_both[0], acc_both[1])
 
-    s, value_all = piece_scores(held)
-    first_top = jnp.max(s, axis=2, keepdims=True)
-    p = jnp.exp(s - first_top)
-    first_total = jnp.sum(p, axis=2, keepdims=True)
-    first_acc = weighted(p, value_all)
-    s, value_all = piece_scores(partner)
-    top = jnp.maximum(first_top, jnp.max(s, axis=2, keepdims=True))
-    p = jnp.exp(s - top)
-    factor = jnp.exp(first_top - top)
-    total = first_total * factor + jnp.sum(p, axis=2, keepdims=True)
-    acc = first_acc * factor + weighted(p, value_all)
+    top = total = acc = None
+    for piece in pieces + [partner]:
+        s, value_all = piece_scores(piece)
+        piece_top = jnp.max(s, axis=2, keepdims=True)
+        if top is None:
+            top = piece_top
+            p = jnp.exp(s - top)
+            total = jnp.sum(p, axis=2, keepdims=True)
+            acc = weighted(p, value_all)
+            continue
+        new_top = jnp.maximum(top, piece_top)
+        p = jnp.exp(s - new_top)
+        factor = jnp.exp(top - new_top)
+        total = total * factor + jnp.sum(p, axis=2, keepdims=True)
+        acc = acc * factor + weighted(p, value_all)
+        top = new_top
     attended = acc / total
     attended = (
         jnp.transpose(attended, (1, 0, 2)).reshape(row_count, local_width).astype(jnp.bfloat16)

time: 100 us -> 101 us (1.010)
  the two profiles are of different devices: /device:TPU:64 before, /device:TPU:6 now
where the time goes in v13:
time: 101 us; the launch traced here: 99.6 us
  blocking collectives  47.6 us (47%)
  starting transfers between devices  25 us (25%)
  waiting for transfers between devices  9.64 us (10%)
  local copies, waits for them, and re-layouts  7.39 us (7%)
  matrix products  3.96 us (4%)
  other arithmetic  3.64 us (4%)
  between operations  2.38 us (2%)
    all_to_all x1, blocking collectives, on_device(): received = lax.all_to_all(partial_sum, 'mp', 0, 0, tiled=True)  47.6 us
    ppermute x3, starting transfers between devices, on_device(): fetched.append(lax.ppermute(outgoing, 'seq', pairs))  14.8 us
    ppermute x2, starting transfers between devices, passed_along(): return lax.ppermute(x, axis, pairs)  8.33 us
    ppermute x3, waiting for transfers between devices, on_device(): fetched.append(lax.ppermute(outgoing, 'seq', pairs))  8.33 us
  transfers between devices with their start and end apart: 6, of which 3 were waited for; matrix products, arithmetic and copies ran while one was open for 7% of the time, Pallas kernels for 0%

profile of v13, /device:TPU:6, one launch (start us, length us, event | category | flops | bytes accessed | tf_op | source)
XLA Modules:
  0.0 99.6 jit_solution(12518528427421807241)
XLA Ops:
  0.0 0.8 dynamic-slice_bitcast_fusion
  0.8 4.3 %collective-permute-start.1 = (bf16[64,512]{1,0:T(8,128)(2,1)S(1)}, bf16[64,512]{1,0:T(8,128)(2,1)S(1)}, u32[]{:S(2)}, u32[]{:S(2)}) collective-permute-start(bf16[64,512]{1,0:T(8,128)(2,1)S(1)} %pad_maximum_fusion.3), channel_id=1, source_target_pairs={{0,192},{96,288},{192,384},{288,480},{384,576},{480,672},{1,193},{... | collective-permute-start | bytes 196616 | tf_op jit(solution)/shard_map/ppermute | solution.py:16
  5.1 4.0 %collective-permute-start = (bf16[64,512]{1,0:T(8,128)(2,1)S(1)}, bf16[64,512]{1,0:T(8,128)(2,1)S(1)}, u32[]{:S(2)}, u32[]{:S(2)}) collective-permute-start(bf16[64,512]{1,0:T(8,128)(2,1)S(1)} %pad_maximum_fusion.3), channel_id=1, source_target_pairs={{0,96},{96,192},{192,288},{288,384},{384,480},{480,576},{576,672},... | collective-permute-start | bytes 196616 | tf_op jit(solution)/shard_map/ppermute | solution.py:16
  9.2 1.5 %fusion.60 = (s32[1,1]{1,0:T(1,128)}, s32[1,1]{1,0:T(1,128)}, s32[1,1]{1,0:T(1,128)}) fusion(s32[8,8]{1,0:T(8,128)} %param.12, s32[]{:T(128)S(6)} %select_n.94, s32[]{:T(128)S(6)} %max.50, s32[]{:T(128)S(6)} %max.54, s32[]{:T(128)S(6)} %max.52), kind=kLoop, calls=%fused_computation.109 | loop fusion | bytes 40 | tf_op jit(solution)/shard_map/jit(dynamic_index_in_dim)/dynamic_slice | solution.py:38
  12.6 0.1 add_compare_fusion
  12.7 0.1 and.87
  12.8 0.1 and.88
  12.9 0.1 and.99
  12.9 0.1 and.93
  13.0 0.1 and.94
  13.1 0.7 fusion.61
  13.8 0.9 reshape_squeeze.3
  14.6 0.0 collective-permute-done.1
  14.7 0.0 collective-permute-done
  14.8 6.8 %collective-permute-start.3 = (bf16[208,512]{1,0:T(8,128)(2,1)S(1)}, bf16[208,512]{1,0:T(8,128)(2,1)S(1)}, u32[]{:S(2)}, u32[]{:S(2)}) collective-permute-start(bf16[208,512]{1,0:T(8,128)(2,1)S(1)} %fusion.21), channel_id=1, source_target_pairs={{0,48},{12,60},{24,72},{36,84},{48,0},{60,12},{72,24},{84,36},{1,4... | collective-permute-start | bytes 638984 | tf_op jit(solution)/shard_map/ppermute | solution.py:50
  21.6 2.7 %collective-permute-start.2 = (bf16[208,512]{1,0:T(8,128)(2,1)S(1)}, bf16[208,512]{1,0:T(8,128)(2,1)S(1)}, u32[]{:S(2)}, u32[]{:S(2)}) collective-permute-start(bf16[208,512]{1,0:T(8,128)(2,1)S(1)} %fusion.21), channel_id=1, source_target_pairs={{0,24},{12,36},{24,48},{36,60},{48,72},{60,84},{72,0},{84,12},{1,2... | collective-permute-start | bytes 638984 | tf_op jit(solution)/shard_map/ppermute | solution.py:50
  24.3 5.3 %collective-permute-start.4 = (bf16[208,512]{1,0:T(8,128)(2,1)S(1)}, bf16[208,512]{1,0:T(8,128)(2,1)S(1)}, u32[]{:S(2)}, u32[]{:S(2)}) collective-permute-start(bf16[208,512]{1,0:T(8,128)(2,1)S(1)} %fusion.21), channel_id=1, source_target_pairs={{0,72},{12,84},{24,0},{36,12},{48,24},{60,36},{72,48},{84,60},{1,7... | collective-permute-start | bytes 638984 | tf_op jit(solution)/shard_map/ppermute | solution.py:50
  29.6 0.1 broadcast_compare_fusion.2
  29.7 0.1 copy.56
  29.8 0.1 reshape_transpose_reshape.3
  29.8 0.1 fusion.59
  30.0 0.2 convolution_bitcast_fusion.2
  30.2 0.2 fusion.53
  30.4 0.2 exponential_reduce_fusion.2
  30.7 1.0 convolution_bitcast_fusion.5
  31.6 4.8 %collective-permute-done.3 = bf16[208,512]{1,0:T(8,128)(2,1)S(1)} collective-permute-done((bf16[208,512]{1,0:T(8,128)(2,1)S(1)}, bf16[208,512]{1,0:T(8,128)(2,1)S(1)}, u32[]{:S(2)}, u32[]{:S(2)}) %collective-permute-start.3) | collective-permute-done | bytes 213024 | tf_op jit(solution)/shard_map/ppermute | solution.py:50
  36.4 3.5 %collective-permute-done.2 = bf16[208,512]{1,0:T(8,128)(2,1)S(1)} collective-permute-done((bf16[208,512]{1,0:T(8,128)(2,1)S(1)}, bf16[208,512]{1,0:T(8,128)(2,1)S(1)}, u32[]{:S(2)}, u32[]{:S(2)}) %collective-permute-start.2) | collective-permute-done | bytes 213024 | tf_op jit(solution)/shard_map/ppermute | solution.py:50
  39.9 0.0 collective-permute-done.4
  40.0 0.1 pad_maximum_fusion
  40.1 0.1 eq.82
  40.2 0.1 broadcast_compare_fusion.1
  40.3 0.1 and.96
  40.4 0.1 and.97
  40.6 0.1 reshape.300
  40.7 1.9 %collective-permute-start.5 = (bf16[4,208,512]{2,1,0:T(8,128)(2,1)S(1)}, bf16[4,208,512]{2,1,0:T(8,128)(2,1)S(1)}, u32[]{:S(2)}, u32[]{:S(2)}) collective-permute-start(bf16[4,208,512]{2,1,0:T(8,128)(2,1)S(1)} %pad_maximum_fusion), channel_id=1, source_target_pairs={{0,12},{12,0},{24,36},{36,24},{48,60},{60,48},{72,84},{84,72},{1,1... | collective-permute-start | bytes 2555912 | tf_op jit(solution)/shard_map/ppermute | solution.py:53
  42.7 0.4 fusion.58
  43.1 0.3 convolution_bitcast_fusion.1
  43.4 0.3 fusion.54
  43.7 1.3 %collective-permute-done.5 = bf16[4,208,512]{2,1,0:T(8,128)(2,1)S(1)} collective-permute-done((bf16[4,208,512]{2,1,0:T(8,128)(2,1)S(1)}, bf16[4,208,512]{2,1,0:T(8,128)(2,1)S(1)}, u32[]{:S(2)}, u32[]{:S(2)}) %collective-permute-start.5) | collective-permute-done | bytes 852000 | tf_op jit(solution)/shard_map/ppermute | solution.py:53
  45.0 0.1 eq.86
  45.1 0.1 slice.127
  45.1 0.1 copy.63
  45.2 0.2 reshape.302
  45.4 0.0 slice-start
  45.4 0.5 fusion.57
  46.0 0.1 broadcast_compare_fusion
  46.1 0.1 and.102
  46.2 0.4 convolution_bitcast_fusion
  46.6 0.3 fusion.55
  46.9 0.0 slice-start.1
  46.9 0.3 exponential_reduce_fusion.1
  47.2 0.4 convolution_bitcast_fusion.4
  47.6 0.3 exponential_reduce_fusion
  47.9 0.0 copy-start
  48.0 0.4 convolution_bitcast_fusion.3
  48.4 0.0 slice-done
  48.4 0.3 slice-done.1
  48.7 0.4 copy-done
  49.0 1.3 %convolution_convert_fusion = bf16[64,6144]{1,0:T(8,128)(2,1)S(1)} fusion(bf16[512,6144]{1,0:T(8,128)(2,1)S(1)} %bitcast.236, f32[4,64]{1,0:T(4,128)S(1)} %get-tuple-element.17, f32[2,4,64,128]{3,2,1,0:T(8,128)S(1)} %convolution_bitcast_fusion.3, f32[4,64]{1,0:T(4,128)S(1)} %get-tuple-element.19, f32[2,4,64,128]{3,2,1,0:T(8,128)S(1)} %convolution_bitcast_fusion.4, ...), kind=kOutput, calls=%fused_computation | convolution fusion | flops 403341312 | bytes 7867396 | tf_op jit(solution)/shard_map/dot_general | solution.py:101
  50.3 0.5 reshape.303
  50.9 0.4 copy.68
  51.3 47.6 %all_to_all.5 = bf16[12,64,512]{2,1,0:T(8,128)(2,1)S(1)} all-to-all(bf16[12,64,512]{2,1,0:T(8,128)(2,1)S(1)} %copy.68), channel_id=1, replica_groups=mesh['span'=8,'seq'=8,'mp'=12] {'mp'}, dimensions={0} | all-to-all | bytes 1572864 | tf_op jit(solution)/shard_map/all_to_all | solution.py:105
  98.9 0.7 reduce_sum.42
  (19 shorter events, 0.3 us)
Async XLA Ops:
  0.8 13.9 %collective-permute-start.1 = (bf16[64,512]{1,0:T(8,128)(2,1)S(1)}, bf16[64,512]{1,0:T(8,128)(2,1)S(1)}, u32[]{:S(2)}, u32[]{:S(2)}) collective-permute-start(bf16[64,512]{1,0:T(8,128)(2,1)S(1)} %pad_maximum_fusion.3), channel_id=1, source_target_pairs={{0,192},{96,288},{192,384},{288,480},{384,576},{480,672},{1,193},{... | collective-permute-start | bytes 196616 | tf_op jit(solution)/shard_map/ppermute | solution.py:16
  5.1 9.5 %collective-permute-start = (bf16[64,512]{1,0:T(8,128)(2,1)S(1)}, bf16[64,512]{1,0:T(8,128)(2,1)S(1)}, u32[]{:S(2)}, u32[]{:S(2)}) collective-permute-start(bf16[64,512]{1,0:T(8,128)(2,1)S(1)} %pad_maximum_fusion.3), channel_id=1, source_target_pairs={{0,96},{96,192},{192,288},{288,384},{384,480},{480,576},{576,672},... | collective-permute-start | bytes 196616 | tf_op jit(solution)/shard_map/ppermute | solution.py:16
  14.8 21.7 %collective-permute-start.3 = (bf16[208,512]{1,0:T(8,128)(2,1)S(1)}, bf16[208,512]{1,0:T(8,128)(2,1)S(1)}, u32[]{:S(2)}, u32[]{:S(2)}) collective-permute-start(bf16[208,512]{1,0:T(8,128)(2,1)S(1)} %fusion.21), channel_id=1, source_target_pairs={{0,48},{12,60},{24,72},{36,84},{48,0},{60,12},{72,24},{84,36},{1,4... | collective-permute-start | bytes 638984 | tf_op jit(solution)/shard_map/ppermute | solution.py:50
  21.6 18.3 %collective-permute-start.2 = (bf16[208,512]{1,0:T(8,128)(2,1)S(1)}, bf16[208,512]{1,0:T(8,128)(2,1)S(1)}, u32[]{:S(2)}, u32[]{:S(2)}) collective-permute-start(bf16[208,512]{1,0:T(8,128)(2,1)S(1)} %fusion.21), channel_id=1, source_target_pairs={{0,24},{12,36},{24,48},{36,60},{48,72},{60,84},{72,0},{84,12},{1,2... | collective-permute-start | bytes 638984 | tf_op jit(solution)/shard_map/ppermute | solution.py:50
  24.3 15.6 %collective-permute-start.4 = (bf16[208,512]{1,0:T(8,128)(2,1)S(1)}, bf16[208,512]{1,0:T(8,128)(2,1)S(1)}, u32[]{:S(2)}, u32[]{:S(2)}) collective-permute-start(bf16[208,512]{1,0:T(8,128)(2,1)S(1)} %fusion.21), channel_id=1, source_target_pairs={{0,72},{12,84},{24,0},{36,12},{48,24},{60,36},{72,48},{84,60},{1,7... | collective-permute-start | bytes 638984 | tf_op jit(solution)/shard_map/ppermute | solution.py:50
  40.7 4.3 %collective-permute-start.5 = (bf16[4,208,512]{2,1,0:T(8,128)(2,1)S(1)}, bf16[4,208,512]{2,1,0:T(8,128)(2,1)S(1)}, u32[]{:S(2)}, u32[]{:S(2)}) collective-permute-start(bf16[4,208,512]{2,1,0:T(8,128)(2,1)S(1)} %pad_maximum_fusion), channel_id=1, source_target_pairs={{0,12},{12,0},{24,36},{36,24},{48,60},{60,48},{72,84},{84,72},{1,1... | collective-permute-start | bytes 2555912 | tf_op jit(solution)/shard_map/ppermute | solution.py:53
  45.4 3.0 %slice-start = ((s8[6291456]{0:T(1024)(128)(4,1)}), s8[4194304]{0:T(1024)(128)(4,1)S(1)}, s32[]{:S(2)}) async-start(s8[6291456]{0:T(1024)(128)(4,1)} %bitcast.235), calls=%async_computation.1 | async-start | bytes 8388608
  46.9 1.8 %slice-start.1 = ((s8[6291456]{0:T(1024)(128)(4,1)}), s8[2097152]{0:T(1024)(128)(4,1)S(1)}, s32[]{:S(2)}) async-start(s8[6291456]{0:T(1024)(128)(4,1)} %bitcast.235), calls=%async_computation.2 | async-start | bytes 4194304
  47.9 1.1 %copy-start = (f32[2,4,64,128]{3,2,1,0:T(8,128)S(1)}, f32[2,4,64,128]{3,2,1,0:T(8,128)}, u32[]{:S(2)}) copy-start(f32[2,4,64,128]{3,2,1,0:T(8,128)} %convolution_bitcast_fusion.5) | copy-start | bytes 786436
